TPU v7x, 1024 devices: a whole 8x8x8 slice. The times are simulated.
1024 devices in a mesh: expert: 16 (over x, core), section: 16 (over z, y_lo), dp: 4 (over y_hi).
Axes of the slice: x: 8, y: 8 (y_hi: 4, y_lo: 2; y = y_hi * 2 + y_lo), z: 8, core: 2. Of those that a mesh axis runs over, the one named last changes fastest.
Arguments:
- tok_input: bfloat16 [16, 4, 2048, 2048], P('section', 'dp', 'expert'), may hold values from -6 to 6
- tok_grad: bfloat16 [16, 4, 2048, 2048], P('section', 'dp', 'expert'), may hold values from -6 to 6
- combine_weight: float32 [16, 4, 2048], P('section', 'dp', 'expert'), may hold values from 0.1 to 1
- route_expert: int32 [16, 4, 2048], P('section', 'dp', 'expert'), may hold values from 0 to 7, as said below
- gate_up_weight: bfloat16 [16, 16, 2048, 768], P('section', 'expert'), may hold values from -0.125 to 0.125
- down_weight: bfloat16 [16, 16, 384, 2048], P('section', 'expert'), may hold values from -0.21875 to 0.21875
Outputs:
- gate_up_grad: bfloat16 [16, 16, 2048, 768], P('section', 'expert', 'dp')
- upstream: bfloat16 [16, 4, 2048, 2048], P('section', 'dp', 'expert')
Inputs may be any that keep to these rules, and one draw needn't show every extreme that they name: `route_expert`: among the tokens of one device, at most 18 name one expert, and in every such block some expert is named by exactly 18; in some section and data group one expert is named by 18 tokens of every device.
All inputs are finite; a program needn't handle non-finite values.
Results may differ from a plain program's by a relative error of at most 0.013.
Values may be sent and summed in bfloat16 or wider, within the bound.
No kernel may reach another device: no remote copies, remote signals or barrier semaphores. Data moves between devices by JAX's collectives and lax.ppermute only.
A program may use at most 64 MiB of HBM per device.

v0:
```python
import jax
import jax.numpy as jnp
from jax import lax
from jax.sharding import PartitionSpec as P


def shifted(block, axis, distance):
    devices = range(lax.axis_size(axis))
    route = [(i - distance, i) for i in devices if i - distance in devices]
    return lax.ppermute(block, axis, route)


def contract(left, right, left_dim, right_dim):
    return lax.dot_general(
        left, right, (((left_dim,), (right_dim,)), ((), ())), preferred_element_type=jnp.float32
    )


def shards(tok_input, tok_grad, combine_weight, route_expert, gate_up_weight, down_weight):
    token_input = tok_input[0, 0]
    token_grad = tok_grad[0, 0]
    weights_tok = combine_weight[0, 0]
    routes = route_expert[0, 0]
    gate_up = gate_up_weight[0, 0]
    down_proj = down_weight[0, 0]
    expert_count = lax.axis_size("expert")
    tok_count = token_input.shape[0]
    cap_rows = 9 * tok_count // (4 * expert_count)
    experts = expert_count // 2
    half_units = down_proj.shape[0]
    onehot = (routes[:, None] == jnp.arange(experts, dtype=jnp.int32)[None, :]).astype(jnp.int32)
    slot_rank = jnp.sum((jnp.cumsum(onehot, axis=0) - onehot) * onehot, axis=1)
    slot_ids = jnp.arange(expert_count * cap_rows, dtype=jnp.int32)
    placer = (
        (slot_ids[:, None] // cap_rows // 2 == routes[None, :])
        & (slot_ids[:, None] % cap_rows == slot_rank[None, :])
    ).astype(jnp.bfloat16)
    scaled = (weights_tok[:, None] * token_grad.astype(jnp.float32)).astype(jnp.bfloat16)
    input_send = jnp.dot(placer, token_input, preferred_element_type=jnp.float32).astype(
        jnp.bfloat16
    )
    grad_send = jnp.dot(placer, scaled, preferred_element_type=jnp.float32).astype(jnp.bfloat16)
    input_rows, grad_rows = (
        lax.all_to_all(input_send, "expert", split_axis=0, concat_axis=0, tiled=True),
        lax.all_to_all(grad_send, "expert", split_axis=0, concat_axis=0, tiled=True),
    )
    preact = jnp.dot(input_rows, gate_up, preferred_element_type=jnp.float32)
    gate_act = preact[:, :half_units]
    up_act = preact[:, half_units:]
    unit_grad = contract(grad_rows, down_proj, 1, 1)
    sigma = jax.nn.sigmoid(gate_act)
    act_grad = jnp.concatenate(
        [
            unit_grad * up_act * sigma * (1.0 + gate_act * (1.0 - sigma)),
            unit_grad * gate_act * sigma,
        ],
        axis=1,
    ).astype(jnp.bfloat16)
    row_grad = contract(act_grad, gate_up, 1, 1).astype(jnp.bfloat16)
    returned = lax.all_to_all(row_grad, "expert", split_axis=0, concat_axis=0, tiled=True)
    token_sum = contract(placer, returned, 0, 0)
    in_grad = (token_grad.astype(jnp.float32) + token_sum).astype(jnp.bfloat16)
    upstream = shifted(in_grad, "section", -1)
    gate_part = contract(input_rows, act_grad, 0, 0)
    gate_sum = lax.psum_scatter(
        gate_part.astype(jnp.bfloat16), "dp", scatter_dimension=0, tiled=True
    )
    return (gate_sum[None, None], upstream[None, None])


def solution(mesh):
    placed = (
        P("section", "dp", "expert", None),
        P("section", "dp", "expert", None),
        P("section", "dp", "expert"),
        P("section", "dp", "expert"),
        P("section", "expert", None, None),
        P("section", "expert", None, None),
    )
    return jax.shard_map(
        shards,
        mesh=mesh,
        in_specs=placed,
        out_specs=(P("section", "expert", "dp", None), P("section", "dp", "expert", None)),
        check_vma=False,
    )
```

profile of v0, /device:TPU:1, one launch (start us, length us, event | category | flops | bytes accessed | tf_op | source)
XLA Modules:
  0.0 211.8 jit_solution(15404805325416116609)
XLA Ops:
  7.2 0.9 fusion.30
  8.3 0.8 select_reduce_fusion
  9.1 2.6 %convolution_convert_fusion.2 = bf16[288,2048]{1,0:T(8,128)(2,1)} fusion(bf16[1,1,128,2048]{3,2,1,0:T(8,128)(2,1)} %param.6, s32[128]{0:T(128)S(1)} %select_reduce_fusion, s32[128]{0:T(128)} %bitcast.32, s32[288]{0:T(512)S(1)} %get-tuple-element.4, s32[288]{0:T(512)S(1)} %get-tuple-element.5), kind=kOutput, calls=%fused_computation.7 | convolution fusion | flops 151695360 | bytes 1707264 | tf_op jit(solution)/shard_map/dot_general | solution.py:39
  11.7 2.4 %all_to_all.24 = bf16[16,18,2048]{2,1,0:T(8,128)(2,1)} reshape(bf16[288,2048]{1,0:T(8,128)(2,1)} %convolution_convert_fusion.2) | data formatting | bytes 2359296 | tf_op jit(solution)/shard_map/all_to_all | solution.py:44
  14.1 18.4 %all-to-all-start = ((bf16[16,18,2048]{2,1,0:T(8,128)(2,1)}), bf16[16,18,2048]{2,1,0:T(8,128)(2,1)}, u32[]{:S(2)}, u32[]{:S(2)}) async-start(bf16[16,18,2048]{2,1,0:T(8,128)(2,1)} %all_to_all.24), calls=%async_computation | async-start | bytes 3145728 | tf_op jit(solution)/shard_map/all_to_all | solution.py:44
  32.6 2.6 %convolution_convert_fusion.1 = bf16[288,2048]{1,0:T(8,128)(2,1)} fusion(bf16[1,1,128,2048]{3,2,1,0:T(8,128)(2,1)} %param.7, f32[128]{0:T(128)S(1)} %bitcast.35, s32[128]{0:T(128)S(1)} %select_reduce_fusion, s32[128]{0:T(128)S(1)} %bitcast.33, s32[288]{0:T(512)S(1)} %get-tuple-element.4, s32[288]{0:T(512)S(1)} %get-tuple-element.5), kind=kOutput, calls=%fused_computation.6 | convolution fusion | flops 152481792 | bytes 1707776 | tf_op jit(solution)/shard_map/dot_general | solution.py:42
  35.2 2.4 %all_to_all.27 = bf16[16,18,2048]{2,1,0:T(8,128)(2,1)} reshape(bf16[288,2048]{1,0:T(8,128)(2,1)} %convolution_convert_fusion.1) | data formatting | bytes 2359296 | tf_op jit(solution)/shard_map/all_to_all | solution.py:45
  37.6 33.5 %all-to-all-done = bf16[16,18,2048]{2,1,0:T(8,128)(2,1)} async-done(((bf16[16,18,2048]{2,1,0:T(8,128)(2,1)}), bf16[16,18,2048]{2,1,0:T(8,128)(2,1)}, u32[]{:S(2)}, u32[]{:S(2)}) %all-to-all-start) | async-done | bytes 1179680 | tf_op jit(solution)/shard_map/all_to_all | solution.py:44
  71.1 4.3 %all-to-all-start.1 = ((bf16[16,18,2048]{2,1,0:T(8,128)(2,1)}), bf16[16,18,2048]{2,1,0:T(8,128)(2,1)}, u32[]{:S(2)}, u32[]{:S(2)}) async-start(bf16[16,18,2048]{2,1,0:T(8,128)(2,1)} %all_to_all.27), calls=%async_computation.1 | async-start | bytes 3145728 | tf_op jit(solution)/shard_map/all_to_all | solution.py:45
  75.5 2.4 %all_to_all.26 = bf16[288,2048]{1,0:T(8,128)(2,1)} reshape(bf16[16,18,2048]{2,1,0:T(8,128)(2,1)} %all-to-all-done) | data formatting | bytes 2359296 | tf_op jit(solution)/shard_map/all_to_all | solution.py:44
  77.9 3.3 %fusion.2 = f32[288,768]{1,0:T(8,128)} fusion(bf16[288,2048]{1,0:T(8,128)(2,1)} %all_to_all.26, bf16[1,1,2048,768]{3,2,1,0:T(8,128)(2,1)S(1)} %copy-done), kind=kOutput, calls=%fused_computation.3 | convolution fusion | flops 905969664 | bytes 5210112 | tf_op jit(solution)/shard_map/dot_general | solution.py:47
  81.2 32.7 %all-to-all-done.1 = bf16[16,18,2048]{2,1,0:T(8,128)(2,1)} async-done(((bf16[16,18,2048]{2,1,0:T(8,128)(2,1)}), bf16[16,18,2048]{2,1,0:T(8,128)(2,1)}, u32[]{:S(2)}, u32[]{:S(2)}) %all-to-all-start.1) | async-done | bytes 1179680 | tf_op jit(solution)/shard_map/all_to_all | solution.py:45
  113.9 2.4 %all_to_all.29 = bf16[288,2048]{1,0:T(8,128)(2,1)} reshape(bf16[16,18,2048]{2,1,0:T(8,128)(2,1)} %all-to-all-done.1) | data formatting | bytes 2359296 | tf_op jit(solution)/shard_map/all_to_all | solution.py:45
  116.3 2.9 %fusion.17 = (bf16[288,384]{1,0:T(8,128)(2,1)S(1)}, bf16[288,384]{1,0:T(8,128)(2,1)S(1)}) fusion(f32[288,768]{1,0:T(8,128)} %fusion.2, bf16[288,2048]{1,0:T(8,128)(2,1)} %all_to_all.29, bf16[1,1,384,2048]{3,2,1,0:T(8,128)(2,1)} %param.11), kind=kOutput, calls=%fused_computation.20 | convolution fusion | flops 454422528 | bytes 4079616 | tf_op jit(solution)/shard_map/dot_general | solution.py:14
  119.3 0.7 copy-done.4
  119.9 3.5 %convolution_convert_fusion = bf16[2048,768]{1,0:T(8,128)(2,1)} fusion(bf16[288,2048]{1,0:T(8,128)(2,1)S(1)} %copy-done.1, bf16[288,384]{1,0:T(8,128)(2,1)S(1)} %get-tuple-element.3, bf16[288,384]{1,0:T(8,128)(2,1)S(1)} %get-tuple-element.2), kind=kOutput, calls=%fused_computation | convolution fusion | flops 908427264 | bytes 4767744 | tf_op jit(solution)/shard_map/dot_general | solution.py:14
  123.5 3.2 %fusion.4 = bf16[288,2048]{1,0:T(8,128)(2,1)} fusion(bf16[1,1,2048,768]{3,2,1,0:T(8,128)(2,1)S(1)} %copy-done, bf16[288,384]{1,0:T(8,128)(2,1)} %copy-done.4, bf16[288,384]{1,0:T(8,128)(2,1)S(1)} %get-tuple-element.2), kind=kOutput, calls=%fused_computation.5 | convolution fusion | flops 907444224 | bytes 4767744 | tf_op jit(solution)/shard_map/dot_general | solution.py:14
  126.6 2.4 %all_to_all.30 = bf16[16,18,2048]{2,1,0:T(8,128)(2,1)} reshape(bf16[288,2048]{1,0:T(8,128)(2,1)} %fusion.4) | data formatting | bytes 2359296 | tf_op jit(solution)/shard_map/all_to_all | solution.py:60
  129.0 44.1 %all_to_all.36 = bf16[16,18,2048]{2,1,0:T(8,128)(2,1)} all-to-all(bf16[16,18,2048]{2,1,0:T(8,128)(2,1)} %all_to_all.30), channel_id=1, replica_groups=mesh['expert'=16,'section'=16,'dp'=4] {'expert'}, dimensions={0} | all-to-all | bytes 2359296 | tf_op jit(solution)/shard_map/all_to_all | solution.py:60
  173.2 2.4 %all_to_all.32 = bf16[288,2048]{1,0:T(8,128)(2,1)} reshape(bf16[16,18,2048]{2,1,0:T(8,128)(2,1)} %all_to_all.36) | data formatting | bytes 2359296 | tf_op jit(solution)/shard_map/all_to_all | solution.py:60
  175.6 2.0 fusion.7
  177.5 1.3 collective-permute-start
  178.8 24.3 %collective-permute-done = bf16[128,2048]{1,0:T(8,128)(2,1)} collective-permute-done((bf16[128,2048]{1,0:T(8,128)(2,1)S(1)}, bf16[128,2048]{1,0:T(8,128)(2,1)}, u32[]{:S(2)}, u32[]{:S(2)}) %collective-permute-start) | collective-permute-done | bytes 524320 | tf_op jit(solution)/shard_map/ppermute | solution.py:10
  203.1 1.9 copy.9
  (14 shorter events, 0.3 us)
Async XLA Ops:
  7.2 70.7 %copy-start = (bf16[1,1,2048,768]{3,2,1,0:T(8,128)(2,1)S(1)}, bf16[1,1,2048,768]{3,2,1,0:T(8,128)(2,1)}, u32[]{:S(2)}) copy-start(bf16[1,1,2048,768]{3,2,1,0:T(8,128)(2,1)} %param.10) | copy-start | bytes 9437188
  14.1 18.4 %copy-start.2 = (s32[1,1,128]{2,1,0:T(1,128)S(1)}, s32[1,1,128]{2,1,0:T(1,128)}, u32[]{:S(2)}) copy-start(s32[1,1,128]{2,1,0:T(1,128)} %param.9) | copy-start | bytes 1540
  14.1 18.4 %copy-start.3 = (f32[1,1,128]{2,1,0:T(1,128)S(1)}, f32[1,1,128]{2,1,0:T(1,128)}, u32[]{:S(2)}) copy-start(f32[1,1,128]{2,1,0:T(1,128)} %param.8) | copy-start | bytes 1540
  14.1 57.0 %all-to-all-start = ((bf16[16,18,2048]{2,1,0:T(8,128)(2,1)}), bf16[16,18,2048]{2,1,0:T(8,128)(2,1)}, u32[]{:S(2)}, u32[]{:S(2)}) async-start(bf16[16,18,2048]{2,1,0:T(8,128)(2,1)} %all_to_all.24), calls=%async_computation | async-start | bytes 3145728 | tf_op jit(solution)/shard_map/all_to_all | solution.py:44
  71.1 42.8 %all-to-all-start.1 = ((bf16[16,18,2048]{2,1,0:T(8,128)(2,1)}), bf16[16,18,2048]{2,1,0:T(8,128)(2,1)}, u32[]{:S(2)}, u32[]{:S(2)}) async-start(bf16[16,18,2048]{2,1,0:T(8,128)(2,1)} %all_to_all.27), calls=%async_computation.1 | async-start | bytes 3145728 | tf_op jit(solution)/shard_map/all_to_all | solution.py:45
  75.5 127.7 %reduce-scatter.2.cloned.1.call-start = ((), (), s32[]{:S(2)}) async-start(), calls=%async_computation.4 | async-start | bytes 3932160 | tf_op jit(solution)/shard_map/reduce_scatter | solution.py:65
  116.3 3.6 %copy-start.1 = (bf16[288,2048]{1,0:T(8,128)(2,1)S(1)}, bf16[288,2048]{1,0:T(8,128)(2,1)}, u32[]{:S(2)}) copy-start(bf16[288,2048]{1,0:T(8,128)(2,1)} %all_to_all.26) | copy-start | bytes 3538948
  119.3 0.7 copy-start.4
  177.5 25.6 %collective-permute-start = (bf16[128,2048]{1,0:T(8,128)(2,1)S(1)}, bf16[128,2048]{1,0:T(8,128)(2,1)}, u32[]{:S(2)}, u32[]{:S(2)}) collective-permute-start(bf16[128,2048]{1,0:T(8,128)(2,1)S(1)} %fusion.7), channel_id=1, source_target_pairs={{4,0},{8,4},{12,8},{16,12},{20,16},{24,20},{28,24},{32,28},{36,32}... | collective-permute-start | bytes 1572872 | tf_op jit(solution)/shard_map/ppermute | solution.py:10
Sparse Core Ops, SparseCore 0:
  123.6 70.2 reduce-scatter.1
where the time goes:
time: 213 us; the launch traced here: 212 us
  waiting for transfers between devices  90.6 us (43%)
  blocking collectives  44.1 us (21%)
  starting transfers between devices  24.1 us (11%)
  matrix products  20.1 us (9%)
  local copies, waits for them, and re-layouts  17 us (8%)
  between operations  14.1 us (7%)
    all_to_all x1, blocking collectives, shards(): lax.all_to_all(row_grad, 'expert', split_axis=0, concat_axis=0, tiled=True)  44.1 us
    all_to_all x1, waiting for transfers between devices, shards(): lax.all_to_all(input_send, 'expert', split_axis=0, concat_axis=0, tiled=T...  33.5 us
    all_to_all x1, waiting for transfers between devices, shards(): lax.all_to_all(grad_send, 'expert', split_axis=0, concat_axis=0, tiled=True)  32.7 us
    ppermute x1, waiting for transfers between devices, shifted(): return lax.ppermute(block, axis, route)  24.3 us
    all_to_all x1, starting transfers between devices, shards(): lax.all_to_all(input_send, 'expert', split_axis=0, concat_axis=0, tiled=T...  18.4 us
    dot_general x4, matrix products, contract(): lax.dot_general(left, right, (((left_dim,), (right_dim,)), ((), ())), pre...  11.5 us
    all_to_all x2, local copies, waits for them, and re-layouts, shards(): lax.all_to_all(input_send, 'expert', split_axis=0, concat_axis=0, tiled=T...  4.82 us
    all_to_all x2, local copies, waits for them, and re-layouts, shards(): lax.all_to_all(row_grad, 'expert', split_axis=0, concat_axis=0, tiled=True)  4.79 us
  transfers between devices with their start and end apart: 4, of which 3 were waited for; matrix products, arithmetic and copies ran while one was open for 5% of the time, Pallas kernels for 0%

commit v1 on v0

v1 whole, which is shorter than its diff:
```python
import jax
import jax.numpy as jnp
from jax import lax
from jax.sharding import Mesh, PartitionSpec as P


def shifted(block, axis, distance):
    devices = range(lax.axis_size(axis))
    route = [(i - distance, i) for i in devices if i - distance in devices]
    return lax.ppermute(block, axis, route)


def swapped(block):
    return lax.ppermute(block, "core", [(0, 1), (1, 0)])


def contract(left, right, left_dim, right_dim):
    return lax.dot_general(
        left, right, (((left_dim,), (right_dim,)), ((), ())), preferred_element_type=jnp.float32
    )


def shards(tok_input, tok_grad, combine_weight, route_expert, gate_up_weight, down_weight):
    token_input = tok_input[0, 0]
    token_grad = tok_grad[0, 0]
    weights_tok = combine_weight[0, 0]
    routes = route_expert[0, 0]
    gate_up = gate_up_weight[0, 0]
    down_proj = down_weight[0, 0]
    chips = lax.axis_size("x")
    tok_count, width = token_input.shape
    cap_rows = 9 * tok_count // (8 * chips)
    half_units = down_proj.shape[0]
    onehot = (routes[:, None] == jnp.arange(chips, dtype=jnp.int32)[None, :]).astype(jnp.int32)
    slot_rank = jnp.sum((jnp.cumsum(onehot, axis=0) - onehot) * onehot, axis=1)
    slot_ids = jnp.arange(chips * cap_rows, dtype=jnp.int32)
    placer = (
        (slot_ids[:, None] // cap_rows == routes[None, :])
        & (slot_ids[:, None] % cap_rows == slot_rank[None, :])
    ).astype(jnp.bfloat16)
    scaled = (weights_tok[:, None] * token_grad.astype(jnp.float32)).astype(jnp.bfloat16)
    both = jnp.concatenate([token_input, scaled], axis=1)
    send = jnp.dot(placer, both, preferred_element_type=jnp.float32).astype(jnp.bfloat16)
    mine = lax.all_to_all(send, "x", split_axis=0, concat_axis=0, tiled=True)
    other = swapped(mine)
    rows = jnp.concatenate([mine, other], axis=0)
    input_rows = rows[:, :width]
    grad_rows = rows[:, width:]
    preact = jnp.dot(input_rows, gate_up, preferred_element_type=jnp.float32)
    gate_act = preact[:, :half_units]
    up_act = preact[:, half_units:]
    unit_grad = contract(grad_rows, down_proj, 1, 1)
    sigma = jax.nn.sigmoid(gate_act)
    act_grad = jnp.concatenate(
        [
            unit_grad * up_act * sigma * (1.0 + gate_act * (1.0 - sigma)),
            unit_grad * gate_act * sigma,
        ],
        axis=1,
    ).astype(jnp.bfloat16)
    row_grad = contract(act_grad, gate_up, 1, 1).astype(jnp.bfloat16)
    local_rows = chips * cap_rows
    partner_part = swapped(row_grad[local_rows:])
    paired = (row_grad[:local_rows].astype(jnp.float32) + partner_part.astype(jnp.float32)).astype(
        jnp.bfloat16
    )
    returned = lax.all_to_all(paired, "x", split_axis=0, concat_axis=0, tiled=True)
    token_sum = contract(placer, returned, 0, 0)
    in_grad = (token_grad.astype(jnp.float32) + token_sum).astype(jnp.bfloat16)
    upstream = shifted(in_grad, "section", -1)
    gate_part = contract(input_rows, act_grad, 0, 0)
    gate_sum = lax.psum_scatter(
        gate_part.astype(jnp.bfloat16), "dp", scatter_dimension=0, tiled=True
    )
    return (gate_sum[None, None], upstream[None, None])


def solution(mesh):
    experts = mesh.shape["expert"]
    names = tuple(mesh.axis_names)
    sizes = []
    split_names = []
    for name in names:
        if name == "expert":
            sizes += [experts // 2, 2]
            split_names += ["x", "core"]
        else:
            sizes.append(mesh.shape[name])
            split_names.append(name)
    split = Mesh(mesh.devices.reshape(sizes), tuple(split_names))
    expert = ("x", "core")
    placed = (
        P("section", "dp", expert, None),
        P("section", "dp", expert, None),
        P("section", "dp", expert),
        P("section", "dp", expert),
        P("section", expert, None, None),
        P("section", expert, None, None),
    )
    return jax.shard_map(
        shards,
        mesh=split,
        in_specs=placed,
        out_specs=(P("section", expert, "dp", None), P("section", "dp", expert, None)),
        check_vma=False,
    )
```

time: 213 us -> 175 us (0.82); the launches traced: 212 us -> 171 us
  waiting for transfers between devices: 90.6 us -> 46.4 us
  blocking collectives: 44.1 us -> 63.6 us
  matrix products: 20.1 us -> 11.7 us
  starting transfers between devices: 24.1 us -> 18 us
  local copies, waits for them, and re-layouts: 17 us -> 13.4 us
  other arithmetic: 1.9 us -> 4.07 us
    all_to_all x2 -> x0, waiting for transfers between devices: 66.3 us -> none  [the longest x1 33.5 us: shards(): lax.all_to_all(input_send, 'expert', split_axis=0, concat_axis=0, tiled=T...]
    all_to_all x2 -> x0, starting transfers between devices: 22.7 us -> none  [the longest x1 18.4 us: shards(): lax.all_to_all(input_send, 'expert', split_axis=0, concat_axis=0, tiled=T...]
    all_to_all x1 -> x2, blocking collectives: 44.1 us -> 63.6 us  [the longest x1 35.8 us: shards(): mine = lax.all_to_all(send, 'x', split_axis=0, concat_axis=0, tiled=True)]
    ppermute x1, waiting for transfers between devices: 24.3 us -> 43.4 us  [shifted(): return lax.ppermute(block, axis, route)]
    ppermute x0 -> x2, starting transfers between devices: none -> 16.7 us  [swapped(): return lax.ppermute(block, 'core', [(0, 1), (1, 0)])]
    all_to_all x6 -> x4, local copies, waits for them, and re-layouts: 14.4 us -> 9.03 us  [the longest x2 4.79 us: shards(): mine = lax.all_to_all(send, 'x', split_axis=0, concat_axis=0, tiled=True)]
    dot_general x4, matrix products: 11.5 us -> 8.06 us  [contract(): lax.dot_general(left, right, (((left_dim,), (right_dim,)), ((), ())), pre...]
    ppermute x0 -> x2, waiting for transfers between devices: none -> 2.92 us  [swapped(): return lax.ppermute(block, 'core', [(0, 1), (1, 0)])]
  transfers between devices with their start and end apart: 4 -> 4, of which waited for: 3 -> 3; matrix products, arithmetic and copies ran while one was open for 5% -> 4% of each run, Pallas kernels for 0% -> 0%
where the time goes in v1:
time: 175 us; the launch traced here: 171 us
  blocking collectives  63.6 us (36%)
  waiting for transfers between devices  46.4 us (27%)
  starting transfers between devices  18 us (10%)
  between operations  14.2 us (8%)
  local copies, waits for them, and re-layouts  13.4 us (8%)
  matrix products  11.7 us (7%)
  other arithmetic  4.07 us (2%)
    ppermute x1, waiting for transfers between devices, shifted(): return lax.ppermute(block, axis, route)  43.4 us
    all_to_all x1, blocking collectives, shards(): mine = lax.all_to_all(send, 'x', split_axis=0, concat_axis=0, tiled=True)  35.8 us
    all_to_all x1, blocking collectives, shards(): lax.all_to_all(paired, 'x', split_axis=0, concat_axis=0, tiled=True)  27.8 us
    ppermute x2, starting transfers between devices, swapped(): return lax.ppermute(block, 'core', [(0, 1), (1, 0)])  16.7 us
    dot_general x4, matrix products, contract(): lax.dot_general(left, right, (((left_dim,), (right_dim,)), ((), ())), pre...  8.06 us
    all_to_all x2, local copies, waits for them, and re-layouts, shards(): mine = lax.all_to_all(send, 'x', split_axis=0, concat_axis=0, tiled=True)  4.79 us
    all_to_all x2, local copies, waits for them, and re-layouts, shards(): lax.all_to_all(paired, 'x', split_axis=0, concat_axis=0, tiled=True)  4.24 us
    unnamed x10, local copies, waits for them, and re-layouts  4.22 us
  transfers between devices with their start and end apart: 4, of which 3 were waited for; matrix products, arithmetic and copies ran while one was open for 4% of the time, Pallas kernels for 0%

profile of v1, /device:TPU:1, one launch (start us, length us, event | category | flops | bytes accessed | tf_op | source)
XLA Modules:
  0.0 171.3 jit_solution(3968514184207107833)
XLA Ops:
  7.2 0.9 fusion.20
  8.3 0.8 select_reduce_fusion
  9.1 1.2 fusion.11
  10.3 2.6 %convolution_convert_fusion = bf16[144,4096]{1,0:T(8,128)(2,1)} fusion(bf16[128,2048]{1,0:T(8,128)(2,1)S(1)} %fusion.11, bf16[128,2048]{1,0:T(8,128)(2,1)} %bitcast.22, s32[128]{0:T(128)S(1)} %select_reduce_fusion, s32[128]{0:T(128)} %bitcast.25, s32[144]{0:T(256)S(1)} %get-tuple-element.4, s32[144]{0:T(256)S(1)} %get-tuple-element.5), kind=kOutput, calls=%fused_computation | convolution fusion | flops 153737216 | bytes 2230400 | tf_op jit(solution)/shard_map/dot_general | solution.py:43
  12.9 2.4 %all_to_all.16 = bf16[8,18,4096]{2,1,0:T(8,128)(2,1)} reshape(bf16[144,4096]{1,0:T(8,128)(2,1)} %convolution_convert_fusion) | data formatting | bytes 2359296 | tf_op jit(solution)/shard_map/all_to_all | solution.py:44
  15.3 35.8 %all_to_all.24 = bf16[8,18,4096]{2,1,0:T(8,128)(2,1)} all-to-all(bf16[8,18,4096]{2,1,0:T(8,128)(2,1)} %all_to_all.16), channel_id=1, replica_groups=mesh['x'=8,'core'=2,'section'=16,'dp'=4] {'x'}, dimensions={0} | all-to-all | bytes 2359296 | tf_op jit(solution)/shard_map/all_to_all | solution.py:44
  51.2 2.4 %all_to_all.18 = bf16[144,4096]{1,0:T(8,128)(2,1)} reshape(bf16[8,18,4096]{2,1,0:T(8,128)(2,1)} %all_to_all.24) | data formatting | bytes 2359296 | tf_op jit(solution)/shard_map/all_to_all | solution.py:44
  53.6 14.4 %collective-permute-start = (bf16[144,4096]{1,0:T(8,128)(2,1)}, bf16[144,4096]{1,0:T(8,128)(2,1)S(1)}, u32[]{:S(2)}, u32[]{:S(2)}) collective-permute-start(bf16[144,4096]{1,0:T(8,128)(2,1)} %all_to_all.18), channel_id=1, source_target_pairs={{0,64},{64,0},{1,65},{65,1},{2,66},{66,2},{3,67},{67,3},{4,68},{68... | collective-permute-start | bytes 3538952 | tf_op jit(solution)/shard_map/ppermute | solution.py:14
  68.0 1.3 constant_dynamic-update-slice_fusion.1
  69.3 1.3 collective-permute-done
  70.7 1.1 fusion.2
  72.1 0.9 fusion.19
  73.7 3.5 %convolution_convert_fusion.1 = bf16[2048,768]{1,0:T(8,128)(2,1)} fusion(bf16[288,4096]{1,0:T(8,128)(2,1)S(1)} %constant_dynamic-update-slice_fusion, bf16[288,384]{1,0:T(8,128)(2,1)S(1)} %get-tuple-element.3, bf16[288,384]{1,0:T(8,128)(2,1)S(1)} %get-tuple-element.2), kind=kOutput, calls=%fused_computation.1 | convolution fusion | flops 908427264 | bytes 4767744 | tf_op jit(solution)/shard_map/dot_general | solution.py:18
  77.2 2.1 %fusion.4 = bf16[288,2048]{1,0:T(8,128)(2,1)S(1)} fusion(bf16[1,1,2048,768]{3,2,1,0:T(8,128)(2,1)S(1)} %copy-done, bf16[288,384]{1,0:T(8,128)(2,1)} %copy-done.3, bf16[288,384]{1,0:T(8,128)(2,1)S(1)} %get-tuple-element.2), kind=kOutput, calls=%fused_computation.6 | convolution fusion | flops 907444224 | bytes 4767744 | tf_op jit(solution)/shard_map/dot_general | solution.py:18
  79.3 2.3 %collective-permute-start.1 = (bf16[144,2048]{1,0:T(8,128)(2,1)S(1)}, bf16[144,2048]{1,0:T(8,128)(2,1)S(1)}, u32[]{:S(2)}, u32[]{:S(2)}) collective-permute-start(bf16[144,2048]{1,0:T(8,128)(2,1)S(1)} %slice.29), channel_id=1, source_target_pairs={{0,64},{64,0},{1,65},{65,1},{2,66},{66,2},{3,67},{67,3},{4,68},{68... | collective-permute-start | bytes 1769480 | tf_op jit(solution)/shard_map/ppermute | solution.py:14
  81.6 1.6 collective-permute-done.1
  83.2 1.0 add_convert_fusion
  84.2 2.1 %all_to_all.19 = bf16[8,18,2048]{2,1,0:T(8,128)(2,1)} reshape(bf16[144,2048]{1,0:T(8,128)(2,1)} %add_convert_fusion) | data formatting | bytes 1179648 | tf_op jit(solution)/shard_map/all_to_all | solution.py:67
  86.3 27.8 %all_to_all.25 = bf16[8,18,2048]{2,1,0:T(8,128)(2,1)} all-to-all(bf16[8,18,2048]{2,1,0:T(8,128)(2,1)} %all_to_all.19), channel_id=1, replica_groups=mesh['x'=8,'core'=2,'section'=16,'dp'=4] {'x'}, dimensions={0} | all-to-all | bytes 1179648 | tf_op jit(solution)/shard_map/all_to_all | solution.py:67
  114.1 2.1 %all_to_all.21 = bf16[144,2048]{1,0:T(8,128)(2,1)} reshape(bf16[8,18,2048]{2,1,0:T(8,128)(2,1)} %all_to_all.25) | data formatting | bytes 1179648 | tf_op jit(solution)/shard_map/all_to_all | solution.py:67
  116.2 1.6 fusion.7
  117.9 1.3 collective-permute-start.2
  119.2 43.4 %collective-permute-done.2 = bf16[128,2048]{1,0:T(8,128)(2,1)} collective-permute-done((bf16[128,2048]{1,0:T(8,128)(2,1)S(1)}, bf16[128,2048]{1,0:T(8,128)(2,1)}, u32[]{:S(2)}, u32[]{:S(2)}) %collective-permute-start.2) | collective-permute-done | bytes 524320 | tf_op jit(solution)/shard_map/ppermute | solution.py:10
  162.6 1.9 %copy.10 = bf16[1,1,128,2048]{3,2,1,0:T(8,128)(2,1)} copy(bf16[1,1,128,2048]{3,2,1,0:T(8,128)(2,1)} %bitcast.8) | data formatting | bytes 1048576
  (15 shorter events, 1.3 us)
Async XLA Ops:
  7.2 63.5 %copy-start = (bf16[1,1,2048,768]{3,2,1,0:T(8,128)(2,1)S(1)}, bf16[1,1,2048,768]{3,2,1,0:T(8,128)(2,1)}, u32[]{:S(2)}) copy-start(bf16[1,1,2048,768]{3,2,1,0:T(8,128)(2,1)} %param.10) | copy-start | bytes 9437188
  7.2 155.4 %reduce-scatter.2.cloned.1.call-start = ((), (), s32[]{:S(2)}) async-start(), calls=%async_computation.3 | async-start | bytes 3932160 | tf_op jit(solution)/shard_map/reduce_scatter | solution.py:72
  53.6 17.1 %collective-permute-start = (bf16[144,4096]{1,0:T(8,128)(2,1)}, bf16[144,4096]{1,0:T(8,128)(2,1)S(1)}, u32[]{:S(2)}, u32[]{:S(2)}) collective-permute-start(bf16[144,4096]{1,0:T(8,128)(2,1)} %all_to_all.18), channel_id=1, source_target_pairs={{0,64},{64,0},{1,65},{65,1},{2,66},{66,2},{3,67},{67,3},{4,68},{68... | collective-permute-start | bytes 3538952 | tf_op jit(solution)/shard_map/ppermute | solution.py:14
  70.7 1.4 copy-start.2
  73.0 0.7 copy-start.3
  79.3 3.9 %collective-permute-start.1 = (bf16[144,2048]{1,0:T(8,128)(2,1)S(1)}, bf16[144,2048]{1,0:T(8,128)(2,1)S(1)}, u32[]{:S(2)}, u32[]{:S(2)}) collective-permute-start(bf16[144,2048]{1,0:T(8,128)(2,1)S(1)} %slice.29), channel_id=1, source_target_pairs={{0,64},{64,0},{1,65},{65,1},{2,66},{66,2},{3,67},{67,3},{4,68},{68... | collective-permute-start | bytes 1769480 | tf_op jit(solution)/shard_map/ppermute | solution.py:14
  84.2 32.0 %copy-start.1 = (s32[1,1,128]{2,1,0:T(1,128)S(1)}, s32[1,1,128]{2,1,0:T(1,128)}, u32[]{:S(2)}) copy-start(s32[1,1,128]{2,1,0:T(1,128)} %param.9) | copy-start | bytes 1540
  117.9 44.7 %collective-permute-start.2 = (bf16[128,2048]{1,0:T(8,128)(2,1)S(1)}, bf16[128,2048]{1,0:T(8,128)(2,1)}, u32[]{:S(2)}, u32[]{:S(2)}) collective-permute-start(bf16[128,2048]{1,0:T(8,128)(2,1)S(1)} %fusion.7), channel_id=1, source_target_pairs={{4,0},{8,4},{12,8},{16,12},{20,16},{24,20},{28,24},{32,28},{36,32}... | collective-permute-start | bytes 1572872 | tf_op jit(solution)/shard_map/ppermute | solution.py:10
Sparse Core Ops, SparseCore 0:
  77.3 75.0 reduce-scatter.1

commit v2 on v1

v2 whole, which is shorter than its diff:
```python
import jax
import jax.numpy as jnp
from jax import lax
from jax.sharding import Mesh, PartitionSpec as P


def shifted(block, axis, distance):
    devices = range(lax.axis_size(axis))
    route = [(i - distance, i) for i in devices if i - distance in devices]
    return lax.ppermute(block, axis, route)


def swapped(block):
    return lax.ppermute(block, "core", [(0, 1), (1, 0)])


def contract(left, right, left_dim, right_dim):
    return lax.dot_general(
        left, right, (((left_dim,), (right_dim,)), ((), ())), preferred_element_type=jnp.float32
    )


def make_placer(routes, chips, cap_rows):
    onehot = (routes[:, None] == jnp.arange(chips, dtype=jnp.int32)[None, :]).astype(jnp.int32)
    slot_rank = jnp.sum((jnp.cumsum(onehot, axis=0) - onehot) * onehot, axis=1)
    slot_ids = jnp.arange(chips * cap_rows, dtype=jnp.int32)
    return (
        (slot_ids[:, None] // cap_rows == routes[None, :])
        & (slot_ids[:, None] % cap_rows == slot_rank[None, :])
    ).astype(jnp.bfloat16)


def expert_half(rows, gate_up, down_proj, width, half_units):
    input_rows = rows[:, :width]
    grad_rows = rows[:, width:]
    preact = jnp.dot(input_rows, gate_up, preferred_element_type=jnp.float32)
    gate_act = preact[:, :half_units]
    up_act = preact[:, half_units:]
    unit_grad = contract(grad_rows, down_proj, 1, 1)
    sigma = jax.nn.sigmoid(gate_act)
    act_grad = jnp.concatenate(
        [
            unit_grad * up_act * sigma * (1.0 + gate_act * (1.0 - sigma)),
            unit_grad * gate_act * sigma,
        ],
        axis=1,
    ).astype(jnp.bfloat16)
    row_grad = contract(act_grad, gate_up, 1, 1).astype(jnp.bfloat16)
    gate_part = contract(input_rows, act_grad, 0, 0)
    return row_grad, gate_part


def shards(tok_input, tok_grad, combine_weight, route_expert, gate_up_weight, down_weight):
    token_input = tok_input[0, 0]
    token_grad = tok_grad[0, 0]
    weights_tok = combine_weight[0, 0]
    routes = route_expert[0, 0]
    gate_up = gate_up_weight[0, 0]
    down_proj = down_weight[0, 0]
    chips = lax.axis_size("x")
    sections = lax.axis_size("section")
    tok_count, width = token_input.shape
    cap_rows = 9 * tok_count // (8 * chips)
    half_units = down_proj.shape[0]
    next_grad = shifted(token_grad, "section", -1)
    next_routes = shifted(routes, "section", -1)
    placer = make_placer(routes, chips, cap_rows)
    scaled = (weights_tok[:, None] * token_grad.astype(jnp.float32)).astype(jnp.bfloat16)
    both = jnp.concatenate([token_input, scaled], axis=1)
    send = jnp.dot(placer, both, preferred_element_type=jnp.float32).astype(jnp.bfloat16)
    mine = lax.all_to_all(send, "x", split_axis=0, concat_axis=0, tiled=True)
    other = swapped(mine)
    grad_mine, gate_mine = expert_half(mine, gate_up, down_proj, width, half_units)
    grad_other, gate_other = expert_half(other, gate_up, down_proj, width, half_units)
    gate_sum = lax.psum_scatter(
        (gate_mine + gate_other).astype(jnp.bfloat16), "dp", scatter_dimension=0, tiled=True
    )
    partner_part = swapped(grad_other)
    paired = (grad_mine.astype(jnp.float32) + partner_part.astype(jnp.float32)).astype(jnp.bfloat16)
    paired = paired.reshape(chips, cap_rows, width)
    here = lax.axis_index("x")
    received = []
    for shift in range(chips):
        block = lax.dynamic_index_in_dim(paired, (here + shift) % chips, 0, keepdims=False)
        route = [
            (x * sections + s, ((x + shift) % chips) * sections + s - 1)
            for x in range(chips)
            for s in range(1, sections)
        ]
        received.append(lax.ppermute(block, ("x", "section"), route))
    returned = jnp.stack(received)
    next_placer = make_placer(next_routes, chips, cap_rows).reshape(chips, cap_rows, tok_count)
    order = (here - jnp.arange(chips, dtype=jnp.int32)) % chips
    placer_by_shift = jnp.take(next_placer, order, axis=0)
    token_sum = lax.dot_general(
        placer_by_shift, returned, (((0, 1), (0, 1)), ((), ())), preferred_element_type=jnp.float32
    )
    upstream = (next_grad.astype(jnp.float32) + token_sum).astype(jnp.bfloat16)
    return (gate_sum[None, None], upstream[None, None])


def solution(mesh):
    experts = mesh.shape["expert"]
    sizes = []
    split_names = []
    for name in mesh.axis_names:
        if name == "expert":
            sizes += [experts // 2, 2]
            split_names += ["x", "core"]
        else:
            sizes.append(mesh.shape[name])
            split_names.append(name)
    split = Mesh(mesh.devices.reshape(sizes), tuple(split_names))
    expert = ("x", "core")
    placed = (
        P("section", "dp", expert, None),
        P("section", "dp", expert, None),
        P("section", "dp", expert),
        P("section", "dp", expert),
        P("section", expert, None, None),
        P("section", expert, None, None),
    )
    return jax.shard_map(
        shards,
        mesh=split,
        in_specs=placed,
        out_specs=(P("section", expert, "dp", None), P("section", "dp", expert, None)),
        check_vma=False,
    )
```

time: 175 us -> 179 us (1.023)
  the two profiles are of different devices: /device:TPU:1 before, /device:TPU:145 now
where the time goes in v2:
time: 179 us; the launch traced here: 178 us
  waiting for transfers between devices  59.3 us (33%)
  blocking collectives  45 us (25%)
  starting transfers between devices  26.6 us (15%)
  matrix products  17.3 us (10%)
  between operations  14.4 us (8%)
  local copies, waits for them, and re-layouts  11.1 us (6%)
  other arithmetic  4.24 us (2%)
    all_to_all x1, blocking collectives, shards(): mine = lax.all_to_all(send, 'x', split_axis=0, concat_axis=0, tiled=True)  45 us
    ppermute x8, waiting for transfers between devices, shards(): received.append(lax.ppermute(block, ('x', 'section'), route))  30.5 us
    reduce_scatter x1, waiting for transfers between devices, shards(): lax.psum_scatter((gate_mine + gate_other).astype(jnp.bfloat16), 'dp', sca...  27.8 us
    ppermute x8, starting transfers between devices, shards(): received.append(lax.ppermute(block, ('x', 'section'), route))  15.9 us
    dot_general x6, matrix products, contract(): lax.dot_general(left, right, (((left_dim,), (right_dim,)), ((), ())), pre...  10.1 us
    ppermute x2, starting transfers between devices, swapped(): return lax.ppermute(block, 'core', [(0, 1), (1, 0)])  6.8 us
    all_to_all x2, local copies, waits for them, and re-layouts, shards(): mine = lax.all_to_all(send, 'x', split_axis=0, concat_axis=0, tiled=True)  4.78 us
    ppermute x2, starting transfers between devices, shifted(): return lax.ppermute(block, axis, route)  3.88 us
  transfers between devices with their start and end apart: 13, of which 7 were waited for; matrix products, arithmetic and copies ran while one was open for 10% of the time, Pallas kernels for 0%

profile of v2, /device:TPU:145, one launch (start us, length us, event | category | flops | bytes accessed | tf_op | source)
XLA Modules:
  0.0 177.9 jit_solution(13501879189167286122)
XLA Ops:
  10.4 2.6 %convolution_convert_fusion = bf16[144,4096]{1,0:T(8,128)(2,1)} fusion(bf16[128,2048]{1,0:T(8,128)(2,1)S(1)} %multiply_convert_fusion, bf16[128,2048]{1,0:T(8,128)(2,1)} %bitcast.73, s32[128]{0:T(128)S(1)} %select_reduce_fusion.1, s32[128]{0:T(128)} %bitcast.77, s32[144]{0:T(256)S(1)} %get-tuple-element.14, s32[144]{0:T(256)S(1)} %get-tuple-element.15), kind=kOutput, calls=%fused_computation.2 | convolution fusion | flops 153737216 | bytes 2230400 | tf_op jit(solution)/shard_map/dot_general | solution.py:70
  13.0 2.4 %all_to_all.8 = bf16[8,18,4096]{2,1,0:T(8,128)(2,1)} reshape(bf16[144,4096]{1,0:T(8,128)(2,1)} %convolution_convert_fusion) | data formatting | bytes 2359296 | tf_op jit(solution)/shard_map/all_to_all | solution.py:71
  15.4 45.0 %all_to_all.12 = bf16[8,18,4096]{2,1,0:T(8,128)(2,1)} all-to-all(bf16[8,18,4096]{2,1,0:T(8,128)(2,1)} %all_to_all.8), channel_id=1, replica_groups=mesh['x'=8,'core'=2,'section'=16,'dp'=4] {'x'}, dimensions={0} | all-to-all | bytes 2359296 | tf_op jit(solution)/shard_map/all_to_all | solution.py:71
  60.4 2.4 %all_to_all.10 = bf16[144,4096]{1,0:T(8,128)(2,1)} reshape(bf16[8,18,4096]{2,1,0:T(8,128)(2,1)} %all_to_all.12) | data formatting | bytes 2359296 | tf_op jit(solution)/shard_map/all_to_all | solution.py:71
  62.8 4.6 %collective-permute-start = (bf16[144,4096]{1,0:T(8,128)(2,1)}, bf16[144,4096]{1,0:T(8,128)(2,1)S(1)}, u32[]{:S(2)}, u32[]{:S(2)}) collective-permute-start(bf16[144,4096]{1,0:T(8,128)(2,1)} %all_to_all.10), channel_id=1, source_target_pairs={{0,64},{64,0},{1,65},{65,1},{2,66},{66,2},{3,67},{67,3},{4,68},{68... | collective-permute-start | bytes 3538952 | tf_op jit(solution)/shard_map/ppermute | solution.py:14
  72.2 2.7 %add_convert_fusion = bf16[2048,768]{1,0:T(8,128)(2,1)} fusion(f32[2048,768]{1,0:T(8,128)S(1)} %fusion.29, bf16[144,4096]{1,0:T(8,128)(2,1)S(1)} %collective-permute-done, bf16[144,384]{1,0:T(8,128)(2,1)S(1)} %get-tuple-element.11, bf16[144,384]{1,0:T(8,128)(2,1)S(1)} %get-tuple-element.10), kind=kOutput, calls=%fused_computation.1 | convolution fusion | flops 456572928 | bytes 10248192 | tf_op jit(solution)/shard_map/dot_general | solution.py:18
  75.5 2.0 %collective-permute-start.2 = (s32[128]{0:T(128)S(1)}, s32[128]{0:T(128)S(1)}, u32[]{:S(2)}, u32[]{:S(2)}) collective-permute-start(s32[128]{0:T(128)S(1)} %bitcast.78), channel_id=1, source_target_pairs={{4,0},{8,4},{12,8},{16,12},{20,16},{24,20},{28,24},{32,28},{36,32}... | collective-permute-start | bytes 1544 | tf_op jit(solution)/shard_map/ppermute | solution.py:10
  77.5 1.9 %collective-permute-start.1 = (bf16[128,2048]{1,0:T(8,128)(2,1)}, bf16[128,2048]{1,0:T(8,128)(2,1)}, u32[]{:S(2)}, u32[]{:S(2)}) collective-permute-start(bf16[128,2048]{1,0:T(8,128)(2,1)} %bitcast.74), channel_id=1, source_target_pairs={{4,0},{8,4},{12,8},{16,12},{20,16},{24,20},{28,24},{32,28},{36,32}... | collective-permute-start | bytes 1572872 | tf_op jit(solution)/shard_map/ppermute | solution.py:10
  79.4 2.0 %fusion.11 = bf16[144,2048]{1,0:T(8,128)(2,1)} fusion(bf16[1,1,2048,768]{3,2,1,0:T(8,128)(2,1)S(1)} %copy-done, bf16[144,384]{1,0:T(8,128)(2,1)S(1)} %get-tuple-element.11, bf16[144,384]{1,0:T(8,128)(2,1)S(1)} %get-tuple-element.10), kind=kOutput, calls=%fused_computation.13 | convolution fusion | flops 453722112 | bytes 3956736 | tf_op jit(solution)/shard_map/dot_general | solution.py:18
  81.4 2.2 %collective-permute-start.3 = (bf16[144,2048]{1,0:T(8,128)(2,1)}, bf16[144,2048]{1,0:T(8,128)(2,1)}, u32[]{:S(2)}, u32[]{:S(2)}) collective-permute-start(bf16[144,2048]{1,0:T(8,128)(2,1)} %fusion.11), channel_id=1, source_target_pairs={{0,64},{64,0},{1,65},{65,1},{2,66},{66,2},{3,67},{67,3},{4,68},{68... | collective-permute-start | bytes 1769480 | tf_op jit(solution)/shard_map/ppermute | solution.py:14
  85.6 3.1 %add_convert_fusion.1 = bf16[144,2048]{1,0:T(8,128)(2,1)} fusion(bf16[144,2048]{1,0:T(8,128)(2,1)} %collective-permute-done.3, bf16[1,1,2048,768]{3,2,1,0:T(8,128)(2,1)S(1)} %copy-done, bf16[144,384]{1,0:T(8,128)(2,1)} %copy-done.2, bf16[144,384]{1,0:T(8,128)(2,1)S(1)} %get-tuple-element.12), kind=kOutput, calls=%fused_computation.19 | convolution fusion | flops 454901760 | bytes 4546560 | tf_op jit(solution)/shard_map/dot_general | solution.py:18
  88.8 2.1 %reshape.130 = bf16[8,18,2048]{2,1,0:T(8,128)(2,1)} reshape(bf16[144,2048]{1,0:T(8,128)(2,1)} %add_convert_fusion.1) | data formatting | bytes 1179648 | tf_op jit(solution)/shard_map/reshape | solution.py:80
  90.9 2.0 %dynamic-slice_bitcast_fusion = (bf16[18,2048]{1,0:T(8,128)(2,1)S(1)}, bf16[18,2048]{1,0:T(8,128)(2,1)S(1)}, bf16[18,2048]{1,0:T(8,128)(2,1)S(1)}, bf16[18,2048]...) fusion(bf16[8,18,2048]{2,1,0:T(8,128)(2,1)} %reshape.130, ...), kind=kLoop, calls=%fused_computation.55 | loop fusion | bytes 1179680 | tf_op jit(solution)/shard_map/jit(dynamic_index_in_dim)/squeeze | solution.py:84
  95.5 1.9 %collective-permute-start.5 = (bf16[18,2048]{1,0:T(8,128)(2,1)}, bf16[18,2048]{1,0:T(8,128)(2,1)S(1)}, u32[]{:S(2)}, u32[]{:S(2)}) collective-permute-start(bf16[18,2048]{1,0:T(8,128)(2,1)} %get-tuple-element.8), channel_id=1, source_target_pairs={{4,128},{8,132},{12,136},{16,140},{20,144},{24,148},{28,152},{32,1... | collective-permute-start | bytes 221192 | tf_op jit(solution)/shard_map/ppermute | solution.py:90
  99.3 2.4 %collective-permute-start.7 = (bf16[18,2048]{1,0:T(8,128)(2,1)}, bf16[18,2048]{1,0:T(8,128)(2,1)S(1)}, u32[]{:S(2)}, u32[]{:S(2)}) collective-permute-start(bf16[18,2048]{1,0:T(8,128)(2,1)} %get-tuple-element.6), channel_id=1, source_target_pairs={{4,384},{8,388},{12,392},{16,396},{20,400},{24,404},{28,408},{32,4... | collective-permute-start | bytes 221192 | tf_op jit(solution)/shard_map/ppermute | solution.py:90
  101.8 15.7 %collective-permute-done.4 = bf16[18,2048]{1,0:T(8,128)(2,1)} collective-permute-done((bf16[18,2048]{1,0:T(8,128)(2,1)}, bf16[18,2048]{1,0:T(8,128)(2,1)}, u32[]{:S(2)}, u32[]{:S(2)}) %collective-permute-start.4) | collective-permute-done | bytes 73760 | tf_op jit(solution)/shard_map/ppermute | solution.py:90
  120.3 1.9 %collective-permute-start.9 = (bf16[18,2048]{1,0:T(8,128)(2,1)S(1)}, bf16[18,2048]{1,0:T(8,128)(2,1)S(1)}, u32[]{:S(2)}, u32[]{:S(2)}) collective-permute-start(bf16[18,2048]{1,0:T(8,128)(2,1)S(1)} %get-tuple-element.4), channel_id=1, source_target_pairs={{4,640},{8,644},{12,648},{16,652},{20,656},{24,660},{28,664},{32,6... | collective-permute-start | bytes 221192 | tf_op jit(solution)/shard_map/ppermute | solution.py:90
  122.3 1.9 %collective-permute-start.10 = (bf16[18,2048]{1,0:T(8,128)(2,1)S(1)}, bf16[18,2048]{1,0:T(8,128)(2,1)S(1)}, u32[]{:S(2)}, u32[]{:S(2)}) collective-permute-start(bf16[18,2048]{1,0:T(8,128)(2,1)S(1)} %get-tuple-element.3), channel_id=1, source_target_pairs={{4,768},{8,772},{12,776},{16,780},{20,784},{24,788},{28,792},{32,7... | collective-permute-start | bytes 221192 | tf_op jit(solution)/shard_map/ppermute | solution.py:90
  124.2 1.9 %collective-permute-start.11 = (bf16[18,2048]{1,0:T(8,128)(2,1)S(1)}, bf16[18,2048]{1,0:T(8,128)(2,1)S(1)}, u32[]{:S(2)}, u32[]{:S(2)}) collective-permute-start(bf16[18,2048]{1,0:T(8,128)(2,1)S(1)} %get-tuple-element.2), channel_id=1, source_target_pairs={{4,896},{8,900},{12,904},{16,908},{20,912},{24,916},{28,920},{32,9... | collective-permute-start | bytes 221192 | tf_op jit(solution)/shard_map/ppermute | solution.py:90
  126.2 3.8 %collective-permute-done.8 = bf16[18,2048]{1,0:T(8,128)(2,1)S(1)} collective-permute-done((bf16[18,2048]{1,0:T(8,128)(2,1)}, bf16[18,2048]{1,0:T(8,128)(2,1)S(1)}, u32[]{:S(2)}, u32[]{:S(2)}) %collective-permute-start.8) | collective-permute-done | bytes 73760 | tf_op jit(solution)/shard_map/ppermute | solution.py:90
  130.0 5.1 %collective-permute-done.9 = bf16[18,2048]{1,0:T(8,128)(2,1)S(1)} collective-permute-done((bf16[18,2048]{1,0:T(8,128)(2,1)S(1)}, bf16[18,2048]{1,0:T(8,128)(2,1)S(1)}, u32[]{:S(2)}, u32[]{:S(2)}) %collective-permute-start.9) | collective-permute-done | bytes 73760 | tf_op jit(solution)/shard_map/ppermute | solution.py:90
  136.9 4.0 %collective-permute-done.11 = bf16[18,2048]{1,0:T(8,128)(2,1)S(1)} collective-permute-done((bf16[18,2048]{1,0:T(8,128)(2,1)S(1)}, bf16[18,2048]{1,0:T(8,128)(2,1)S(1)}, u32[]{:S(2)}, u32[]{:S(2)}) %collective-permute-start.11) | collective-permute-done | bytes 73760 | tf_op jit(solution)/shard_map/ppermute | solution.py:90
  141.0 2.3 %fusion.26 = bf16[1,1,128,2048]{3,2,1,0:T(8,128)(2,1)} fusion(bf16[128,2048]{1,0:T(8,128)(2,1)} %collective-permute-done.1, bf16[8,18,2048]{2,1,0:T(8,128)(2,1)S(1)} %bitcast_dynamic-update-slice_fusion, bf16[8,18,128]{2,1,0:T(8,128)(2,1)S(1)} %gather_fusion, pred[8]{0:T(512)(128)(4,1)} %compare_and_fusion), kind=kOutput, calls=%fused_computation.27 | convolution fusion | flops 76302336 | bytes 1675272 | tf_op jit(solution)/shard_map/dot_general | solution.py:95
  143.2 27.8 %reduce-scatter.2.cloned.1.call-done = bf16[512,768]{1,0:T(8,128)(2,1)} async-done(((bf16[2048,768]{1,0:T(8,128)(2,1)}), bf16[512,768]{1,0:T(8,128)(2,1)}) %reduce-scatter.2.cloned.1.call-update) | async-done | bytes 786448 | tf_op jit(solution)/shard_map/reduce_scatter | solution.py:75
  (50 shorter events, 19.7 us)
Async XLA Ops:
  7.2 60.3 %copy-start = (bf16[1,1,2048,768]{3,2,1,0:T(8,128)(2,1)S(1)}, bf16[1,1,2048,768]{3,2,1,0:T(8,128)(2,1)}, u32[]{:S(2)}) copy-start(bf16[1,1,2048,768]{3,2,1,0:T(8,128)(2,1)} %param.10) | copy-start | bytes 9437188
  7.2 163.9 %reduce-scatter.2.cloned.1.call-start = ((), (), s32[]{:S(2)}) async-start(), calls=%async_computation.2 | async-start | bytes 3932160 | tf_op jit(solution)/shard_map/reduce_scatter | solution.py:75
  62.8 6.3 %copy-start.1 = (bf16[144,4096]{1,0:T(8,128)(2,1)S(1)}, bf16[144,4096]{1,0:T(8,128)(2,1)}, u32[]{:S(2)}) copy-start(bf16[144,4096]{1,0:T(8,128)(2,1)} %all_to_all.10) | copy-start | bytes 3538948
  62.8 6.3 %copy-start.4 = (bf16[1,1,384,2048]{3,2,1,0:T(8,128)(2,1)S(1)}, bf16[1,1,384,2048]{3,2,1,0:T(8,128)(2,1)}, u32[]{:S(2)}) copy-start(bf16[1,1,384,2048]{3,2,1,0:T(8,128)(2,1)} %param.11) | copy-start | bytes 4718596
  62.8 8.1 %collective-permute-start = (bf16[144,4096]{1,0:T(8,128)(2,1)}, bf16[144,4096]{1,0:T(8,128)(2,1)S(1)}, u32[]{:S(2)}, u32[]{:S(2)}) collective-permute-start(bf16[144,4096]{1,0:T(8,128)(2,1)} %all_to_all.10), channel_id=1, source_target_pairs={{0,64},{64,0},{1,65},{65,1},{2,66},{66,2},{3,67},{67,3},{4,68},{68... | collective-permute-start | bytes 3538952 | tf_op jit(solution)/shard_map/ppermute | solution.py:14
  69.8 1.1 copy-start.2
  74.9 0.7 copy-start.3
  75.5 8.7 %collective-permute-start.2 = (s32[128]{0:T(128)S(1)}, s32[128]{0:T(128)S(1)}, u32[]{:S(2)}, u32[]{:S(2)}) collective-permute-start(s32[128]{0:T(128)S(1)} %bitcast.78), channel_id=1, source_target_pairs={{4,0},{8,4},{12,8},{16,12},{20,16},{24,20},{28,24},{32,28},{36,32}... | collective-permute-start | bytes 1544 | tf_op jit(solution)/shard_map/ppermute | solution.py:10
  77.5 63.5 %collective-permute-start.1 = (bf16[128,2048]{1,0:T(8,128)(2,1)}, bf16[128,2048]{1,0:T(8,128)(2,1)}, u32[]{:S(2)}, u32[]{:S(2)}) collective-permute-start(bf16[128,2048]{1,0:T(8,128)(2,1)} %bitcast.74), channel_id=1, source_target_pairs={{4,0},{8,4},{12,8},{16,12},{20,16},{24,20},{28,24},{32,28},{36,32}... | collective-permute-start | bytes 1572872 | tf_op jit(solution)/shard_map/ppermute | solution.py:10
  81.4 4.2 %collective-permute-start.3 = (bf16[144,2048]{1,0:T(8,128)(2,1)}, bf16[144,2048]{1,0:T(8,128)(2,1)}, u32[]{:S(2)}, u32[]{:S(2)}) collective-permute-start(bf16[144,2048]{1,0:T(8,128)(2,1)} %fusion.11), channel_id=1, source_target_pairs={{0,64},{64,0},{1,65},{65,1},{2,66},{66,2},{3,67},{67,3},{4,68},{68... | collective-permute-start | bytes 1769480 | tf_op jit(solution)/shard_map/ppermute | solution.py:14
  92.9 24.6 %collective-permute-start.4 = (bf16[18,2048]{1,0:T(8,128)(2,1)}, bf16[18,2048]{1,0:T(8,128)(2,1)}, u32[]{:S(2)}, u32[]{:S(2)}) collective-permute-start(bf16[18,2048]{1,0:T(8,128)(2,1)} %get-tuple-element.9), channel_id=1, source_target_pairs={{4,0},{8,4},{12,8},{16,12},{20,16},{24,20},{28,24},{32,28},{36,32}... | collective-permute-start | bytes 221192 | tf_op jit(solution)/shard_map/ppermute | solution.py:90
  95.5 24.8 %collective-permute-start.5 = (bf16[18,2048]{1,0:T(8,128)(2,1)}, bf16[18,2048]{1,0:T(8,128)(2,1)S(1)}, u32[]{:S(2)}, u32[]{:S(2)}) collective-permute-start(bf16[18,2048]{1,0:T(8,128)(2,1)} %get-tuple-element.8), channel_id=1, source_target_pairs={{4,128},{8,132},{12,136},{16,140},{20,144},{24,148},{28,152},{32,1... | collective-permute-start | bytes 221192 | tf_op jit(solution)/shard_map/ppermute | solution.py:90
  97.4 24.9 %collective-permute-start.6 = (bf16[18,2048]{1,0:T(8,128)(2,1)}, bf16[18,2048]{1,0:T(8,128)(2,1)S(1)}, u32[]{:S(2)}, u32[]{:S(2)}) collective-permute-start(bf16[18,2048]{1,0:T(8,128)(2,1)} %get-tuple-element.7), channel_id=1, source_target_pairs={{4,256},{8,260},{12,264},{16,268},{20,272},{24,276},{28,280},{32,2... | collective-permute-start | bytes 221192 | tf_op jit(solution)/shard_map/ppermute | solution.py:90
  99.3 24.9 %collective-permute-start.7 = (bf16[18,2048]{1,0:T(8,128)(2,1)}, bf16[18,2048]{1,0:T(8,128)(2,1)S(1)}, u32[]{:S(2)}, u32[]{:S(2)}) collective-permute-start(bf16[18,2048]{1,0:T(8,128)(2,1)} %get-tuple-element.6), channel_id=1, source_target_pairs={{4,384},{8,388},{12,392},{16,396},{20,400},{24,404},{28,408},{32,4... | collective-permute-start | bytes 221192 | tf_op jit(solution)/shard_map/ppermute | solution.py:90
  117.5 12.5 %collective-permute-start.8 = (bf16[18,2048]{1,0:T(8,128)(2,1)}, bf16[18,2048]{1,0:T(8,128)(2,1)S(1)}, u32[]{:S(2)}, u32[]{:S(2)}) collective-permute-start(bf16[18,2048]{1,0:T(8,128)(2,1)} %get-tuple-element.5), channel_id=1, source_target_pairs={{4,512},{8,516},{12,520},{16,524},{20,528},{24,532},{28,536},{32,5... | collective-permute-start | bytes 221192 | tf_op jit(solution)/shard_map/ppermute | solution.py:90
  120.3 14.8 %collective-permute-start.9 = (bf16[18,2048]{1,0:T(8,128)(2,1)S(1)}, bf16[18,2048]{1,0:T(8,128)(2,1)S(1)}, u32[]{:S(2)}, u32[]{:S(2)}) collective-permute-start(bf16[18,2048]{1,0:T(8,128)(2,1)S(1)} %get-tuple-element.4), channel_id=1, source_target_pairs={{4,640},{8,644},{12,648},{16,652},{20,656},{24,660},{28,664},{32,6... | collective-permute-start | bytes 221192 | tf_op jit(solution)/shard_map/ppermute | solution.py:90
  122.3 14.6 %collective-permute-start.10 = (bf16[18,2048]{1,0:T(8,128)(2,1)S(1)}, bf16[18,2048]{1,0:T(8,128)(2,1)S(1)}, u32[]{:S(2)}, u32[]{:S(2)}) collective-permute-start(bf16[18,2048]{1,0:T(8,128)(2,1)S(1)} %get-tuple-element.3), channel_id=1, source_target_pairs={{4,768},{8,772},{12,776},{16,780},{20,784},{24,788},{28,792},{32,7... | collective-permute-start | bytes 221192 | tf_op jit(solution)/shard_map/ppermute | solution.py:90
  124.2 16.7 %collective-permute-start.11 = (bf16[18,2048]{1,0:T(8,128)(2,1)S(1)}, bf16[18,2048]{1,0:T(8,128)(2,1)S(1)}, u32[]{:S(2)}, u32[]{:S(2)}) collective-permute-start(bf16[18,2048]{1,0:T(8,128)(2,1)S(1)} %get-tuple-element.2), channel_id=1, source_target_pairs={{4,896},{8,900},{12,904},{16,908},{20,912},{24,916},{28,920},{32,9... | collective-permute-start | bytes 221192 | tf_op jit(solution)/shard_map/ppermute | solution.py:90
Sparse Core Ops, SparseCore 0:
  75.0 95.9 reduce-scatter.1

commit v3 on v2

--- a/solution.py
+++ b/solution.py
@@ -50,6 +50,32 @@
     return row_grad, gate_part
 
 
+def ring_scatter(part, axis):
+    count = lax.axis_size(axis)
+    here = lax.axis_index(axis)
+    rows, cols = part.shape
+    blocks = part.reshape(count, rows // count, cols)
+    ahead = blocks[:, :, : cols // 2]
+    behind = blocks[:, :, cols // 2 :]
+    right = [(j, (j + 1) % count) for j in range(count)]
+    left = [(j, (j - 1) % count) for j in range(count)]
+
+    def pick(stack, index):
+        return lax.dynamic_index_in_dim(stack, index % count, 0, keepdims=False)
+
+    acc_ahead = pick(ahead, here - 1)
+    acc_behind = pick(behind, here + 1)
+    for step in range(count - 1):
+        got_ahead = lax.ppermute(acc_ahead, axis, right)
+        got_behind = lax.ppermute(acc_behind, axis, left)
+        acc_ahead = got_ahead.astype(jnp.float32) + pick(ahead, here - step - 2).astype(jnp.float32)
+        acc_behind = got_behind.astype(jnp.float32) + pick(behind, here + step + 2).astype(jnp.float32)
+        if step < count - 2:
+            acc_ahead = acc_ahead.astype(jnp.bfloat16)
+            acc_behind = acc_behind.astype(jnp.bfloat16)
+    return jnp.concatenate([acc_ahead, acc_behind], axis=1).astype(jnp.bfloat16)
+
+
 def shards(tok_input, tok_grad, combine_weight, route_expert, gate_up_weight, down_weight):
     token_input = tok_input[0, 0]
     token_grad = tok_grad[0, 0]
@@ -72,9 +98,7 @@
     other = swapped(mine)
     grad_mine, gate_mine = expert_half(mine, gate_up, down_proj, width, half_units)
     grad_other, gate_other = expert_half(other, gate_up, down_proj, width, half_units)
-    gate_sum = lax.psum_scatter(
-        (gate_mine + gate_other).astype(jnp.bfloat16), "dp", scatter_dimension=0, tiled=True
-    )
+    gate_sum = ring_scatter((gate_mine + gate_other).astype(jnp.bfloat16), "dp")
     partner_part = swapped(grad_other)
     paired = (grad_mine.astype(jnp.float32) + partner_part.astype(jnp.float32)).astype(jnp.bfloat16)
     paired = paired.reshape(chips, cap_rows, width)

time: 179 us -> 193 us (1.078)
  the two profiles are of different devices: /device:TPU:145 before, /device:TPU:479 now
where the time goes in v3:
time: 193 us; the launch traced here: 192 us
  waiting for transfers between devices  77 us (40%)
  starting transfers between devices  72.8 us (38%)
  matrix products  18.9 us (10%)
  local copies, waits for them, and re-layouts  13.1 us (7%)
  other arithmetic  9.12 us (5%)
    ppermute x8, starting transfers between devices, shards(): received.append(lax.ppermute(block, ('x', 'section'), route))  35.3 us
    ppermute x8, waiting for transfers between devices, shards(): received.append(lax.ppermute(block, ('x', 'section'), route))  28.3 us
    all_to_all x1, waiting for transfers between devices, shards(): mine = lax.all_to_all(send, 'x', split_axis=0, concat_axis=0, tiled=True)  28 us
    ppermute x3, waiting for transfers between devices, ring_scatter(): got_behind = lax.ppermute(acc_behind, axis, left)  12.5 us
    ppermute x3, starting transfers between devices, ring_scatter(): got_ahead = lax.ppermute(acc_ahead, axis, right)  10.8 us
    dot_general x6, matrix products, contract(): lax.dot_general(left, right, (((left_dim,), (right_dim,)), ((), ())), pre...  10.5 us
    ppermute x3, starting transfers between devices, ring_scatter(): got_behind = lax.ppermute(acc_behind, axis, left)  8.5 us
    ppermute x3, waiting for transfers between devices, ring_scatter(): got_ahead = lax.ppermute(acc_ahead, axis, right)  8.22 us
  transfers between devices with their start and end apart: 19, of which 10 were waited for; matrix products, arithmetic and copies ran while one was open for 15% of the time, Pallas kernels for 0%

profile of v3, /device:TPU:479, one launch (start us, length us, event | category | flops | bytes accessed | tf_op | source)
XLA Modules:
  0.0 192.3 jit_solution(14040945167950004071)
XLA Ops:
  3.8 2.6 %convolution_convert_fusion = bf16[144,4096]{1,0:T(8,128)(2,1)} fusion(bf16[128,2048]{1,0:T(8,128)(2,1)S(1)} %multiply_convert_fusion, bf16[128,2048]{1,0:T(8,128)(2,1)} %bitcast.100, s32[128]{0:T(128)S(1)} %select_reduce_fusion.1, s32[128]{0:T(128)} %bitcast.104, s32[144]{0:T(256)S(1)} %get-tuple-element.18, s32[144]{0:T(256)S(1)} %get-tuple-element.19), kind=kOutput, calls=%fused_computation.2 | convolution fusion | flops 153737216 | bytes 2230400 | tf_op jit(solution)/shard_map/dot_general | solution.py:96
  8.8 6.7 %all-to-all-start = ((bf16[8,18,4096]{2,1,0:T(8,128)(2,1)}), bf16[8,18,4096]{2,1,0:T(8,128)(2,1)}, u32[]{:S(2)}, u32[]{:S(2)}) async-start(bf16[8,18,4096]{2,1,0:T(8,128)(2,1)} %all_to_all.8), calls=%async_computation | async-start | bytes 3145728 | tf_op jit(solution)/shard_map/all_to_all | solution.py:97
  15.5 2.9 %collective-permute-start.8 = (s32[128]{0:T(128)S(1)}, s32[128]{0:T(128)S(1)}, u32[]{:S(2)}, u32[]{:S(2)}) collective-permute-start(s32[128]{0:T(128)S(1)} %bitcast.105), channel_id=1, source_target_pairs={{4,0},{8,4},{12,8},{16,12},{20,16},{24,20},{28,24},{32,28},{36,32}... | collective-permute-start | bytes 1544 | tf_op jit(solution)/shard_map/ppermute | solution.py:10
  20.6 28.0 %all-to-all-done = bf16[8,18,4096]{2,1,0:T(8,128)(2,1)} async-done(((bf16[8,18,4096]{2,1,0:T(8,128)(2,1)}), bf16[8,18,4096]{2,1,0:T(8,128)(2,1)}, u32[]{:S(2)}, u32[]{:S(2)}) %all-to-all-start) | async-done | bytes 1179680 | tf_op jit(solution)/shard_map/all_to_all | solution.py:97
  48.7 2.4 %all_to_all.10 = bf16[144,4096]{1,0:T(8,128)(2,1)} reshape(bf16[8,18,4096]{2,1,0:T(8,128)(2,1)} %all-to-all-done) | data formatting | bytes 2359296 | tf_op jit(solution)/shard_map/all_to_all | solution.py:97
  51.0 4.5 %collective-permute-start = (bf16[144,4096]{1,0:T(8,128)(2,1)}, bf16[144,4096]{1,0:T(8,128)(2,1)}, u32[]{:S(2)}, u32[]{:S(2)}) collective-permute-start(bf16[144,4096]{1,0:T(8,128)(2,1)} %all_to_all.10), channel_id=1, source_target_pairs={{0,64},{64,0},{1,65},{65,1},{2,66},{66,2},{3,67},{67,3},{4,68},{68... | collective-permute-start | bytes 3538952 | tf_op jit(solution)/shard_map/ppermute | solution.py:14
  67.4 2.6 %collective-permute-start.4 = (bf16[512,384]{1,0:T(8,128)(2,1)}, bf16[512,384]{1,0:T(8,128)(2,1)}, u32[]{:S(2)}, u32[]{:S(2)}) collective-permute-start(bf16[512,384]{1,0:T(8,128)(2,1)} %dynamic-slice_bitcast_fusion), channel_id=1, source_target_pairs={{0,3},{1,0},{2,1},{3,2},{4,7},{5,4},{6,5},{7,6},{8,11},{9,8},{10,9... | collective-permute-start | bytes 1179656 | tf_op jit(solution)/shard_map/ppermute | solution.py:70
  76.7 3.5 %collective-permute-start.1 = (bf16[512,384]{1,0:T(8,128)(2,1)}, bf16[512,384]{1,0:T(8,128)(2,1)}, u32[]{:S(2)}, u32[]{:S(2)}) collective-permute-start(bf16[512,384]{1,0:T(8,128)(2,1)} %dynamic-slice_bitcast_fusion.1), channel_id=1, source_target_pairs={{0,1},{1,2},{2,3},{3,0},{4,5},{5,6},{6,7},{7,4},{8,9},{9,10},{10,1... | collective-permute-start | bytes 1179656 | tf_op jit(solution)/shard_map/ppermute | solution.py:69
  80.3 4.2 %collective-permute-done.4 = bf16[512,384]{1,0:T(8,128)(2,1)} collective-permute-done((bf16[512,384]{1,0:T(8,128)(2,1)}, bf16[512,384]{1,0:T(8,128)(2,1)}, u32[]{:S(2)}, u32[]{:S(2)}) %collective-permute-start.4) | collective-permute-done | bytes 393248 | tf_op jit(solution)/shard_map/ppermute | solution.py:70
  86.4 4.0 %collective-permute-start.5 = (bf16[512,384]{1,0:T(8,128)(2,1)}, bf16[512,384]{1,0:T(8,128)(2,1)}, u32[]{:S(2)}, u32[]{:S(2)}) collective-permute-start(bf16[512,384]{1,0:T(8,128)(2,1)} %fusion.26), channel_id=1, source_target_pairs={{0,3},{1,0},{2,1},{3,2},{4,7},{5,4},{6,5},{7,6},{8,11},{9,8},{10,9... | collective-permute-start | bytes 1179656 | tf_op jit(solution)/shard_map/ppermute | solution.py:70
  90.4 3.0 %add_convert_fusion.1 = bf16[144,2048]{1,0:T(8,128)(2,1)} fusion(bf16[144,2048]{1,0:T(8,128)(2,1)} %collective-permute-done.9, bf16[1,1,2048,768]{3,2,1,0:T(8,128)(2,1)S(1)} %copy-done, bf16[144,384]{1,0:T(8,128)(2,1)S(1)} %get-tuple-element.15, bf16[144,384]{1,0:T(8,128)(2,1)S(1)} %get-tuple-element.14), kind=kOutput, calls=%fused_computation.19 | convolution fusion | flops 454901760 | bytes 4546560 | tf_op jit(solution)/shard_map/dot_general | solution.py:18
  97.0 7.5 %collective-permute-start.10 = (bf16[18,2048]{1,0:T(8,128)(2,1)S(1)}, bf16[18,2048]{1,0:T(8,128)(2,1)S(1)}, u32[]{:S(2)}, u32[]{:S(2)}) collective-permute-start(bf16[18,2048]{1,0:T(8,128)(2,1)S(1)} %get-tuple-element.11), channel_id=1, source_target_pairs={{4,0},{8,4},{12,8},{16,12},{20,16},{24,20},{28,24},{32,28},{36,32}... | collective-permute-start | bytes 221192 | tf_op jit(solution)/shard_map/ppermute | solution.py:114
  105.6 3.0 %collective-permute-start.2 = (bf16[512,384]{1,0:T(8,128)(2,1)S(1)}, bf16[512,384]{1,0:T(8,128)(2,1)S(1)}, u32[]{:S(2)}, u32[]{:S(2)}) collective-permute-start(bf16[512,384]{1,0:T(8,128)(2,1)S(1)} %fusion.29), channel_id=1, source_target_pairs={{0,1},{1,2},{2,3},{3,0},{4,5},{5,6},{6,7},{7,4},{8,9},{9,10},{10,1... | collective-permute-start | bytes 1179656 | tf_op jit(solution)/shard_map/ppermute | solution.py:69
  108.6 6.9 %collective-permute-start.11 = (bf16[18,2048]{1,0:T(8,128)(2,1)S(1)}, bf16[18,2048]{1,0:T(8,128)(2,1)S(1)}, u32[]{:S(2)}, u32[]{:S(2)}) collective-permute-start(bf16[18,2048]{1,0:T(8,128)(2,1)S(1)} %get-tuple-element.10), channel_id=1, source_target_pairs={{4,128},{8,132},{12,136},{16,140},{20,144},{24,148},{28,152},{32,1... | collective-permute-start | bytes 221192 | tf_op jit(solution)/shard_map/ppermute | solution.py:114
  115.6 9.3 %collective-permute-start.12 = (bf16[18,2048]{1,0:T(8,128)(2,1)S(1)}, bf16[18,2048]{1,0:T(8,128)(2,1)S(1)}, u32[]{:S(2)}, u32[]{:S(2)}) collective-permute-start(bf16[18,2048]{1,0:T(8,128)(2,1)S(1)} %get-tuple-element.9), channel_id=1, source_target_pairs={{4,256},{8,260},{12,264},{16,268},{20,272},{24,276},{28,280},{32,2... | collective-permute-start | bytes 221192 | tf_op jit(solution)/shard_map/ppermute | solution.py:114
  126.8 4.1 %collective-permute-done.12 = bf16[18,2048]{1,0:T(8,128)(2,1)S(1)} collective-permute-done((bf16[18,2048]{1,0:T(8,128)(2,1)S(1)}, bf16[18,2048]{1,0:T(8,128)(2,1)S(1)}, u32[]{:S(2)}, u32[]{:S(2)}) %collective-permute-start.12) | collective-permute-done | bytes 73760 | tf_op jit(solution)/shard_map/ppermute | solution.py:114
  132.9 5.1 %collective-permute-done.13 = bf16[18,2048]{1,0:T(8,128)(2,1)S(1)} collective-permute-done((bf16[18,2048]{1,0:T(8,128)(2,1)S(1)}, bf16[18,2048]{1,0:T(8,128)(2,1)S(1)}, u32[]{:S(2)}, u32[]{:S(2)}) %collective-permute-start.13) | collective-permute-done | bytes 73760 | tf_op jit(solution)/shard_map/ppermute | solution.py:114
  140.0 3.3 %collective-permute-done.14 = bf16[18,2048]{1,0:T(8,128)(2,1)S(1)} collective-permute-done((bf16[18,2048]{1,0:T(8,128)(2,1)S(1)}, bf16[18,2048]{1,0:T(8,128)(2,1)S(1)}, u32[]{:S(2)}, u32[]{:S(2)}) %collective-permute-start.14) | collective-permute-done | bytes 73760 | tf_op jit(solution)/shard_map/ppermute | solution.py:114
  143.2 4.0 %collective-permute-start.16 = (bf16[18,2048]{1,0:T(8,128)(2,1)S(1)}, bf16[18,2048]{1,0:T(8,128)(2,1)S(1)}, u32[]{:S(2)}, u32[]{:S(2)}) collective-permute-start(bf16[18,2048]{1,0:T(8,128)(2,1)S(1)} %get-tuple-element.5), channel_id=1, source_target_pairs={{4,768},{8,772},{12,776},{16,780},{20,784},{24,788},{28,792},{32,7... | collective-permute-start | bytes 221192 | tf_op jit(solution)/shard_map/ppermute | solution.py:114
  147.2 8.1 %collective-permute-done.15 = bf16[18,2048]{1,0:T(8,128)(2,1)S(1)} collective-permute-done((bf16[18,2048]{1,0:T(8,128)(2,1)S(1)}, bf16[18,2048]{1,0:T(8,128)(2,1)S(1)}, u32[]{:S(2)}, u32[]{:S(2)}) %collective-permute-start.15) | collective-permute-done | bytes 73760 | tf_op jit(solution)/shard_map/ppermute | solution.py:114
  159.4 5.5 %collective-permute-done.17 = bf16[18,2048]{1,0:T(8,128)(2,1)S(1)} collective-permute-done((bf16[18,2048]{1,0:T(8,128)(2,1)S(1)}, bf16[18,2048]{1,0:T(8,128)(2,1)S(1)}, u32[]{:S(2)}, u32[]{:S(2)}) %collective-permute-start.17) | collective-permute-done | bytes 73760 | tf_op jit(solution)/shard_map/ppermute | solution.py:114
  168.1 4.3 %collective-permute-start.3 = (bf16[512,384]{1,0:T(8,128)(2,1)S(1)}, bf16[512,384]{1,0:T(8,128)(2,1)S(1)}, u32[]{:S(2)}, u32[]{:S(2)}) collective-permute-start(bf16[512,384]{1,0:T(8,128)(2,1)S(1)} %fusion.28), channel_id=1, source_target_pairs={{0,1},{1,2},{2,3},{3,0},{4,5},{5,6},{6,7},{7,4},{8,9},{9,10},{10,1... | collective-permute-start | bytes 1179656 | tf_op jit(solution)/shard_map/ppermute | solution.py:69
  174.6 8.3 %collective-permute-done.6 = bf16[512,384]{1,0:T(8,128)(2,1)S(1)} collective-permute-done((bf16[512,384]{1,0:T(8,128)(2,1)S(1)}, bf16[512,384]{1,0:T(8,128)(2,1)S(1)}, u32[]{:S(2)}, u32[]{:S(2)}) %collective-permute-start.6) | collective-permute-done | bytes 393248 | tf_op jit(solution)/shard_map/ppermute | solution.py:70
  183.0 8.2 %collective-permute-done.3 = bf16[512,384]{1,0:T(8,128)(2,1)S(1)} collective-permute-done((bf16[512,384]{1,0:T(8,128)(2,1)S(1)}, bf16[512,384]{1,0:T(8,128)(2,1)S(1)}, u32[]{:S(2)}, u32[]{:S(2)}) %collective-permute-start.3) | collective-permute-done | bytes 393248 | tf_op jit(solution)/shard_map/ppermute | solution.py:69
  (74 shorter events, 48.9 us)
Async XLA Ops:
  0.6 55.3 %copy-start = (bf16[1,1,2048,768]{3,2,1,0:T(8,128)(2,1)S(1)}, bf16[1,1,2048,768]{3,2,1,0:T(8,128)(2,1)}, u32[]{:S(2)}) copy-start(bf16[1,1,2048,768]{3,2,1,0:T(8,128)(2,1)} %param.10) | copy-start | bytes 9437188
  8.8 6.7 %copy-start.5 = (s32[1,1,128]{2,1,0:T(1,128)S(1)}, s32[1,1,128]{2,1,0:T(1,128)}, u32[]{:S(2)}) copy-start(s32[1,1,128]{2,1,0:T(1,128)} %param.9) | copy-start | bytes 1540
  8.8 39.9 %all-to-all-start = ((bf16[8,18,4096]{2,1,0:T(8,128)(2,1)}), bf16[8,18,4096]{2,1,0:T(8,128)(2,1)}, u32[]{:S(2)}, u32[]{:S(2)}) async-start(bf16[8,18,4096]{2,1,0:T(8,128)(2,1)} %all_to_all.8), calls=%async_computation | async-start | bytes 3145728 | tf_op jit(solution)/shard_map/all_to_all | solution.py:97
  15.5 40.0 %collective-permute-start.8 = (s32[128]{0:T(128)S(1)}, s32[128]{0:T(128)S(1)}, u32[]{:S(2)}, u32[]{:S(2)}) collective-permute-start(s32[128]{0:T(128)S(1)} %bitcast.105), channel_id=1, source_target_pairs={{4,0},{8,4},{12,8},{16,12},{20,16},{24,20},{28,24},{32,28},{36,32}... | collective-permute-start | bytes 1544 | tf_op jit(solution)/shard_map/ppermute | solution.py:10
  18.3 154.1 %collective-permute-start.7 = (bf16[128,2048]{1,0:T(8,128)(2,1)}, bf16[128,2048]{1,0:T(8,128)(2,1)}, u32[]{:S(2)}, u32[]{:S(2)}) collective-permute-start(bf16[128,2048]{1,0:T(8,128)(2,1)} %bitcast.101), channel_id=1, source_target_pairs={{4,0},{8,4},{12,8},{16,12},{20,16},{24,20},{28,24},{32,28},{36,32}... | collective-permute-start | bytes 1572872 | tf_op jit(solution)/shard_map/ppermute | solution.py:10
  51.0 8.6 %collective-permute-start = (bf16[144,4096]{1,0:T(8,128)(2,1)}, bf16[144,4096]{1,0:T(8,128)(2,1)}, u32[]{:S(2)}, u32[]{:S(2)}) collective-permute-start(bf16[144,4096]{1,0:T(8,128)(2,1)} %all_to_all.10), channel_id=1, source_target_pairs={{0,64},{64,0},{1,65},{65,1},{2,66},{66,2},{3,67},{67,3},{4,68},{68... | collective-permute-start | bytes 3538952 | tf_op jit(solution)/shard_map/ppermute | solution.py:14
  66.6 5.5 %copy-start.3 = (bf16[4,512,384]{2,1,0:T(8,128)(2,1)}, bf16[4,512,384]{2,1,0:T(8,128)(2,1)S(1)}, u32[]{:S(2)}) copy-start(bf16[4,512,384]{2,1,0:T(8,128)(2,1)S(1)} %get-tuple-element.3) | copy-start | bytes 4718596
  67.4 17.0 %collective-permute-start.4 = (bf16[512,384]{1,0:T(8,128)(2,1)}, bf16[512,384]{1,0:T(8,128)(2,1)}, u32[]{:S(2)}, u32[]{:S(2)}) collective-permute-start(bf16[512,384]{1,0:T(8,128)(2,1)} %dynamic-slice_bitcast_fusion), channel_id=1, source_target_pairs={{0,3},{1,0},{2,1},{3,2},{4,7},{5,4},{6,5},{7,6},{8,11},{9,8},{10,9... | collective-permute-start | bytes 1179656 | tf_op jit(solution)/shard_map/ppermute | solution.py:70
  72.1 18.3 %collective-permute-start.9 = (bf16[144,2048]{1,0:T(8,128)(2,1)}, bf16[144,2048]{1,0:T(8,128)(2,1)}, u32[]{:S(2)}, u32[]{:S(2)}) collective-permute-start(bf16[144,2048]{1,0:T(8,128)(2,1)} %fusion.11), channel_id=1, source_target_pairs={{0,64},{64,0},{1,65},{65,1},{2,66},{66,2},{3,67},{67,3},{4,68},{68... | collective-permute-start | bytes 1769480 | tf_op jit(solution)/shard_map/ppermute | solution.py:14
  76.7 27.7 %collective-permute-start.1 = (bf16[512,384]{1,0:T(8,128)(2,1)}, bf16[512,384]{1,0:T(8,128)(2,1)}, u32[]{:S(2)}, u32[]{:S(2)}) collective-permute-start(bf16[512,384]{1,0:T(8,128)(2,1)} %dynamic-slice_bitcast_fusion.1), channel_id=1, source_target_pairs={{0,1},{1,2},{2,3},{3,0},{4,5},{5,6},{6,7},{7,4},{8,9},{9,10},{10,1... | collective-permute-start | bytes 1179656 | tf_op jit(solution)/shard_map/ppermute | solution.py:69
  86.4 78.5 %collective-permute-start.5 = (bf16[512,384]{1,0:T(8,128)(2,1)}, bf16[512,384]{1,0:T(8,128)(2,1)}, u32[]{:S(2)}, u32[]{:S(2)}) collective-permute-start(bf16[512,384]{1,0:T(8,128)(2,1)} %fusion.26), channel_id=1, source_target_pairs={{0,3},{1,0},{2,1},{3,2},{4,7},{5,4},{6,5},{7,6},{8,11},{9,8},{10,9... | collective-permute-start | bytes 1179656 | tf_op jit(solution)/shard_map/ppermute | solution.py:70
  95.5 8.9 %copy-start.2 = (bf16[4,512,384]{2,1,0:T(8,128)(2,1)S(1)}, bf16[4,512,384]{2,1,0:T(8,128)(2,1)}, u32[]{:S(2)}) copy-start(bf16[4,512,384]{2,1,0:T(8,128)(2,1)} %get-tuple-element.2) | copy-start | bytes 4718596
  96.9 68.0 %copy-start.4 = (bf16[4,512,384]{2,1,0:T(8,128)(2,1)S(1)}, bf16[4,512,384]{2,1,0:T(8,128)(2,1)}, u32[]{:S(2)}) copy-start(bf16[4,512,384]{2,1,0:T(8,128)(2,1)} %copy-done.3) | copy-start | bytes 4718596
  97.0 18.6 %collective-permute-start.10 = (bf16[18,2048]{1,0:T(8,128)(2,1)S(1)}, bf16[18,2048]{1,0:T(8,128)(2,1)S(1)}, u32[]{:S(2)}, u32[]{:S(2)}) collective-permute-start(bf16[18,2048]{1,0:T(8,128)(2,1)S(1)} %get-tuple-element.11), channel_id=1, source_target_pairs={{4,0},{8,4},{12,8},{16,12},{20,16},{24,20},{28,24},{32,28},{36,32}... | collective-permute-start | bytes 221192 | tf_op jit(solution)/shard_map/ppermute | solution.py:114
  105.6 62.4 %collective-permute-start.2 = (bf16[512,384]{1,0:T(8,128)(2,1)S(1)}, bf16[512,384]{1,0:T(8,128)(2,1)S(1)}, u32[]{:S(2)}, u32[]{:S(2)}) collective-permute-start(bf16[512,384]{1,0:T(8,128)(2,1)S(1)} %fusion.29), channel_id=1, source_target_pairs={{0,1},{1,2},{2,3},{3,0},{4,5},{5,6},{6,7},{7,4},{8,9},{9,10},{10,1... | collective-permute-start | bytes 1179656 | tf_op jit(solution)/shard_map/ppermute | solution.py:69
  108.6 16.3 %collective-permute-start.11 = (bf16[18,2048]{1,0:T(8,128)(2,1)S(1)}, bf16[18,2048]{1,0:T(8,128)(2,1)S(1)}, u32[]{:S(2)}, u32[]{:S(2)}) collective-permute-start(bf16[18,2048]{1,0:T(8,128)(2,1)S(1)} %get-tuple-element.10), channel_id=1, source_target_pairs={{4,128},{8,132},{12,136},{16,140},{20,144},{24,148},{28,152},{32,1... | collective-permute-start | bytes 221192 | tf_op jit(solution)/shard_map/ppermute | solution.py:114
  115.6 15.4 %collective-permute-start.12 = (bf16[18,2048]{1,0:T(8,128)(2,1)S(1)}, bf16[18,2048]{1,0:T(8,128)(2,1)S(1)}, u32[]{:S(2)}, u32[]{:S(2)}) collective-permute-start(bf16[18,2048]{1,0:T(8,128)(2,1)S(1)} %get-tuple-element.9), channel_id=1, source_target_pairs={{4,256},{8,260},{12,264},{16,268},{20,272},{24,276},{28,280},{32,2... | collective-permute-start | bytes 221192 | tf_op jit(solution)/shard_map/ppermute | solution.py:114
  124.9 13.2 %collective-permute-start.13 = (bf16[18,2048]{1,0:T(8,128)(2,1)S(1)}, bf16[18,2048]{1,0:T(8,128)(2,1)S(1)}, u32[]{:S(2)}, u32[]{:S(2)}) collective-permute-start(bf16[18,2048]{1,0:T(8,128)(2,1)S(1)} %get-tuple-element.8), channel_id=1, source_target_pairs={{4,384},{8,388},{12,392},{16,396},{20,400},{24,404},{28,408},{32,4... | collective-permute-start | bytes 221192 | tf_op jit(solution)/shard_map/ppermute | solution.py:114
  131.0 12.3 %collective-permute-start.14 = (bf16[18,2048]{1,0:T(8,128)(2,1)S(1)}, bf16[18,2048]{1,0:T(8,128)(2,1)S(1)}, u32[]{:S(2)}, u32[]{:S(2)}) collective-permute-start(bf16[18,2048]{1,0:T(8,128)(2,1)S(1)} %get-tuple-element.7), channel_id=1, source_target_pairs={{4,512},{8,516},{12,520},{16,524},{20,528},{24,532},{28,536},{32,5... | collective-permute-start | bytes 221192 | tf_op jit(solution)/shard_map/ppermute | solution.py:114
  138.0 17.3 %collective-permute-start.15 = (bf16[18,2048]{1,0:T(8,128)(2,1)S(1)}, bf16[18,2048]{1,0:T(8,128)(2,1)S(1)}, u32[]{:S(2)}, u32[]{:S(2)}) collective-permute-start(bf16[18,2048]{1,0:T(8,128)(2,1)S(1)} %get-tuple-element.6), channel_id=1, source_target_pairs={{4,640},{8,644},{12,648},{16,652},{20,656},{24,660},{28,664},{32,6... | collective-permute-start | bytes 221192 | tf_op jit(solution)/shard_map/ppermute | solution.py:114
  143.2 16.1 %collective-permute-start.16 = (bf16[18,2048]{1,0:T(8,128)(2,1)S(1)}, bf16[18,2048]{1,0:T(8,128)(2,1)S(1)}, u32[]{:S(2)}, u32[]{:S(2)}) collective-permute-start(bf16[18,2048]{1,0:T(8,128)(2,1)S(1)} %get-tuple-element.5), channel_id=1, source_target_pairs={{4,768},{8,772},{12,776},{16,780},{20,784},{24,788},{28,792},{32,7... | collective-permute-start | bytes 221192 | tf_op jit(solution)/shard_map/ppermute | solution.py:114
  155.4 9.6 %collective-permute-start.17 = (bf16[18,2048]{1,0:T(8,128)(2,1)S(1)}, bf16[18,2048]{1,0:T(8,128)(2,1)S(1)}, u32[]{:S(2)}, u32[]{:S(2)}) collective-permute-start(bf16[18,2048]{1,0:T(8,128)(2,1)S(1)} %get-tuple-element.4), channel_id=1, source_target_pairs={{4,896},{8,900},{12,904},{16,908},{20,912},{24,916},{28,920},{32,9... | collective-permute-start | bytes 221192 | tf_op jit(solution)/shard_map/ppermute | solution.py:114
  166.1 16.9 %collective-permute-start.6 = (bf16[512,384]{1,0:T(8,128)(2,1)S(1)}, bf16[512,384]{1,0:T(8,128)(2,1)S(1)}, u32[]{:S(2)}, u32[]{:S(2)}) collective-permute-start(bf16[512,384]{1,0:T(8,128)(2,1)S(1)} %fusion.25), channel_id=1, source_target_pairs={{0,3},{1,0},{2,1},{3,2},{4,7},{5,4},{6,5},{7,6},{8,11},{9,8},{10,9... | collective-permute-start | bytes 1179656 | tf_op jit(solution)/shard_map/ppermute | solution.py:70
  168.1 23.1 %collective-permute-start.3 = (bf16[512,384]{1,0:T(8,128)(2,1)S(1)}, bf16[512,384]{1,0:T(8,128)(2,1)S(1)}, u32[]{:S(2)}, u32[]{:S(2)}) collective-permute-start(bf16[512,384]{1,0:T(8,128)(2,1)S(1)} %fusion.28), channel_id=1, source_target_pairs={{0,1},{1,2},{2,3},{3,0},{4,5},{5,6},{6,7},{7,4},{8,9},{9,10},{10,1... | collective-permute-start | bytes 1179656 | tf_op jit(solution)/shard_map/ppermute | solution.py:69
  (2 other events, 3.8 us)

commit v4 on v2

--- a/solution.py
+++ b/solution.py
@@ -69,6 +69,7 @@
     both = jnp.concatenate([token_input, scaled], axis=1)
     send = jnp.dot(placer, both, preferred_element_type=jnp.float32).astype(jnp.bfloat16)
     mine = lax.all_to_all(send, "x", split_axis=0, concat_axis=0, tiled=True)
+    mine, next_grad, next_routes = lax.optimization_barrier((mine, next_grad, next_routes))
     other = swapped(mine)
     grad_mine, gate_mine = expert_half(mine, gate_up, down_proj, width, half_units)
     grad_other, gate_other = expert_half(other, gate_up, down_proj, width, half_units)

time: 179 us -> 176 us (0.983)
  the two profiles are of different devices: /device:TPU:145 before, /device:TPU:287 now
where the time goes in v4:
time: 176 us; the launch traced here: 175 us
  waiting for transfers between devices  76 us (43%)
  starting transfers between devices  51.1 us (29%)
  matrix products  18.1 us (10%)
  between operations  14.4 us (8%)
  local copies, waits for them, and re-layouts  10.4 us (6%)
  other arithmetic  4.81 us (3%)
    ppermute x8, starting transfers between devices, shards(): received.append(lax.ppermute(block, ('x', 'section'), route))  33.5 us
    reduce_scatter x1, waiting for transfers between devices, shards(): lax.psum_scatter((gate_mine + gate_other).astype(jnp.bfloat16), 'dp', sca...  32.2 us
    all_to_all x1, waiting for transfers between devices, shards(): mine = lax.all_to_all(send, 'x', split_axis=0, concat_axis=0, tiled=True)  29.3 us
    ppermute x8, waiting for transfers between devices, shards(): received.append(lax.ppermute(block, ('x', 'section'), route))  13.8 us
    dot_general x6, matrix products, contract(): lax.dot_general(left, right, (((left_dim,), (right_dim,)), ((), ())), pre...  11 us
    ppermute x2, starting transfers between devices, swapped(): return lax.ppermute(block, 'core', [(0, 1), (1, 0)])  7 us
    all_to_all x1, starting transfers between devices, shards(): mine = lax.all_to_all(send, 'x', split_axis=0, concat_axis=0, tiled=True)  6.69 us
    all_to_all x2, local copies, waits for them, and re-layouts, shards(): mine = lax.all_to_all(send, 'x', split_axis=0, concat_axis=0, tiled=True)  4.76 us
  transfers between devices with their start and end apart: 14, of which 7 were waited for; matrix products, arithmetic and copies ran while one was open for 10% of the time, Pallas kernels for 0%

profile of v4, /device:TPU:287, one launch (start us, length us, event | category | flops | bytes accessed | tf_op | source)
XLA Modules:
  0.0 174.8 jit_solution(15524292199061346002)
XLA Ops:
  10.3 2.6 %convolution_convert_fusion = bf16[144,4096]{1,0:T(8,128)(2,1)} fusion(bf16[128,2048]{1,0:T(8,128)(2,1)S(1)} %multiply_convert_fusion, bf16[128,2048]{1,0:T(8,128)(2,1)} %bitcast.73, s32[128]{0:T(128)S(1)} %select_reduce_fusion.1, s32[128]{0:T(128)} %bitcast.77, s32[144]{0:T(256)S(1)} %get-tuple-element.20, s32[144]{0:T(256)S(1)} %get-tuple-element.21), kind=kOutput, calls=%fused_computation.2 | convolution fusion | flops 153737216 | bytes 2230400 | tf_op jit(solution)/shard_map/dot_general | solution.py:70
  12.9 2.4 %all_to_all.8 = bf16[8,18,4096]{2,1,0:T(8,128)(2,1)} reshape(bf16[144,4096]{1,0:T(8,128)(2,1)} %convolution_convert_fusion) | data formatting | bytes 2359296 | tf_op jit(solution)/shard_map/all_to_all | solution.py:71
  15.3 6.7 %all-to-all-start = ((bf16[8,18,4096]{2,1,0:T(8,128)(2,1)}), bf16[8,18,4096]{2,1,0:T(8,128)(2,1)}, u32[]{:S(2)}, u32[]{:S(2)}) async-start(bf16[8,18,4096]{2,1,0:T(8,128)(2,1)} %all_to_all.8), calls=%async_computation | async-start | bytes 3145728 | tf_op jit(solution)/shard_map/all_to_all | solution.py:71
  25.9 29.3 %all-to-all-done = bf16[8,18,4096]{2,1,0:T(8,128)(2,1)} async-done(((bf16[8,18,4096]{2,1,0:T(8,128)(2,1)}), bf16[8,18,4096]{2,1,0:T(8,128)(2,1)}, u32[]{:S(2)}, u32[]{:S(2)}) %all-to-all-start) | async-done | bytes 1179680 | tf_op jit(solution)/shard_map/all_to_all | solution.py:71
  55.2 2.4 %all_to_all.10 = bf16[144,4096]{1,0:T(8,128)(2,1)} reshape(bf16[8,18,4096]{2,1,0:T(8,128)(2,1)} %all-to-all-done) | data formatting | bytes 2359296 | tf_op jit(solution)/shard_map/all_to_all | solution.py:71
  57.6 4.7 %collective-permute-start.2 = (bf16[144,4096]{1,0:T(8,128)(2,1)}, bf16[144,4096]{1,0:T(8,128)(2,1)S(1)}, u32[]{:S(2)}, u32[]{:S(2)}) collective-permute-start(bf16[144,4096]{1,0:T(8,128)(2,1)} %all_to_all.10), channel_id=1, source_target_pairs={{0,64},{64,0},{1,65},{65,1},{2,66},{66,2},{3,67},{67,3},{4,68},{68... | collective-permute-start | bytes 3538952 | tf_op jit(solution)/shard_map/ppermute | solution.py:14
  67.4 2.7 %add_convert_fusion = bf16[2048,768]{1,0:T(8,128)(2,1)} fusion(f32[2048,768]{1,0:T(8,128)S(1)} %fusion.27, bf16[144,4096]{1,0:T(8,128)(2,1)S(1)} %copy-done.1, bf16[144,384]{1,0:T(8,128)(2,1)S(1)} %get-tuple-element.17, bf16[144,384]{1,0:T(8,128)(2,1)S(1)} %get-tuple-element.16), kind=kOutput, calls=%fused_computation.1 | convolution fusion | flops 456572928 | bytes 10248192 | tf_op jit(solution)/shard_map/dot_general | solution.py:18
  70.1 2.9 %fusion.11 = bf16[144,2048]{1,0:T(8,128)(2,1)} fusion(bf16[1,1,2048,768]{3,2,1,0:T(8,128)(2,1)S(1)} %copy-done, bf16[144,384]{1,0:T(8,128)(2,1)} %copy-done.2, bf16[144,384]{1,0:T(8,128)(2,1)S(1)} %get-tuple-element.18), kind=kOutput, calls=%fused_computation.13 | convolution fusion | flops 453722112 | bytes 3956736 | tf_op jit(solution)/shard_map/dot_general | solution.py:18
  73.0 2.3 %collective-permute-start.3 = (bf16[144,2048]{1,0:T(8,128)(2,1)}, bf16[144,2048]{1,0:T(8,128)(2,1)}, u32[]{:S(2)}, u32[]{:S(2)}) collective-permute-start(bf16[144,2048]{1,0:T(8,128)(2,1)} %fusion.11), channel_id=1, source_target_pairs={{0,64},{64,0},{1,65},{65,1},{2,66},{66,2},{3,67},{67,3},{4,68},{68... | collective-permute-start | bytes 1769480 | tf_op jit(solution)/shard_map/ppermute | solution.py:14
  77.2 3.0 %add_convert_fusion.1 = bf16[144,2048]{1,0:T(8,128)(2,1)} fusion(bf16[144,2048]{1,0:T(8,128)(2,1)} %collective-permute-done.3, bf16[1,1,2048,768]{3,2,1,0:T(8,128)(2,1)S(1)} %copy-done, bf16[144,384]{1,0:T(8,128)(2,1)S(1)} %get-tuple-element.17, bf16[144,384]{1,0:T(8,128)(2,1)S(1)} %get-tuple-element.16), kind=kOutput, calls=%fused_computation.19 | convolution fusion | flops 454901760 | bytes 4546560 | tf_op jit(solution)/shard_map/dot_general | solution.py:18
  80.2 2.1 %reshape.130 = bf16[8,18,2048]{2,1,0:T(8,128)(2,1)} reshape(bf16[144,2048]{1,0:T(8,128)(2,1)} %add_convert_fusion.1) | data formatting | bytes 1179648 | tf_op jit(solution)/shard_map/reshape | solution.py:81
  82.4 2.0 %dynamic-slice_bitcast_fusion = (bf16[18,2048]{1,0:T(8,128)(2,1)S(1)}, bf16[18,2048]{1,0:T(8,128)(2,1)S(1)}, bf16[18,2048]{1,0:T(8,128)(2,1)S(1)}, bf16[18,2048]...) fusion(bf16[8,18,2048]{2,1,0:T(8,128)(2,1)} %reshape.130, ...), kind=kLoop, calls=%fused_computation.55 | loop fusion | bytes 1179680 | tf_op jit(solution)/shard_map/jit(dynamic_index_in_dim)/squeeze | solution.py:85
  87.0 4.7 %collective-permute-start.11 = (bf16[18,2048]{1,0:T(8,128)(2,1)S(1)}, bf16[18,2048]{1,0:T(8,128)(2,1)S(1)}, u32[]{:S(2)}, u32[]{:S(2)}) collective-permute-start(bf16[18,2048]{1,0:T(8,128)(2,1)S(1)} %get-tuple-element.8), channel_id=1, source_target_pairs={{4,896},{8,900},{12,904},{16,908},{20,912},{24,916},{28,920},{32,9... | collective-permute-start | bytes 221192 | tf_op jit(solution)/shard_map/ppermute | solution.py:91
  91.8 2.0 %collective-permute-start.10 = (bf16[18,2048]{1,0:T(8,128)(2,1)S(1)}, bf16[18,2048]{1,0:T(8,128)(2,1)S(1)}, u32[]{:S(2)}, u32[]{:S(2)}) collective-permute-start(bf16[18,2048]{1,0:T(8,128)(2,1)S(1)} %get-tuple-element.9), channel_id=1, source_target_pairs={{4,768},{8,772},{12,776},{16,780},{20,784},{24,788},{28,792},{32,7... | collective-permute-start | bytes 221192 | tf_op jit(solution)/shard_map/ppermute | solution.py:91
  93.8 5.4 %collective-permute-start.9 = (bf16[18,2048]{1,0:T(8,128)(2,1)S(1)}, bf16[18,2048]{1,0:T(8,128)(2,1)S(1)}, u32[]{:S(2)}, u32[]{:S(2)}) collective-permute-start(bf16[18,2048]{1,0:T(8,128)(2,1)S(1)} %get-tuple-element.10), channel_id=1, source_target_pairs={{4,640},{8,644},{12,648},{16,652},{20,656},{24,660},{28,664},{32,6... | collective-permute-start | bytes 221192 | tf_op jit(solution)/shard_map/ppermute | solution.py:91
  99.2 2.8 %collective-permute-start.8 = (bf16[18,2048]{1,0:T(8,128)(2,1)}, bf16[18,2048]{1,0:T(8,128)(2,1)S(1)}, u32[]{:S(2)}, u32[]{:S(2)}) collective-permute-start(bf16[18,2048]{1,0:T(8,128)(2,1)} %get-tuple-element.11), channel_id=1, source_target_pairs={{4,512},{8,516},{12,520},{16,524},{20,528},{24,532},{28,536},{32,5... | collective-permute-start | bytes 221192 | tf_op jit(solution)/shard_map/ppermute | solution.py:91
  102.1 3.7 %collective-permute-start.5 = (bf16[18,2048]{1,0:T(8,128)(2,1)}, bf16[18,2048]{1,0:T(8,128)(2,1)S(1)}, u32[]{:S(2)}, u32[]{:S(2)}) collective-permute-start(bf16[18,2048]{1,0:T(8,128)(2,1)} %get-tuple-element.14), channel_id=1, source_target_pairs={{4,128},{8,132},{12,136},{16,140},{20,144},{24,148},{28,152},{32,1... | collective-permute-start | bytes 221192 | tf_op jit(solution)/shard_map/ppermute | solution.py:91
  106.7 7.2 %collective-permute-done.5 = bf16[18,2048]{1,0:T(8,128)(2,1)S(1)} collective-permute-done((bf16[18,2048]{1,0:T(8,128)(2,1)}, bf16[18,2048]{1,0:T(8,128)(2,1)S(1)}, u32[]{:S(2)}, u32[]{:S(2)}) %collective-permute-start.5) | collective-permute-done | bytes 73760 | tf_op jit(solution)/shard_map/ppermute | solution.py:91
  113.9 4.6 %collective-permute-start.6 = (bf16[18,2048]{1,0:T(8,128)(2,1)}, bf16[18,2048]{1,0:T(8,128)(2,1)S(1)}, u32[]{:S(2)}, u32[]{:S(2)}) collective-permute-start(bf16[18,2048]{1,0:T(8,128)(2,1)} %get-tuple-element.13), channel_id=1, source_target_pairs={{4,256},{8,260},{12,264},{16,268},{20,272},{24,276},{28,280},{32,2... | collective-permute-start | bytes 221192 | tf_op jit(solution)/shard_map/ppermute | solution.py:91
  118.5 3.8 %collective-permute-done.6 = bf16[18,2048]{1,0:T(8,128)(2,1)S(1)} collective-permute-done((bf16[18,2048]{1,0:T(8,128)(2,1)}, bf16[18,2048]{1,0:T(8,128)(2,1)S(1)}, u32[]{:S(2)}, u32[]{:S(2)}) %collective-permute-start.6) | collective-permute-done | bytes 73760 | tf_op jit(solution)/shard_map/ppermute | solution.py:91
  122.3 8.2 %collective-permute-start.7 = (bf16[18,2048]{1,0:T(8,128)(2,1)}, bf16[18,2048]{1,0:T(8,128)(2,1)S(1)}, u32[]{:S(2)}, u32[]{:S(2)}) collective-permute-start(bf16[18,2048]{1,0:T(8,128)(2,1)} %get-tuple-element.12), channel_id=1, source_target_pairs={{4,384},{8,388},{12,392},{16,396},{20,400},{24,404},{28,408},{32,4... | collective-permute-start | bytes 221192 | tf_op jit(solution)/shard_map/ppermute | solution.py:91
  130.6 2.8 %collective-permute-done.7 = bf16[18,2048]{1,0:T(8,128)(2,1)S(1)} collective-permute-done((bf16[18,2048]{1,0:T(8,128)(2,1)}, bf16[18,2048]{1,0:T(8,128)(2,1)S(1)}, u32[]{:S(2)}, u32[]{:S(2)}) %collective-permute-start.7) | collective-permute-done | bytes 73760 | tf_op jit(solution)/shard_map/ppermute | solution.py:91
  133.5 2.3 %fusion.26 = bf16[1,1,128,2048]{3,2,1,0:T(8,128)(2,1)} fusion(bf16[128,2048]{1,0:T(8,128)(2,1)} %collective-permute-done, bf16[8,18,2048]{2,1,0:T(8,128)(2,1)S(1)} %bitcast_dynamic-update-slice_fusion, bf16[8,18,128]{2,1,0:T(8,128)(2,1)S(1)} %gather_fusion, pred[8]{0:T(512)(128)(4,1)} %compare_and_fusion), kind=kOutput, calls=%fused_computation.27 | convolution fusion | flops 76302336 | bytes 1675272 | tf_op jit(solution)/shard_map/dot_general | solution.py:96
  135.7 32.2 %reduce-scatter.2.cloned.1.call-done = bf16[512,768]{1,0:T(8,128)(2,1)} async-done(((bf16[2048,768]{1,0:T(8,128)(2,1)}), bf16[512,768]{1,0:T(8,128)(2,1)}) %reduce-scatter.2.cloned.1.call-update) | async-done | bytes 786448 | tf_op jit(solution)/shard_map/reduce_scatter | solution.py:76
  (53 shorter events, 17.6 us)
Async XLA Ops:
  7.2 55.2 %copy-start = (bf16[1,1,2048,768]{3,2,1,0:T(8,128)(2,1)S(1)}, bf16[1,1,2048,768]{3,2,1,0:T(8,128)(2,1)}, u32[]{:S(2)}) copy-start(bf16[1,1,2048,768]{3,2,1,0:T(8,128)(2,1)} %param.10) | copy-start | bytes 9437188
  15.3 8.7 %copy-start.3 = (s32[1,1,128]{2,1,0:T(1,128)S(1)}, s32[1,1,128]{2,1,0:T(1,128)}, u32[]{:S(2)}) copy-start(s32[1,1,128]{2,1,0:T(1,128)} %param.9) | copy-start | bytes 1540
  15.3 39.9 %all-to-all-start = ((bf16[8,18,4096]{2,1,0:T(8,128)(2,1)}), bf16[8,18,4096]{2,1,0:T(8,128)(2,1)}, u32[]{:S(2)}, u32[]{:S(2)}) async-start(bf16[8,18,4096]{2,1,0:T(8,128)(2,1)} %all_to_all.8), calls=%async_computation | async-start | bytes 3145728 | tf_op jit(solution)/shard_map/all_to_all | solution.py:71
  22.0 146.0 %reduce-scatter.2.cloned.1.call-start = ((), (), s32[]{:S(2)}) async-start(), calls=%async_computation.2 | async-start | bytes 3932160 | tf_op jit(solution)/shard_map/reduce_scatter | solution.py:76
  22.0 35.6 %collective-permute-start = (bf16[128,2048]{1,0:T(8,128)(2,1)}, bf16[128,2048]{1,0:T(8,128)(2,1)}, u32[]{:S(2)}, u32[]{:S(2)}) collective-permute-start(bf16[128,2048]{1,0:T(8,128)(2,1)} %bitcast.74), channel_id=1, source_target_pairs={{4,0},{8,4},{12,8},{16,12},{20,16},{24,20},{28,24},{32,28},{36,32}... | collective-permute-start | bytes 1572872 | tf_op jit(solution)/shard_map/ppermute | solution.py:10
  24.0 33.6 %collective-permute-start.1 = (s32[128]{0:T(128)S(1)}, s32[128]{0:T(128)S(1)}, u32[]{:S(2)}, u32[]{:S(2)}) collective-permute-start(s32[128]{0:T(128)S(1)} %bitcast.78), channel_id=1, source_target_pairs={{4,0},{8,4},{12,8},{16,12},{20,16},{24,20},{28,24},{32,28},{36,32}... | collective-permute-start | bytes 1544 | tf_op jit(solution)/shard_map/ppermute | solution.py:10
  57.6 6.5 %copy-start.1 = (bf16[144,4096]{1,0:T(8,128)(2,1)S(1)}, bf16[144,4096]{1,0:T(8,128)(2,1)}, u32[]{:S(2)}) copy-start(bf16[144,4096]{1,0:T(8,128)(2,1)} %all_to_all.10) | copy-start | bytes 3538948
  57.6 6.5 %copy-start.5 = (bf16[1,1,384,2048]{3,2,1,0:T(8,128)(2,1)S(1)}, bf16[1,1,384,2048]{3,2,1,0:T(8,128)(2,1)}, u32[]{:S(2)}) copy-start(bf16[1,1,384,2048]{3,2,1,0:T(8,128)(2,1)} %param.11) | copy-start | bytes 4718596
  57.6 7.4 %collective-permute-start.2 = (bf16[144,4096]{1,0:T(8,128)(2,1)}, bf16[144,4096]{1,0:T(8,128)(2,1)S(1)}, u32[]{:S(2)}, u32[]{:S(2)}) collective-permute-start(bf16[144,4096]{1,0:T(8,128)(2,1)} %all_to_all.10), channel_id=1, source_target_pairs={{0,64},{64,0},{1,65},{65,1},{2,66},{66,2},{3,67},{67,3},{4,68},{68... | collective-permute-start | bytes 3538952 | tf_op jit(solution)/shard_map/ppermute | solution.py:14
  66.3 1.1 copy-start.2
  73.0 4.2 %collective-permute-start.3 = (bf16[144,2048]{1,0:T(8,128)(2,1)}, bf16[144,2048]{1,0:T(8,128)(2,1)}, u32[]{:S(2)}, u32[]{:S(2)}) collective-permute-start(bf16[144,2048]{1,0:T(8,128)(2,1)} %fusion.11), channel_id=1, source_target_pairs={{0,64},{64,0},{1,65},{65,1},{2,66},{66,2},{3,67},{67,3},{4,68},{68... | collective-permute-start | bytes 1769480 | tf_op jit(solution)/shard_map/ppermute | solution.py:14
  80.2 6.1 %copy-start.4 = (s32[128]{0:T(128)S(1)}, s32[128]{0:T(128)}, u32[]{:S(2)}) copy-start(s32[128]{0:T(128)} %select_reduce_fusion) | copy-start | bytes 1540
  84.4 17.7 %collective-permute-start.4 = (bf16[18,2048]{1,0:T(8,128)(2,1)}, bf16[18,2048]{1,0:T(8,128)(2,1)}, u32[]{:S(2)}, u32[]{:S(2)}) collective-permute-start(bf16[18,2048]{1,0:T(8,128)(2,1)} %get-tuple-element.15), channel_id=1, source_target_pairs={{4,0},{8,4},{12,8},{16,12},{20,16},{24,20},{28,24},{32,28},{36,32}... | collective-permute-start | bytes 221192 | tf_op jit(solution)/shard_map/ppermute | solution.py:91
  87.0 46.4 %collective-permute-start.11 = (bf16[18,2048]{1,0:T(8,128)(2,1)S(1)}, bf16[18,2048]{1,0:T(8,128)(2,1)S(1)}, u32[]{:S(2)}, u32[]{:S(2)}) collective-permute-start(bf16[18,2048]{1,0:T(8,128)(2,1)S(1)} %get-tuple-element.8), channel_id=1, source_target_pairs={{4,896},{8,900},{12,904},{16,908},{20,912},{24,916},{28,920},{32,9... | collective-permute-start | bytes 221192 | tf_op jit(solution)/shard_map/ppermute | solution.py:91
  91.8 41.7 %collective-permute-start.10 = (bf16[18,2048]{1,0:T(8,128)(2,1)S(1)}, bf16[18,2048]{1,0:T(8,128)(2,1)S(1)}, u32[]{:S(2)}, u32[]{:S(2)}) collective-permute-start(bf16[18,2048]{1,0:T(8,128)(2,1)S(1)} %get-tuple-element.9), channel_id=1, source_target_pairs={{4,768},{8,772},{12,776},{16,780},{20,784},{24,788},{28,792},{32,7... | collective-permute-start | bytes 221192 | tf_op jit(solution)/shard_map/ppermute | solution.py:91
  93.8 39.6 %collective-permute-start.9 = (bf16[18,2048]{1,0:T(8,128)(2,1)S(1)}, bf16[18,2048]{1,0:T(8,128)(2,1)S(1)}, u32[]{:S(2)}, u32[]{:S(2)}) collective-permute-start(bf16[18,2048]{1,0:T(8,128)(2,1)S(1)} %get-tuple-element.10), channel_id=1, source_target_pairs={{4,640},{8,644},{12,648},{16,652},{20,656},{24,660},{28,664},{32,6... | collective-permute-start | bytes 221192 | tf_op jit(solution)/shard_map/ppermute | solution.py:91
  99.2 34.2 %collective-permute-start.8 = (bf16[18,2048]{1,0:T(8,128)(2,1)}, bf16[18,2048]{1,0:T(8,128)(2,1)S(1)}, u32[]{:S(2)}, u32[]{:S(2)}) collective-permute-start(bf16[18,2048]{1,0:T(8,128)(2,1)} %get-tuple-element.11), channel_id=1, source_target_pairs={{4,512},{8,516},{12,520},{16,524},{20,528},{24,532},{28,536},{32,5... | collective-permute-start | bytes 221192 | tf_op jit(solution)/shard_map/ppermute | solution.py:91
  102.1 11.8 %collective-permute-start.5 = (bf16[18,2048]{1,0:T(8,128)(2,1)}, bf16[18,2048]{1,0:T(8,128)(2,1)S(1)}, u32[]{:S(2)}, u32[]{:S(2)}) collective-permute-start(bf16[18,2048]{1,0:T(8,128)(2,1)} %get-tuple-element.14), channel_id=1, source_target_pairs={{4,128},{8,132},{12,136},{16,140},{20,144},{24,148},{28,152},{32,1... | collective-permute-start | bytes 221192 | tf_op jit(solution)/shard_map/ppermute | solution.py:91
  113.9 8.4 %collective-permute-start.6 = (bf16[18,2048]{1,0:T(8,128)(2,1)}, bf16[18,2048]{1,0:T(8,128)(2,1)S(1)}, u32[]{:S(2)}, u32[]{:S(2)}) collective-permute-start(bf16[18,2048]{1,0:T(8,128)(2,1)} %get-tuple-element.13), channel_id=1, source_target_pairs={{4,256},{8,260},{12,264},{16,268},{20,272},{24,276},{28,280},{32,2... | collective-permute-start | bytes 221192 | tf_op jit(solution)/shard_map/ppermute | solution.py:91
  122.3 11.1 %collective-permute-start.7 = (bf16[18,2048]{1,0:T(8,128)(2,1)}, bf16[18,2048]{1,0:T(8,128)(2,1)S(1)}, u32[]{:S(2)}, u32[]{:S(2)}) collective-permute-start(bf16[18,2048]{1,0:T(8,128)(2,1)} %get-tuple-element.12), channel_id=1, source_target_pairs={{4,384},{8,388},{12,392},{16,396},{20,400},{24,404},{28,408},{32,4... | collective-permute-start | bytes 221192 | tf_op jit(solution)/shard_map/ppermute | solution.py:91
Sparse Core Ops, SparseCore 0:
  70.2 97.7 reduce-scatter.1

commit v5 on v1

--- a/solution.py
+++ b/solution.py
@@ -67,11 +67,12 @@
     returned = lax.all_to_all(paired, "x", split_axis=0, concat_axis=0, tiled=True)
     token_sum = contract(placer, returned, 0, 0)
     in_grad = (token_grad.astype(jnp.float32) + token_sum).astype(jnp.bfloat16)
-    upstream = shifted(in_grad, "section", -1)
     gate_part = contract(input_rows, act_grad, 0, 0)
     gate_sum = lax.psum_scatter(
         gate_part.astype(jnp.bfloat16), "dp", scatter_dimension=0, tiled=True
     )
+    gate_sum, in_grad = lax.optimization_barrier((gate_sum, in_grad))
+    upstream = shifted(in_grad, "section", -1)
     return (gate_sum[None, None], upstream[None, None])
 
 

time: 175 us -> 180 us (1.029); the launches traced: 171 us -> 178 us
  waiting for transfers between devices: 46.4 us -> 53.5 us
    reduce_scatter x1, waiting for transfers between devices: 0.01 us -> 37.1 us  [shards(): lax.psum_scatter(gate_part.astype(jnp.bfloat16), 'dp', scatter_dimension=...]
    ppermute x1, waiting for transfers between devices: 43.4 us -> 13.5 us  [shifted(): return lax.ppermute(block, axis, route)]
  transfers between devices with their start and end apart: 4 -> 4, of which waited for: 3 -> 4; matrix products, arithmetic and copies ran while one was open for 4% -> 4% of each run, Pallas kernels for 0% -> 0%
where the time goes in v5:
time: 180 us; the launch traced here: 178 us
  blocking collectives  63.6 us (35%)
  waiting for transfers between devices  53.5 us (30%)
  starting transfers between devices  18 us (10%)
  between operations  14.2 us (8%)
  matrix products  12.5 us (7%)
  local copies, waits for them, and re-layouts  12.3 us (7%)
  other arithmetic  4.07 us (2%)
    reduce_scatter x1, waiting for transfers between devices, shards(): lax.psum_scatter(gate_part.astype(jnp.bfloat16), 'dp', scatter_dimension=...  37.1 us
    all_to_all x1, blocking collectives, shards(): mine = lax.all_to_all(send, 'x', split_axis=0, concat_axis=0, tiled=True)  35.8 us
    all_to_all x1, blocking collectives, shards(): lax.all_to_all(paired, 'x', split_axis=0, concat_axis=0, tiled=True)  27.8 us
    ppermute x2, starting transfers between devices, swapped(): return lax.ppermute(block, 'core', [(0, 1), (1, 0)])  16.7 us
    ppermute x1, waiting for transfers between devices, shifted(): return lax.ppermute(block, axis, route)  13.5 us
    dot_general x4, matrix products, contract(): lax.dot_general(left, right, (((left_dim,), (right_dim,)), ((), ())), pre...  8.86 us
    all_to_all x2, local copies, waits for them, and re-layouts, shards(): mine = lax.all_to_all(send, 'x', split_axis=0, concat_axis=0, tiled=True)  4.79 us
    all_to_all x2, local copies, waits for them, and re-layouts, shards(): lax.all_to_all(paired, 'x', split_axis=0, concat_axis=0, tiled=True)  4.24 us
  transfers between devices with their start and end apart: 4, of which 4 were waited for; matrix products, arithmetic and copies ran while one was open for 4% of the time, Pallas kernels for 0%

profile of v5, /device:TPU:1, one launch (start us, length us, event | category | flops | bytes accessed | tf_op | source)
XLA Modules:
  0.0 178.2 jit_solution(2693109881998595482)
XLA Ops:
  7.2 0.9 fusion.20
  8.3 0.8 select_reduce_fusion
  9.1 1.2 fusion.11
  10.3 2.6 %convolution_convert_fusion = bf16[144,4096]{1,0:T(8,128)(2,1)} fusion(bf16[128,2048]{1,0:T(8,128)(2,1)S(1)} %fusion.11, bf16[128,2048]{1,0:T(8,128)(2,1)} %bitcast.22, s32[128]{0:T(128)S(1)} %select_reduce_fusion, s32[128]{0:T(128)} %bitcast.26, s32[144]{0:T(256)S(1)} %get-tuple-element.8, s32[144]{0:T(256)S(1)} %get-tuple-element.9), kind=kOutput, calls=%fused_computation | convolution fusion | flops 153737216 | bytes 2230400 | tf_op jit(solution)/shard_map/dot_general | solution.py:43
  12.9 2.4 %all_to_all.16 = bf16[8,18,4096]{2,1,0:T(8,128)(2,1)} reshape(bf16[144,4096]{1,0:T(8,128)(2,1)} %convolution_convert_fusion) | data formatting | bytes 2359296 | tf_op jit(solution)/shard_map/all_to_all | solution.py:44
  15.3 35.8 %all_to_all.24 = bf16[8,18,4096]{2,1,0:T(8,128)(2,1)} all-to-all(bf16[8,18,4096]{2,1,0:T(8,128)(2,1)} %all_to_all.16), channel_id=1, replica_groups=mesh['x'=8,'core'=2,'section'=16,'dp'=4] {'x'}, dimensions={0} | all-to-all | bytes 2359296 | tf_op jit(solution)/shard_map/all_to_all | solution.py:44
  51.2 2.4 %all_to_all.18 = bf16[144,4096]{1,0:T(8,128)(2,1)} reshape(bf16[8,18,4096]{2,1,0:T(8,128)(2,1)} %all_to_all.24) | data formatting | bytes 2359296 | tf_op jit(solution)/shard_map/all_to_all | solution.py:44
  53.6 14.4 %collective-permute-start = (bf16[144,4096]{1,0:T(8,128)(2,1)}, bf16[144,4096]{1,0:T(8,128)(2,1)S(1)}, u32[]{:S(2)}, u32[]{:S(2)}) collective-permute-start(bf16[144,4096]{1,0:T(8,128)(2,1)} %all_to_all.18), channel_id=1, source_target_pairs={{0,64},{64,0},{1,65},{65,1},{2,66},{66,2},{3,67},{67,3},{4,68},{68... | collective-permute-start | bytes 3538952 | tf_op jit(solution)/shard_map/ppermute | solution.py:14
  68.0 1.3 constant_dynamic-update-slice_fusion.1
  69.3 1.3 collective-permute-done
  70.7 1.1 fusion.2
  72.1 0.9 fusion.19
  73.7 3.5 %convolution_convert_fusion.1 = bf16[2048,768]{1,0:T(8,128)(2,1)} fusion(bf16[288,4096]{1,0:T(8,128)(2,1)S(1)} %constant_dynamic-update-slice_fusion, bf16[288,384]{1,0:T(8,128)(2,1)S(1)} %get-tuple-element.7, bf16[288,384]{1,0:T(8,128)(2,1)S(1)} %get-tuple-element.6), kind=kOutput, calls=%fused_computation.1 | convolution fusion | flops 908427264 | bytes 4767744 | tf_op jit(solution)/shard_map/dot_general | solution.py:18
  77.2 2.1 %fusion.4 = bf16[288,2048]{1,0:T(8,128)(2,1)S(1)} fusion(bf16[1,1,2048,768]{3,2,1,0:T(8,128)(2,1)S(1)} %copy-done, bf16[288,384]{1,0:T(8,128)(2,1)} %copy-done.3, bf16[288,384]{1,0:T(8,128)(2,1)S(1)} %get-tuple-element.6), kind=kOutput, calls=%fused_computation.6 | convolution fusion | flops 907444224 | bytes 4767744 | tf_op jit(solution)/shard_map/dot_general | solution.py:18
  79.3 2.3 %collective-permute-start.1 = (bf16[144,2048]{1,0:T(8,128)(2,1)S(1)}, bf16[144,2048]{1,0:T(8,128)(2,1)S(1)}, u32[]{:S(2)}, u32[]{:S(2)}) collective-permute-start(bf16[144,2048]{1,0:T(8,128)(2,1)S(1)} %slice.29), channel_id=1, source_target_pairs={{0,64},{64,0},{1,65},{65,1},{2,66},{66,2},{3,67},{67,3},{4,68},{68... | collective-permute-start | bytes 1769480 | tf_op jit(solution)/shard_map/ppermute | solution.py:14
  81.6 1.6 collective-permute-done.1
  83.2 1.0 add_convert_fusion
  84.2 2.1 %all_to_all.19 = bf16[8,18,2048]{2,1,0:T(8,128)(2,1)} reshape(bf16[144,2048]{1,0:T(8,128)(2,1)} %add_convert_fusion) | data formatting | bytes 1179648 | tf_op jit(solution)/shard_map/all_to_all | solution.py:67
  86.3 27.8 %all_to_all.25 = bf16[8,18,2048]{2,1,0:T(8,128)(2,1)} all-to-all(bf16[8,18,2048]{2,1,0:T(8,128)(2,1)} %all_to_all.19), channel_id=1, replica_groups=mesh['x'=8,'core'=2,'section'=16,'dp'=4] {'x'}, dimensions={0} | all-to-all | bytes 1179648 | tf_op jit(solution)/shard_map/all_to_all | solution.py:67
  114.1 2.1 %all_to_all.21 = bf16[144,2048]{1,0:T(8,128)(2,1)} reshape(bf16[8,18,2048]{2,1,0:T(8,128)(2,1)} %all_to_all.25) | data formatting | bytes 1179648 | tf_op jit(solution)/shard_map/all_to_all | solution.py:67
  116.2 2.4 %fusion.7 = bf16[128,2048]{1,0:T(8,128)(2,1)} fusion(bf16[144,2048]{1,0:T(8,128)(2,1)} %all_to_all.21, bf16[1,1,128,2048]{3,2,1,0:T(8,128)(2,1)} %param.7, s32[128]{0:T(128)S(1)} %select_reduce_fusion, s32[128]{0:T(128)S(1)} %bitcast.27, s32[144]{0:T(256)S(1)} %get-tuple-element.8, s32[144]{0:T(256)S(1)} %get-tuple-element.9), kind=kOutput, calls=%fused_computation.8 | convolution fusion | flops 76339200 | bytes 1640576 | tf_op jit(solution)/shard_map/dot_general | solution.py:18
  118.7 37.1 %reduce-scatter.2.cloned.1.call-done = bf16[512,768]{1,0:T(8,128)(2,1)} async-done(((bf16[2048,768]{1,0:T(8,128)(2,1)}), bf16[512,768]{1,0:T(8,128)(2,1)}) %reduce-scatter.2.cloned.1.call-update) | async-done | bytes 786448 | tf_op jit(solution)/shard_map/reduce_scatter | solution.py:71
  155.7 1.3 collective-permute-start.2
  157.0 13.5 %collective-permute-done.2 = bf16[128,2048]{1,0:T(8,128)(2,1)S(1)} collective-permute-done((bf16[128,2048]{1,0:T(8,128)(2,1)}, bf16[128,2048]{1,0:T(8,128)(2,1)S(1)}, u32[]{:S(2)}, u32[]{:S(2)}) %collective-permute-start.2) | collective-permute-done | bytes 524320 | tf_op jit(solution)/shard_map/ppermute | solution.py:10
  (15 shorter events, 2.1 us)
Async XLA Ops:
  7.2 63.5 %copy-start = (bf16[1,1,2048,768]{3,2,1,0:T(8,128)(2,1)S(1)}, bf16[1,1,2048,768]{3,2,1,0:T(8,128)(2,1)}, u32[]{:S(2)}) copy-start(bf16[1,1,2048,768]{3,2,1,0:T(8,128)(2,1)} %param.10) | copy-start | bytes 9437188
  7.2 148.5 %reduce-scatter.2.cloned.1.call-start = ((), (), s32[]{:S(2)}) async-start(), calls=%async_computation.3 | async-start | bytes 3932160 | tf_op jit(solution)/shard_map/reduce_scatter | solution.py:71
  53.6 17.1 %collective-permute-start = (bf16[144,4096]{1,0:T(8,128)(2,1)}, bf16[144,4096]{1,0:T(8,128)(2,1)S(1)}, u32[]{:S(2)}, u32[]{:S(2)}) collective-permute-start(bf16[144,4096]{1,0:T(8,128)(2,1)} %all_to_all.18), channel_id=1, source_target_pairs={{0,64},{64,0},{1,65},{65,1},{2,66},{66,2},{3,67},{67,3},{4,68},{68... | collective-permute-start | bytes 3538952 | tf_op jit(solution)/shard_map/ppermute | solution.py:14
  70.7 1.4 copy-start.2
  73.0 0.7 copy-start.3
  79.3 3.9 %collective-permute-start.1 = (bf16[144,2048]{1,0:T(8,128)(2,1)S(1)}, bf16[144,2048]{1,0:T(8,128)(2,1)S(1)}, u32[]{:S(2)}, u32[]{:S(2)}) collective-permute-start(bf16[144,2048]{1,0:T(8,128)(2,1)S(1)} %slice.29), channel_id=1, source_target_pairs={{0,64},{64,0},{1,65},{65,1},{2,66},{66,2},{3,67},{67,3},{4,68},{68... | collective-permute-start | bytes 1769480 | tf_op jit(solution)/shard_map/ppermute | solution.py:14
  84.2 32.0 %copy-start.1 = (s32[1,1,128]{2,1,0:T(1,128)S(1)}, s32[1,1,128]{2,1,0:T(1,128)}, u32[]{:S(2)}) copy-start(s32[1,1,128]{2,1,0:T(1,128)} %param.9) | copy-start | bytes 1540
  155.7 14.8 %collective-permute-start.2 = (bf16[128,2048]{1,0:T(8,128)(2,1)}, bf16[128,2048]{1,0:T(8,128)(2,1)S(1)}, u32[]{:S(2)}, u32[]{:S(2)}) collective-permute-start(bf16[128,2048]{1,0:T(8,128)(2,1)} %fusion.7), channel_id=1, source_target_pairs={{4,0},{8,4},{12,8},{16,12},{20,16},{24,20},{28,24},{32,28},{36,32}... | collective-permute-start | bytes 1572872 | tf_op jit(solution)/shard_map/ppermute | solution.py:10
Sparse Core Ops, SparseCore 0:
  77.3 78.3 reduce-scatter.1

commit v6 on v1

--- a/solution.py
+++ b/solution.py
@@ -12,6 +12,14 @@
 
 def swapped(block):
     return lax.ppermute(block, "core", [(0, 1), (1, 0)])
+
+
+def exchanged(rows, parts):
+    lanes = 128
+    count, width = rows.shape
+    blocks = rows.reshape(parts, count * width // (parts * lanes), lanes)
+    moved = lax.all_to_all(blocks, "x", split_axis=0, concat_axis=0, tiled=True)
+    return moved.reshape(count, width)
 
 
 def contract(left, right, left_dim, right_dim):
@@ -41,7 +49,7 @@
     scaled = (weights_tok[:, None] * token_grad.astype(jnp.float32)).astype(jnp.bfloat16)
     both = jnp.concatenate([token_input, scaled], axis=1)
     send = jnp.dot(placer, both, preferred_element_type=jnp.float32).astype(jnp.bfloat16)
-    mine = lax.all_to_all(send, "x", split_axis=0, concat_axis=0, tiled=True)
+    mine = exchanged(send, chips)
     other = swapped(mine)
     rows = jnp.concatenate([mine, other], axis=0)
     input_rows = rows[:, :width]
@@ -64,7 +72,7 @@
     paired = (row_grad[:local_rows].astype(jnp.float32) + partner_part.astype(jnp.float32)).astype(
         jnp.bfloat16
     )
-    returned = lax.all_to_all(paired, "x", split_axis=0, concat_axis=0, tiled=True)
+    returned = exchanged(paired, chips)
     token_sum = contract(placer, returned, 0, 0)
     in_grad = (token_grad.astype(jnp.float32) + token_sum).astype(jnp.bfloat16)
     upstream = shifted(in_grad, "section", -1)

time: 175 us -> 168 us (0.960)
  the two profiles are of different devices: /device:TPU:1 before, /device:TPU:17 now
where the time goes in v6:
time: 168 us; the launch traced here: 167 us
  blocking collectives  60.5 us (36%)
  waiting for transfers between devices  53.4 us (32%)
  local copies, waits for them, and re-layouts  14.6 us (9%)
  between operations  14.2 us (8%)
  matrix products  11.8 us (7%)
  starting transfers between devices  8.27 us (5%)
  other arithmetic  4.07 us (2%)
    all_to_all x2, blocking collectives, exchanged(): moved = lax.all_to_all(blocks, 'x', split_axis=0, concat_axis=0, tiled=True)  60.5 us
    ppermute x1, waiting for transfers between devices, shifted(): return lax.ppermute(block, axis, route)  46.1 us
    dot_general x4, matrix products, contract(): lax.dot_general(left, right, (((left_dim,), (right_dim,)), ((), ())), pre...  8.05 us
    ppermute x2, starting transfers between devices, swapped(): return lax.ppermute(block, 'core', [(0, 1), (1, 0)])  6.28 us
    reshape x2, local copies, waits for them, and re-layouts, exchanged(): blocks = rows.reshape(parts, count * width // (parts * lanes), lanes)  5.17 us
    reshape x2, local copies, waits for them, and re-layouts, exchanged(): return moved.reshape(count, width)  5.13 us
    reduce_scatter x1, waiting for transfers between devices, shards(): lax.psum_scatter(gate_part.astype(jnp.bfloat16), 'dp', scatter_dimension=...  4.39 us
    unnamed x10, local copies, waits for them, and re-layouts  4.22 us
  transfers between devices with their start and end apart: 4, of which 4 were waited for; matrix products, arithmetic and copies ran while one was open for 6% of the time, Pallas kernels for 0%

profile of v6, /device:TPU:17, one launch (start us, length us, event | category | flops | bytes accessed | tf_op | source)
XLA Modules:
  0.0 166.8 jit_solution(8127724137392835810)
XLA Ops:
  7.2 0.9 fusion.20
  9.1 1.2 fusion.11
  10.3 2.6 %convolution_convert_fusion = bf16[144,4096]{1,0:T(8,128)(2,1)} fusion(bf16[128,2048]{1,0:T(8,128)(2,1)S(1)} %fusion.11, bf16[128,2048]{1,0:T(8,128)(2,1)} %bitcast.22, s32[128]{0:T(128)S(1)} %select_reduce_fusion, s32[128]{0:T(128)} %bitcast.25, s32[144]{0:T(256)S(1)} %get-tuple-element.4, s32[144]{0:T(256)S(1)} %get-tuple-element.5), kind=kOutput, calls=%fused_computation | convolution fusion | flops 153737216 | bytes 2230400 | tf_op jit(solution)/shard_map/dot_general | solution.py:51
  13.0 3.1 %reshape.57 = bf16[8,576,128]{2,1,0:T(8,128)(2,1)} reshape(bf16[144,4096]{1,0:T(8,128)(2,1)} %convolution_convert_fusion) | data formatting | bytes 2359296 | tf_op jit(solution)/shard_map/reshape | solution.py:20
  16.0 37.0 %all_to_all.10 = bf16[8,576,128]{2,1,0:T(8,128)(2,1)} all-to-all(bf16[8,576,128]{2,1,0:T(8,128)(2,1)} %reshape.57), channel_id=1, replica_groups=mesh['x'=8,'core'=2,'section'=16,'dp'=4] {'x'}, dimensions={0} | all-to-all | bytes 2359296 | tf_op jit(solution)/shard_map/all_to_all | solution.py:21
  53.0 3.0 %reshape.58 = bf16[144,4096]{1,0:T(8,128)(2,1)} reshape(bf16[8,576,128]{2,1,0:T(8,128)(2,1)} %all_to_all.10) | data formatting | bytes 2359296 | tf_op jit(solution)/shard_map/reshape | solution.py:22
  56.0 4.0 %collective-permute-start = (bf16[144,4096]{1,0:T(8,128)(2,1)}, bf16[144,4096]{1,0:T(8,128)(2,1)S(1)}, u32[]{:S(2)}, u32[]{:S(2)}) collective-permute-start(bf16[144,4096]{1,0:T(8,128)(2,1)} %reshape.58), channel_id=1, source_target_pairs={{0,64},{64,0},{1,65},{65,1},{2,66},{66,2},{3,67},{67,3},{4,68},{68... | collective-permute-start | bytes 3538952 | tf_op jit(solution)/shard_map/ppermute | solution.py:14
  60.0 1.3 constant_dynamic-update-slice_fusion.1
  61.4 1.3 collective-permute-done
  62.8 1.1 fusion.2
  64.2 0.9 fusion.19
  65.7 3.5 %convolution_convert_fusion.1 = bf16[2048,768]{1,0:T(8,128)(2,1)} fusion(bf16[288,4096]{1,0:T(8,128)(2,1)S(1)} %constant_dynamic-update-slice_fusion, bf16[288,384]{1,0:T(8,128)(2,1)S(1)} %get-tuple-element.3, bf16[288,384]{1,0:T(8,128)(2,1)S(1)} %get-tuple-element.2), kind=kOutput, calls=%fused_computation.1 | convolution fusion | flops 908427264 | bytes 4767744 | tf_op jit(solution)/shard_map/dot_general | solution.py:26
  69.3 2.1 %fusion.4 = bf16[288,2048]{1,0:T(8,128)(2,1)S(1)} fusion(bf16[1,1,2048,768]{3,2,1,0:T(8,128)(2,1)S(1)} %copy-done, bf16[288,384]{1,0:T(8,128)(2,1)} %copy-done.3, bf16[288,384]{1,0:T(8,128)(2,1)S(1)} %get-tuple-element.2), kind=kOutput, calls=%fused_computation.6 | convolution fusion | flops 907444224 | bytes 4767744 | tf_op jit(solution)/shard_map/dot_general | solution.py:26
  71.4 2.3 %collective-permute-start.1 = (bf16[144,2048]{1,0:T(8,128)(2,1)S(1)}, bf16[144,2048]{1,0:T(8,128)(2,1)S(1)}, u32[]{:S(2)}, u32[]{:S(2)}) collective-permute-start(bf16[144,2048]{1,0:T(8,128)(2,1)S(1)} %slice.29), channel_id=1, source_target_pairs={{0,64},{64,0},{1,65},{65,1},{2,66},{66,2},{3,67},{67,3},{4,68},{68... | collective-permute-start | bytes 1769480 | tf_op jit(solution)/shard_map/ppermute | solution.py:14
  73.7 1.6 collective-permute-done.1
  75.3 1.0 add_convert_fusion
  76.3 2.1 %reshape.59 = bf16[8,288,128]{2,1,0:T(8,128)(2,1)} reshape(bf16[144,2048]{1,0:T(8,128)(2,1)} %add_convert_fusion) | data formatting | bytes 1179648 | tf_op jit(solution)/shard_map/reshape | solution.py:20
  78.4 23.6 %all_to_all.11 = bf16[8,288,128]{2,1,0:T(8,128)(2,1)} all-to-all(bf16[8,288,128]{2,1,0:T(8,128)(2,1)} %reshape.59), channel_id=1, replica_groups=mesh['x'=8,'core'=2,'section'=16,'dp'=4] {'x'}, dimensions={0} | all-to-all | bytes 1179648 | tf_op jit(solution)/shard_map/all_to_all | solution.py:21
  101.9 2.1 %reshape.60 = bf16[144,2048]{1,0:T(8,128)(2,1)} reshape(bf16[8,288,128]{2,1,0:T(8,128)(2,1)} %all_to_all.11) | data formatting | bytes 1179648 | tf_op jit(solution)/shard_map/reshape | solution.py:22
  104.0 1.6 fusion.7
  105.7 2.0 %collective-permute-start.2 = (bf16[128,2048]{1,0:T(8,128)(2,1)S(1)}, bf16[128,2048]{1,0:T(8,128)(2,1)}, u32[]{:S(2)}, u32[]{:S(2)}) collective-permute-start(bf16[128,2048]{1,0:T(8,128)(2,1)S(1)} %fusion.7), channel_id=1, source_target_pairs={{4,0},{8,4},{12,8},{16,12},{20,16},{24,20},{28,24},{32,28},{36,32}... | collective-permute-start | bytes 1572872 | tf_op jit(solution)/shard_map/ppermute | solution.py:10
  107.6 46.1 %collective-permute-done.2 = bf16[128,2048]{1,0:T(8,128)(2,1)} collective-permute-done((bf16[128,2048]{1,0:T(8,128)(2,1)S(1)}, bf16[128,2048]{1,0:T(8,128)(2,1)}, u32[]{:S(2)}, u32[]{:S(2)}) %collective-permute-start.2) | collective-permute-done | bytes 524320 | tf_op jit(solution)/shard_map/ppermute | solution.py:10
  153.7 4.4 %reduce-scatter.2.cloned.1.call-done = bf16[512,768]{1,0:T(8,128)(2,1)} async-done(((bf16[2048,768]{1,0:T(8,128)(2,1)}), bf16[512,768]{1,0:T(8,128)(2,1)}) %reduce-scatter.2.cloned.1.call-update) | async-done | bytes 786448 | tf_op jit(solution)/shard_map/reduce_scatter | solution.py:80
  158.1 1.9 %copy.10 = bf16[1,1,128,2048]{3,2,1,0:T(8,128)(2,1)} copy(bf16[1,1,128,2048]{3,2,1,0:T(8,128)(2,1)} %bitcast.8) | data formatting | bytes 1048576
  (15 shorter events, 2.2 us)
Async XLA Ops:
  7.2 55.6 %copy-start = (bf16[1,1,2048,768]{3,2,1,0:T(8,128)(2,1)S(1)}, bf16[1,1,2048,768]{3,2,1,0:T(8,128)(2,1)}, u32[]{:S(2)}) copy-start(bf16[1,1,2048,768]{3,2,1,0:T(8,128)(2,1)} %param.10) | copy-start | bytes 9437188
  7.2 150.9 %reduce-scatter.2.cloned.1.call-start = ((), (), s32[]{:S(2)}) async-start(), calls=%async_computation.3 | async-start | bytes 3932160 | tf_op jit(solution)/shard_map/reduce_scatter | solution.py:80
  56.0 6.7 %collective-permute-start = (bf16[144,4096]{1,0:T(8,128)(2,1)}, bf16[144,4096]{1,0:T(8,128)(2,1)S(1)}, u32[]{:S(2)}, u32[]{:S(2)}) collective-permute-start(bf16[144,4096]{1,0:T(8,128)(2,1)} %reshape.58), channel_id=1, source_target_pairs={{0,64},{64,0},{1,65},{65,1},{2,66},{66,2},{3,67},{67,3},{4,68},{68... | collective-permute-start | bytes 3538952 | tf_op jit(solution)/shard_map/ppermute | solution.py:14
  62.8 1.4 copy-start.2
  65.1 0.7 copy-start.3
  71.4 3.9 %collective-permute-start.1 = (bf16[144,2048]{1,0:T(8,128)(2,1)S(1)}, bf16[144,2048]{1,0:T(8,128)(2,1)S(1)}, u32[]{:S(2)}, u32[]{:S(2)}) collective-permute-start(bf16[144,2048]{1,0:T(8,128)(2,1)S(1)} %slice.29), channel_id=1, source_target_pairs={{0,64},{64,0},{1,65},{65,1},{2,66},{66,2},{3,67},{67,3},{4,68},{68... | collective-permute-start | bytes 1769480 | tf_op jit(solution)/shard_map/ppermute | solution.py:14
  76.3 27.8 %copy-start.1 = (s32[1,1,128]{2,1,0:T(1,128)S(1)}, s32[1,1,128]{2,1,0:T(1,128)}, u32[]{:S(2)}) copy-start(s32[1,1,128]{2,1,0:T(1,128)} %param.9) | copy-start | bytes 1540
  105.7 48.1 %collective-permute-start.2 = (bf16[128,2048]{1,0:T(8,128)(2,1)S(1)}, bf16[128,2048]{1,0:T(8,128)(2,1)}, u32[]{:S(2)}, u32[]{:S(2)}) collective-permute-start(bf16[128,2048]{1,0:T(8,128)(2,1)S(1)} %fusion.7), channel_id=1, source_target_pairs={{4,0},{8,4},{12,8},{16,12},{20,16},{24,20},{28,24},{32,28},{36,32}... | collective-permute-start | bytes 1572872 | tf_op jit(solution)/shard_map/ppermute | solution.py:10
Sparse Core Ops, SparseCore 0:
  69.4 88.6 reduce-scatter.1

commit v7 on v6

--- a/solution.py
+++ b/solution.py
@@ -77,9 +77,15 @@
     in_grad = (token_grad.astype(jnp.float32) + token_sum).astype(jnp.bfloat16)
     upstream = shifted(in_grad, "section", -1)
     gate_part = contract(input_rows, act_grad, 0, 0)
-    gate_sum = lax.psum_scatter(
-        gate_part.astype(jnp.bfloat16), "dp", scatter_dimension=0, tiled=True
-    )
+    gate_total = gate_part.astype(jnp.bfloat16)
+    groups = lax.axis_size("dp")
+    direct_cols = 256
+    ring_cols = gate_total.shape[1] - direct_cols
+    gate_ring = lax.psum_scatter(gate_total[:, :ring_cols], "dp", scatter_dimension=0, tiled=True)
+    direct = gate_total[:, ring_cols:].reshape(groups, gate_total.shape[0] // groups, direct_cols)
+    direct = lax.all_to_all(direct, "dp", split_axis=0, concat_axis=0, tiled=True)
+    gate_direct = jnp.sum(direct.astype(jnp.float32), axis=0).astype(jnp.bfloat16)
+    gate_sum = jnp.concatenate([gate_ring, gate_direct], axis=1)
     return (gate_sum[None, None], upstream[None, None])
 
 

time: 168 us -> 176 us (1.048)
  the two profiles are of different devices: /device:TPU:17 before, /device:TPU:1 now
where the time goes in v7:
time: 176 us; the launch traced here: 175 us
  waiting for transfers between devices  66.5 us (38%)
  starting transfers between devices  29.7 us (17%)
  blocking collectives  27.2 us (15%)
  local copies, waits for them, and re-layouts  19.4 us (11%)
  between operations  14.2 us (8%)
  matrix products  10.9 us (6%)
  other arithmetic  7.51 us (4%)
    all_to_all x1, waiting for transfers between devices, shards(): lax.all_to_all(direct, 'dp', split_axis=0, concat_axis=0, tiled=True)  39.4 us
    all_to_all x1, blocking collectives, exchanged(): moved = lax.all_to_all(blocks, 'x', split_axis=0, concat_axis=0, tiled=True)  27.2 us
    all_to_all x1, waiting for transfers between devices, exchanged(): moved = lax.all_to_all(blocks, 'x', split_axis=0, concat_axis=0, tiled=True)  17.1 us
    ppermute x2, starting transfers between devices, swapped(): return lax.ppermute(block, 'core', [(0, 1), (1, 0)])  16.9 us
    all_to_all x1, starting transfers between devices, shards(): lax.all_to_all(direct, 'dp', split_axis=0, concat_axis=0, tiled=True)  7.27 us
    dot_general x4, matrix products, contract(): lax.dot_general(left, right, (((left_dim,), (right_dim,)), ((), ())), pre...  7.22 us
    ppermute x1, waiting for transfers between devices, shifted(): return lax.ppermute(block, axis, route)  7.02 us
    unnamed x12, local copies, waits for them, and re-layouts  5.2 us
  transfers between devices with their start and end apart: 6, of which 5 were waited for; matrix products, arithmetic and copies ran while one was open for 8% of the time, Pallas kernels for 0%

profile of v7, /device:TPU:1, one launch (start us, length us, event | category | flops | bytes accessed | tf_op | source)
XLA Modules:
  0.0 175.3 jit_solution(3354800048229775383)
XLA Ops:
  10.3 2.6 %convolution_convert_fusion = bf16[144,4096]{1,0:T(8,128)(2,1)} fusion(bf16[128,2048]{1,0:T(8,128)(2,1)S(1)} %fusion.11, bf16[128,2048]{1,0:T(8,128)(2,1)} %bitcast.25, s32[128]{0:T(128)S(1)} %select_reduce_fusion, s32[128]{0:T(128)} %bitcast.28, s32[144]{0:T(256)S(1)} %get-tuple-element.4, s32[144]{0:T(256)S(1)} %get-tuple-element.5), kind=kOutput, calls=%fused_computation | convolution fusion | flops 153737216 | bytes 2230400 | tf_op jit(solution)/shard_map/dot_general | solution.py:51
  12.9 3.1 %reshape.60 = bf16[8,576,128]{2,1,0:T(8,128)(2,1)} reshape(bf16[144,4096]{1,0:T(8,128)(2,1)} %convolution_convert_fusion) | data formatting | bytes 2359296 | tf_op jit(solution)/shard_map/reshape | solution.py:20
  16.0 27.2 %all_to_all.15 = bf16[8,576,128]{2,1,0:T(8,128)(2,1)} all-to-all(bf16[8,576,128]{2,1,0:T(8,128)(2,1)} %reshape.60), channel_id=1, replica_groups=mesh['x'=8,'core'=2,'section'=16,'dp'=4] {'x'}, dimensions={0} | all-to-all | bytes 2359296 | tf_op jit(solution)/shard_map/all_to_all | solution.py:21
  43.2 3.0 %reshape.61 = bf16[144,4096]{1,0:T(8,128)(2,1)} reshape(bf16[8,576,128]{2,1,0:T(8,128)(2,1)} %all_to_all.15) | data formatting | bytes 2359296 | tf_op jit(solution)/shard_map/reshape | solution.py:22
  46.2 14.6 %collective-permute-start = (bf16[144,4096]{1,0:T(8,128)(2,1)}, bf16[144,4096]{1,0:T(8,128)(2,1)S(1)}, u32[]{:S(2)}, u32[]{:S(2)}) collective-permute-start(bf16[144,4096]{1,0:T(8,128)(2,1)} %reshape.61), channel_id=1, source_target_pairs={{0,64},{64,0},{1,65},{65,1},{2,66},{66,2},{3,67},{67,3},{4,68},{68... | collective-permute-start | bytes 3538952 | tf_op jit(solution)/shard_map/ppermute | solution.py:14
  60.8 1.3 constant_dynamic-update-slice_fusion.1
  65.9 1.8 %convolution_convert_fusion.1 = bf16[2048,768]{1,0:T(8,128)(2,1)S(1)} fusion(bf16[288,4096]{1,0:T(8,128)(2,1)S(1)} %constant_dynamic-update-slice_fusion, bf16[288,384]{1,0:T(8,128)(2,1)S(1)} %get-tuple-element.3, bf16[288,384]{1,0:T(8,128)(2,1)S(1)} %get-tuple-element.2), kind=kOutput, calls=%fused_computation.1 | convolution fusion | flops 908427264 | bytes 4767744 | tf_op jit(solution)/shard_map/dot_general | solution.py:26
  67.8 1.6 copy-done.1
  69.4 1.5 slice.36
  70.9 2.1 %fusion.4 = bf16[288,2048]{1,0:T(8,128)(2,1)S(1)} fusion(bf16[1,1,2048,768]{3,2,1,0:T(8,128)(2,1)S(1)} %copy-done, bf16[288,384]{1,0:T(8,128)(2,1)} %copy-done.4, bf16[288,384]{1,0:T(8,128)(2,1)S(1)} %get-tuple-element.2), kind=kOutput, calls=%fused_computation.6 | convolution fusion | flops 907444224 | bytes 4767744 | tf_op jit(solution)/shard_map/dot_general | solution.py:26
  73.1 2.3 %collective-permute-start.1 = (bf16[144,2048]{1,0:T(8,128)(2,1)S(1)}, bf16[144,2048]{1,0:T(8,128)(2,1)S(1)}, u32[]{:S(2)}, u32[]{:S(2)}) collective-permute-start(bf16[144,2048]{1,0:T(8,128)(2,1)S(1)} %slice.39), channel_id=1, source_target_pairs={{0,64},{64,0},{1,65},{65,1},{2,66},{66,2},{3,67},{67,3},{4,68},{68... | collective-permute-start | bytes 1769480 | tf_op jit(solution)/shard_map/ppermute | solution.py:14
  75.4 1.6 collective-permute-done.1
  77.9 2.1 %reshape.63 = bf16[8,288,128]{2,1,0:T(8,128)(2,1)} reshape(bf16[144,2048]{1,0:T(8,128)(2,1)} %add_convert_fusion) | data formatting | bytes 1179648 | tf_op jit(solution)/shard_map/reshape | solution.py:20
  80.0 4.2 %all-to-all-start.2 = ((bf16[8,288,128]{2,1,0:T(8,128)(2,1)}), bf16[8,288,128]{2,1,0:T(8,128)(2,1)}, u32[]{:S(2)}, u32[]{:S(2)}) async-start(bf16[8,288,128]{2,1,0:T(8,128)(2,1)} %reshape.63), calls=%async_computation.3 | async-start | bytes 1179648 | tf_op jit(solution)/shard_map/all_to_all | solution.py:21
  84.2 2.3 %slice.37 = bf16[2048,256]{1,0:T(8,128)(2,1)} slice(bf16[2048,768]{1,0:T(8,128)(2,1)} %copy-done.1), slice={[0:2048], [512:768]} | slice | bytes 2097152 | tf_op jit(solution)/shard_map/slice | solution.py:85
  86.5 17.1 %all-to-all-done.2 = bf16[8,288,128]{2,1,0:T(8,128)(2,1)} async-done(((bf16[8,288,128]{2,1,0:T(8,128)(2,1)}), bf16[8,288,128]{2,1,0:T(8,128)(2,1)}, u32[]{:S(2)}, u32[]{:S(2)}) %all-to-all-start.2) | async-done | bytes 589856 | tf_op jit(solution)/shard_map/all_to_all | solution.py:21
  103.7 7.3 %all-to-all-start.1 = ((bf16[4,512,256]{2,1,0:T(8,128)(2,1)}), bf16[4,512,256]{2,1,0:T(8,128)(2,1)}, u32[]{:S(2)}, u32[]{:S(2)}) async-start(bf16[4,512,256]{2,1,0:T(8,128)(2,1)} %bitcast.24), calls=%async_computation.2 | async-start | bytes 2097152 | tf_op jit(solution)/shard_map/all_to_all | solution.py:86
  110.9 2.1 %reshape.64 = bf16[144,2048]{1,0:T(8,128)(2,1)} reshape(bf16[8,288,128]{2,1,0:T(8,128)(2,1)} %all-to-all-done.2) | data formatting | bytes 1179648 | tf_op jit(solution)/shard_map/reshape | solution.py:22
  113.0 2.4 %fusion.7 = bf16[128,2048]{1,0:T(8,128)(2,1)} fusion(bf16[144,2048]{1,0:T(8,128)(2,1)} %reshape.64, bf16[1,1,128,2048]{3,2,1,0:T(8,128)(2,1)} %param.7, s32[128]{0:T(128)S(1)} %select_reduce_fusion, s32[128]{0:T(128)S(1)} %bitcast.29, s32[144]{0:T(256)S(1)} %get-tuple-element.4, s32[144]{0:T(256)S(1)} %get-tuple-element.5), kind=kOutput, calls=%fused_computation.8 | convolution fusion | flops 76339200 | bytes 1640576 | tf_op jit(solution)/shard_map/dot_general | solution.py:26
  116.7 39.4 %all-to-all-done.1 = bf16[4,512,256]{2,1,0:T(8,128)(2,1)} async-done(((bf16[4,512,256]{2,1,0:T(8,128)(2,1)}), bf16[4,512,256]{2,1,0:T(8,128)(2,1)}, u32[]{:S(2)}, u32[]{:S(2)}) %all-to-all-start.1) | async-done | bytes 1048608 | tf_op jit(solution)/shard_map/all_to_all | solution.py:86
  156.2 1.5 reduce_sum.22
  157.6 7.0 %collective-permute-done.2 = bf16[128,2048]{1,0:T(8,128)(2,1)} collective-permute-done((bf16[128,2048]{1,0:T(8,128)(2,1)}, bf16[128,2048]{1,0:T(8,128)(2,1)}, u32[]{:S(2)}, u32[]{:S(2)}) %collective-permute-start.2) | collective-permute-done | bytes 524320 | tf_op jit(solution)/shard_map/ppermute | solution.py:10
  164.6 2.0 %maximum_bitcast_fusion = bf16[1,1,512,768]{3,2,1,0:T(8,128)(2,1)} fusion(bf16[512,256]{1,0:T(8,128)(2,1)S(1)} %reduce_sum.22, bf16[512,512]{1,0:T(8,128)(2,1)} %reduce-scatter.2.cloned.1.call-done), kind=kLoop, calls=%fused_computation.20 | loop fusion | flops 1572864 | bytes 1572864 | tf_op jit(solution)/shard_map/broadcast_in_dim | solution.py:89
  166.6 1.9 %copy.10 = bf16[1,1,128,2048]{3,2,1,0:T(8,128)(2,1)} copy(bf16[1,1,128,2048]{3,2,1,0:T(8,128)(2,1)} %bitcast.9) | data formatting | bytes 1048576
  (24 shorter events, 9.1 us)
Async XLA Ops:
  7.2 56.4 %copy-start = (bf16[1,1,2048,768]{3,2,1,0:T(8,128)(2,1)S(1)}, bf16[1,1,2048,768]{3,2,1,0:T(8,128)(2,1)}, u32[]{:S(2)}) copy-start(bf16[1,1,2048,768]{3,2,1,0:T(8,128)(2,1)} %param.10) | copy-start | bytes 9437188
  7.2 157.5 %reduce-scatter.2.cloned.1.call-start = ((), (), s32[]{:S(2)}) async-start(), calls=%async_computation.4 | async-start | bytes 2621440 | tf_op jit(solution)/shard_map/reduce_scatter | solution.py:84
  46.2 17.3 %collective-permute-start = (bf16[144,4096]{1,0:T(8,128)(2,1)}, bf16[144,4096]{1,0:T(8,128)(2,1)S(1)}, u32[]{:S(2)}, u32[]{:S(2)}) collective-permute-start(bf16[144,4096]{1,0:T(8,128)(2,1)} %reshape.61), channel_id=1, source_target_pairs={{0,64},{64,0},{1,65},{65,1},{2,66},{66,2},{3,67},{67,3},{4,68},{68... | collective-permute-start | bytes 3538952 | tf_op jit(solution)/shard_map/ppermute | solution.py:14
  63.6 1.4 copy-start.3
  65.9 1.9 %copy-start.4 = (bf16[288,384]{1,0:T(8,128)(2,1)}, bf16[288,384]{1,0:T(8,128)(2,1)S(1)}, u32[]{:S(2)}) copy-start(bf16[288,384]{1,0:T(8,128)(2,1)S(1)} %get-tuple-element.3) | copy-start | bytes 663556
  67.8 1.7 copy-start.1
  73.1 3.9 %collective-permute-start.1 = (bf16[144,2048]{1,0:T(8,128)(2,1)S(1)}, bf16[144,2048]{1,0:T(8,128)(2,1)S(1)}, u32[]{:S(2)}, u32[]{:S(2)}) collective-permute-start(bf16[144,2048]{1,0:T(8,128)(2,1)S(1)} %slice.39), channel_id=1, source_target_pairs={{0,64},{64,0},{1,65},{65,1},{2,66},{66,2},{3,67},{67,3},{4,68},{68... | collective-permute-start | bytes 1769480 | tf_op jit(solution)/shard_map/ppermute | solution.py:14
  80.0 23.6 %all-to-all-start.2 = ((bf16[8,288,128]{2,1,0:T(8,128)(2,1)}), bf16[8,288,128]{2,1,0:T(8,128)(2,1)}, u32[]{:S(2)}, u32[]{:S(2)}) async-start(bf16[8,288,128]{2,1,0:T(8,128)(2,1)} %reshape.63), calls=%async_computation.3 | async-start | bytes 1179648 | tf_op jit(solution)/shard_map/all_to_all | solution.py:21
  86.5 26.5 %copy-start.2 = (s32[1,1,128]{2,1,0:T(1,128)S(1)}, s32[1,1,128]{2,1,0:T(1,128)}, u32[]{:S(2)}) copy-start(s32[1,1,128]{2,1,0:T(1,128)} %param.9) | copy-start | bytes 1540
  103.7 52.5 %all-to-all-start.1 = ((bf16[4,512,256]{2,1,0:T(8,128)(2,1)}), bf16[4,512,256]{2,1,0:T(8,128)(2,1)}, u32[]{:S(2)}, u32[]{:S(2)}) async-start(bf16[4,512,256]{2,1,0:T(8,128)(2,1)} %bitcast.24), calls=%async_computation.2 | async-start | bytes 2097152 | tf_op jit(solution)/shard_map/all_to_all | solution.py:86
  115.4 49.2 %collective-permute-start.2 = (bf16[128,2048]{1,0:T(8,128)(2,1)}, bf16[128,2048]{1,0:T(8,128)(2,1)}, u32[]{:S(2)}, u32[]{:S(2)}) collective-permute-start(bf16[128,2048]{1,0:T(8,128)(2,1)} %fusion.7), channel_id=1, source_target_pairs={{4,0},{8,4},{12,8},{16,12},{20,16},{24,20},{28,24},{32,28},{36,32}... | collective-permute-start | bytes 1572872 | tf_op jit(solution)/shard_map/ppermute | solution.py:10
Sparse Core Ops, SparseCore 0:
  71.1 72.2 reduce-scatter.1

commit v8 on v6

--- a/solution.py
+++ b/solution.py
@@ -47,13 +47,12 @@
         & (slot_ids[:, None] % cap_rows == slot_rank[None, :])
     ).astype(jnp.bfloat16)
     scaled = (weights_tok[:, None] * token_grad.astype(jnp.float32)).astype(jnp.bfloat16)
-    both = jnp.concatenate([token_input, scaled], axis=1)
-    send = jnp.dot(placer, both, preferred_element_type=jnp.float32).astype(jnp.bfloat16)
-    mine = exchanged(send, chips)
-    other = swapped(mine)
-    rows = jnp.concatenate([mine, other], axis=0)
-    input_rows = rows[:, :width]
-    grad_rows = rows[:, width:]
+    send_input = jnp.dot(placer, token_input, preferred_element_type=jnp.float32).astype(jnp.bfloat16)
+    send_grad = jnp.dot(placer, scaled, preferred_element_type=jnp.float32).astype(jnp.bfloat16)
+    mine_input = exchanged(send_input, chips)
+    mine_grad = exchanged(send_grad, chips)
+    input_rows = jnp.concatenate([mine_input, swapped(mine_input)], axis=0)
+    grad_rows = jnp.concatenate([mine_grad, swapped(mine_grad)], axis=0)
     preact = jnp.dot(input_rows, gate_up, preferred_element_type=jnp.float32)
     gate_act = preact[:, :half_units]
     up_act = preact[:, half_units:]

time: 168 us -> 175 us (1.042)
  blocking collectives: 60.5 us -> 23.6 us
  waiting for transfers between devices: 53.4 us -> 81 us
  starting transfers between devices: 8.27 us -> 20.5 us
  local copies, waits for them, and re-layouts: 14.6 us -> 17.9 us
  matrix products: 11.8 us -> 13.6 us
    all_to_all x2 -> x1, blocking collectives: 60.5 us -> 23.6 us  [exchanged(): moved = lax.all_to_all(blocks, 'x', split_axis=0, concat_axis=0, tiled=True)]
    all_to_all x0 -> x2, waiting for transfers between devices: none -> 29.9 us  [exchanged(): moved = lax.all_to_all(blocks, 'x', split_axis=0, concat_axis=0, tiled=True)]
    all_to_all x0 -> x2, starting transfers between devices: none -> 10.7 us  [exchanged(): moved = lax.all_to_all(blocks, 'x', split_axis=0, concat_axis=0, tiled=True)]
    dot_general x1 -> x2, matrix products: 2.61 us -> 4.5 us  [the longest x1 2.26 us: shards(): jnp.dot(placer, scaled, preferred_element_type=jnp.float32)]
    reshape x2 -> x3, local copies, waits for them, and re-layouts: 5.17 us -> 6.35 us  [exchanged(): blocks = rows.reshape(parts, count * width // (parts * lanes), lanes)]
    reshape x2 -> x3, local copies, waits for them, and re-layouts: 5.13 us -> 6.27 us  [exchanged(): return moved.reshape(count, width)]
    ppermute x2 -> x3, starting transfers between devices: 6.28 us -> 6.7 us  [swapped(): return lax.ppermute(block, 'core', [(0, 1), (1, 0)])]
    unnamed x10 -> x14, local copies, waits for them, and re-layouts: 4.22 us -> 4.14 us
  transfers between devices with their start and end apart: 4 -> 7, of which waited for: 4 -> 5; matrix products, arithmetic and copies ran while one was open for 6% -> 12% of each run, Pallas kernels for 0% -> 0%
where the time goes in v8:
time: 175 us; the launch traced here: 174 us
  waiting for transfers between devices  81 us (46%)
  blocking collectives  23.6 us (13%)
  starting transfers between devices  20.5 us (12%)
  local copies, waits for them, and re-layouts  17.9 us (10%)
  between operations  14.2 us (8%)
  matrix products  13.6 us (8%)
  other arithmetic  2.87 us (2%)
    ppermute x1, waiting for transfers between devices, shifted(): return lax.ppermute(block, axis, route)  45 us
    all_to_all x2, waiting for transfers between devices, exchanged(): moved = lax.all_to_all(blocks, 'x', split_axis=0, concat_axis=0, tiled=True)  29.9 us
    all_to_all x1, blocking collectives, exchanged(): moved = lax.all_to_all(blocks, 'x', split_axis=0, concat_axis=0, tiled=True)  23.6 us
    all_to_all x2, starting transfers between devices, exchanged(): moved = lax.all_to_all(blocks, 'x', split_axis=0, concat_axis=0, tiled=True)  10.7 us
    dot_general x4, matrix products, contract(): lax.dot_general(left, right, (((left_dim,), (right_dim,)), ((), ())), pre...  8.04 us
    ppermute x3, starting transfers between devices, swapped(): return lax.ppermute(block, 'core', [(0, 1), (1, 0)])  6.7 us
    reshape x3, local copies, waits for them, and re-layouts, exchanged(): blocks = rows.reshape(parts, count * width // (parts * lanes), lanes)  6.35 us
    reshape x3, local copies, waits for them, and re-layouts, exchanged(): return moved.reshape(count, width)  6.27 us
  transfers between devices with their start and end apart: 7, of which 5 were waited for; matrix products, arithmetic and copies ran while one was open for 12% of the time, Pallas kernels for 0%

profile of v8, /device:TPU:17, one launch (start us, length us, event | category | flops | bytes accessed | tf_op | source)
XLA Modules:
  0.0 173.8 jit_solution(7010046377670324874)
XLA Ops:
  9.1 2.2 %convolution_convert_fusion.2 = bf16[144,2048]{1,0:T(8,128)(2,1)} fusion(bf16[1,1,128,2048]{3,2,1,0:T(8,128)(2,1)} %param.6, s32[128]{0:T(128)S(1)} %select_reduce_fusion, s32[128]{0:T(128)} %bitcast.31, s32[144]{0:T(256)S(1)} %get-tuple-element.4, s32[144]{0:T(256)S(1)} %get-tuple-element.5), kind=kOutput, calls=%fused_computation.8 | convolution fusion | flops 75847680 | bytes 1116288 | tf_op jit(solution)/shard_map/dot_general | solution.py:50
  11.3 2.1 %reshape.63 = bf16[8,288,128]{2,1,0:T(8,128)(2,1)} reshape(bf16[144,2048]{1,0:T(8,128)(2,1)} %convolution_convert_fusion.2) | data formatting | bytes 1179648 | tf_op jit(solution)/shard_map/reshape | solution.py:20
  13.5 6.5 %all-to-all-start = ((bf16[8,288,128]{2,1,0:T(8,128)(2,1)}), bf16[8,288,128]{2,1,0:T(8,128)(2,1)}, u32[]{:S(2)}, u32[]{:S(2)}) async-start(bf16[8,288,128]{2,1,0:T(8,128)(2,1)} %reshape.63), calls=%async_computation | async-start | bytes 1179648 | tf_op jit(solution)/shard_map/all_to_all | solution.py:21
  20.0 2.3 %convolution_convert_fusion.1 = bf16[144,2048]{1,0:T(8,128)(2,1)} fusion(bf16[1,1,128,2048]{3,2,1,0:T(8,128)(2,1)} %param.7, f32[128]{0:T(128)S(1)} %bitcast.34, s32[128]{0:T(128)S(1)} %select_reduce_fusion, s32[128]{0:T(128)S(1)} %bitcast.32, s32[144]{0:T(256)S(1)} %get-tuple-element.4, s32[144]{0:T(256)S(1)} %get-tuple-element.5), kind=kOutput, calls=%fused_computation.7 | convolution fusion | flops 76634112 | bytes 1116800 | tf_op jit(solution)/shard_map/dot_general | solution.py:51
  22.2 2.1 %reshape.65 = bf16[8,288,128]{2,1,0:T(8,128)(2,1)} reshape(bf16[144,2048]{1,0:T(8,128)(2,1)} %convolution_convert_fusion.1) | data formatting | bytes 1179648 | tf_op jit(solution)/shard_map/reshape | solution.py:20
  24.3 15.1 %all-to-all-done = bf16[8,288,128]{2,1,0:T(8,128)(2,1)} async-done(((bf16[8,288,128]{2,1,0:T(8,128)(2,1)}), bf16[8,288,128]{2,1,0:T(8,128)(2,1)}, u32[]{:S(2)}, u32[]{:S(2)}) %all-to-all-start) | async-done | bytes 589856 | tf_op jit(solution)/shard_map/all_to_all | solution.py:21
  39.4 4.2 %all-to-all-start.1 = ((bf16[8,288,128]{2,1,0:T(8,128)(2,1)}), bf16[8,288,128]{2,1,0:T(8,128)(2,1)}, u32[]{:S(2)}, u32[]{:S(2)}) async-start(bf16[8,288,128]{2,1,0:T(8,128)(2,1)} %reshape.65), calls=%async_computation.1 | async-start | bytes 1179648 | tf_op jit(solution)/shard_map/all_to_all | solution.py:21
  43.7 2.1 %reshape.64 = bf16[144,2048]{1,0:T(8,128)(2,1)} reshape(bf16[8,288,128]{2,1,0:T(8,128)(2,1)} %all-to-all-done) | data formatting | bytes 1179648 | tf_op jit(solution)/shard_map/reshape | solution.py:22
  45.7 2.4 %collective-permute-start = (bf16[144,2048]{1,0:T(8,128)(2,1)}, bf16[144,2048]{1,0:T(8,128)(2,1)}, u32[]{:S(2)}, u32[]{:S(2)}) collective-permute-start(bf16[144,2048]{1,0:T(8,128)(2,1)} %reshape.64), channel_id=1, source_target_pairs={{0,64},{64,0},{1,65},{65,1},{2,66},{66,2},{3,67},{67,3},{4,68},{68... | collective-permute-start | bytes 1769480 | tf_op jit(solution)/shard_map/ppermute | solution.py:14
  48.1 14.9 %all-to-all-done.1 = bf16[8,288,128]{2,1,0:T(8,128)(2,1)} async-done(((bf16[8,288,128]{2,1,0:T(8,128)(2,1)}), bf16[8,288,128]{2,1,0:T(8,128)(2,1)}, u32[]{:S(2)}, u32[]{:S(2)}) %all-to-all-start.1) | async-done | bytes 589856 | tf_op jit(solution)/shard_map/all_to_all | solution.py:21
  63.0 2.1 %reshape.66 = bf16[144,2048]{1,0:T(8,128)(2,1)} reshape(bf16[8,288,128]{2,1,0:T(8,128)(2,1)} %all-to-all-done.1) | data formatting | bytes 1179648 | tf_op jit(solution)/shard_map/reshape | solution.py:22
  65.1 2.4 %collective-permute-start.1 = (bf16[144,2048]{1,0:T(8,128)(2,1)}, bf16[144,2048]{1,0:T(8,128)(2,1)S(1)}, u32[]{:S(2)}, u32[]{:S(2)}) collective-permute-start(bf16[144,2048]{1,0:T(8,128)(2,1)} %reshape.66), channel_id=1, source_target_pairs={{0,64},{64,0},{1,65},{65,1},{2,66},{66,2},{3,67},{67,3},{4,68},{68... | collective-permute-start | bytes 1769480 | tf_op jit(solution)/shard_map/ppermute | solution.py:14
  72.9 3.5 %convolution_convert_fusion = bf16[2048,768]{1,0:T(8,128)(2,1)} fusion(bf16[288,2048]{1,0:T(8,128)(2,1)S(1)} %constant_dynamic-update-slice_fusion, bf16[288,384]{1,0:T(8,128)(2,1)S(1)} %get-tuple-element.3, bf16[288,384]{1,0:T(8,128)(2,1)S(1)} %get-tuple-element.2), kind=kOutput, calls=%fused_computation | convolution fusion | flops 908427264 | bytes 4767744 | tf_op jit(solution)/shard_map/dot_general | solution.py:26
  76.4 2.1 %fusion.4 = bf16[288,2048]{1,0:T(8,128)(2,1)S(1)} fusion(bf16[1,1,2048,768]{3,2,1,0:T(8,128)(2,1)S(1)} %copy-done, bf16[288,384]{1,0:T(8,128)(2,1)} %copy-done.5, bf16[288,384]{1,0:T(8,128)(2,1)S(1)} %get-tuple-element.2), kind=kOutput, calls=%fused_computation.5 | convolution fusion | flops 907444224 | bytes 4767744 | tf_op jit(solution)/shard_map/dot_general | solution.py:26
  78.5 1.9 %collective-permute-start.2 = (bf16[144,2048]{1,0:T(8,128)(2,1)S(1)}, bf16[144,2048]{1,0:T(8,128)(2,1)S(1)}, u32[]{:S(2)}, u32[]{:S(2)}) collective-permute-start(bf16[144,2048]{1,0:T(8,128)(2,1)S(1)} %slice.19), channel_id=1, source_target_pairs={{0,64},{64,0},{1,65},{65,1},{2,66},{66,2},{3,67},{67,3},{4,68},{68... | collective-permute-start | bytes 1769480 | tf_op jit(solution)/shard_map/ppermute | solution.py:14
  80.4 2.0 %collective-permute-done.2 = bf16[144,2048]{1,0:T(8,128)(2,1)S(1)} collective-permute-done((bf16[144,2048]{1,0:T(8,128)(2,1)S(1)}, bf16[144,2048]{1,0:T(8,128)(2,1)S(1)}, u32[]{:S(2)}, u32[]{:S(2)}) %collective-permute-start.2) | collective-permute-done | bytes 589856 | tf_op jit(solution)/shard_map/ppermute | solution.py:14
  83.4 2.1 %reshape.67 = bf16[8,288,128]{2,1,0:T(8,128)(2,1)} reshape(bf16[144,2048]{1,0:T(8,128)(2,1)} %add_convert_fusion) | data formatting | bytes 1179648 | tf_op jit(solution)/shard_map/reshape | solution.py:20
  85.5 23.6 %all_to_all.15 = bf16[8,288,128]{2,1,0:T(8,128)(2,1)} all-to-all(bf16[8,288,128]{2,1,0:T(8,128)(2,1)} %reshape.67), channel_id=1, replica_groups=mesh['x'=8,'core'=2,'section'=16,'dp'=4] {'x'}, dimensions={0} | all-to-all | bytes 1179648 | tf_op jit(solution)/shard_map/all_to_all | solution.py:21
  109.1 2.1 %reshape.68 = bf16[144,2048]{1,0:T(8,128)(2,1)} reshape(bf16[8,288,128]{2,1,0:T(8,128)(2,1)} %all_to_all.15) | data formatting | bytes 1179648 | tf_op jit(solution)/shard_map/reshape | solution.py:22
  111.2 1.6 fusion.7
  112.8 3.1 %collective-permute-start.3 = (bf16[128,2048]{1,0:T(8,128)(2,1)S(1)}, bf16[128,2048]{1,0:T(8,128)(2,1)}, u32[]{:S(2)}, u32[]{:S(2)}) collective-permute-start(bf16[128,2048]{1,0:T(8,128)(2,1)S(1)} %fusion.7), channel_id=1, source_target_pairs={{4,0},{8,4},{12,8},{16,12},{20,16},{24,20},{28,24},{32,28},{36,32}... | collective-permute-start | bytes 1572872 | tf_op jit(solution)/shard_map/ppermute | solution.py:10
  115.9 45.0 %collective-permute-done.3 = bf16[128,2048]{1,0:T(8,128)(2,1)} collective-permute-done((bf16[128,2048]{1,0:T(8,128)(2,1)S(1)}, bf16[128,2048]{1,0:T(8,128)(2,1)}, u32[]{:S(2)}, u32[]{:S(2)}) %collective-permute-start.3) | collective-permute-done | bytes 524320 | tf_op jit(solution)/shard_map/ppermute | solution.py:10
  160.9 4.1 %reduce-scatter.2.cloned.1.call-done = bf16[512,768]{1,0:T(8,128)(2,1)} async-done(((bf16[2048,768]{1,0:T(8,128)(2,1)}), bf16[512,768]{1,0:T(8,128)(2,1)}) %reduce-scatter.2.cloned.1.call-update) | async-done | bytes 786448 | tf_op jit(solution)/shard_map/reduce_scatter | solution.py:79
  165.0 1.9 %copy.10 = bf16[1,1,128,2048]{3,2,1,0:T(8,128)(2,1)} copy(bf16[1,1,128,2048]{3,2,1,0:T(8,128)(2,1)} %bitcast.8) | data formatting | bytes 1048576
  (26 shorter events, 8.3 us)
Async XLA Ops:
  7.2 62.5 %copy-start = (bf16[1,1,2048,768]{3,2,1,0:T(8,128)(2,1)S(1)}, bf16[1,1,2048,768]{3,2,1,0:T(8,128)(2,1)}, u32[]{:S(2)}) copy-start(bf16[1,1,2048,768]{3,2,1,0:T(8,128)(2,1)} %param.10) | copy-start | bytes 9437188
  11.3 8.6 %copy-start.2 = (s32[1,1,128]{2,1,0:T(1,128)S(1)}, s32[1,1,128]{2,1,0:T(1,128)}, u32[]{:S(2)}) copy-start(s32[1,1,128]{2,1,0:T(1,128)} %param.9) | copy-start | bytes 1540
  11.3 8.6 %copy-start.3 = (f32[1,1,128]{2,1,0:T(1,128)S(1)}, f32[1,1,128]{2,1,0:T(1,128)}, u32[]{:S(2)}) copy-start(f32[1,1,128]{2,1,0:T(1,128)} %param.8) | copy-start | bytes 1540
  13.5 25.9 %all-to-all-start = ((bf16[8,288,128]{2,1,0:T(8,128)(2,1)}), bf16[8,288,128]{2,1,0:T(8,128)(2,1)}, u32[]{:S(2)}, u32[]{:S(2)}) async-start(bf16[8,288,128]{2,1,0:T(8,128)(2,1)} %reshape.63), calls=%async_computation | async-start | bytes 1179648 | tf_op jit(solution)/shard_map/all_to_all | solution.py:21
  39.4 23.6 %all-to-all-start.1 = ((bf16[8,288,128]{2,1,0:T(8,128)(2,1)}), bf16[8,288,128]{2,1,0:T(8,128)(2,1)}, u32[]{:S(2)}, u32[]{:S(2)}) async-start(bf16[8,288,128]{2,1,0:T(8,128)(2,1)} %reshape.65), calls=%async_computation.1 | async-start | bytes 1179648 | tf_op jit(solution)/shard_map/all_to_all | solution.py:21
  43.6 121.4 %reduce-scatter.2.cloned.1.call-start = ((), (), s32[]{:S(2)}) async-start(), calls=%async_computation.4 | async-start | bytes 3932160 | tf_op jit(solution)/shard_map/reduce_scatter | solution.py:79
  45.7 22.9 %collective-permute-start = (bf16[144,2048]{1,0:T(8,128)(2,1)}, bf16[144,2048]{1,0:T(8,128)(2,1)}, u32[]{:S(2)}, u32[]{:S(2)}) collective-permute-start(bf16[144,2048]{1,0:T(8,128)(2,1)} %reshape.64), channel_id=1, source_target_pairs={{0,64},{64,0},{1,65},{65,1},{2,66},{66,2},{3,67},{67,3},{4,68},{68... | collective-permute-start | bytes 1769480 | tf_op jit(solution)/shard_map/ppermute | solution.py:14
  65.1 5.8 %collective-permute-start.1 = (bf16[144,2048]{1,0:T(8,128)(2,1)}, bf16[144,2048]{1,0:T(8,128)(2,1)S(1)}, u32[]{:S(2)}, u32[]{:S(2)}) collective-permute-start(bf16[144,2048]{1,0:T(8,128)(2,1)} %reshape.66), channel_id=1, source_target_pairs={{0,64},{64,0},{1,65},{65,1},{2,66},{66,2},{3,67},{67,3},{4,68},{68... | collective-permute-start | bytes 1769480 | tf_op jit(solution)/shard_map/ppermute | solution.py:14
  69.7 1.1 copy-start.1
  69.7 1.6 copy-start.4
  72.2 0.7 copy-start.5
  78.5 3.9 %collective-permute-start.2 = (bf16[144,2048]{1,0:T(8,128)(2,1)S(1)}, bf16[144,2048]{1,0:T(8,128)(2,1)S(1)}, u32[]{:S(2)}, u32[]{:S(2)}) collective-permute-start(bf16[144,2048]{1,0:T(8,128)(2,1)S(1)} %slice.19), channel_id=1, source_target_pairs={{0,64},{64,0},{1,65},{65,1},{2,66},{66,2},{3,67},{67,3},{4,68},{68... | collective-permute-start | bytes 1769480 | tf_op jit(solution)/shard_map/ppermute | solution.py:14
  112.8 48.1 %collective-permute-start.3 = (bf16[128,2048]{1,0:T(8,128)(2,1)S(1)}, bf16[128,2048]{1,0:T(8,128)(2,1)}, u32[]{:S(2)}, u32[]{:S(2)}) collective-permute-start(bf16[128,2048]{1,0:T(8,128)(2,1)S(1)} %fusion.7), channel_id=1, source_target_pairs={{4,0},{8,4},{12,8},{16,12},{20,16},{24,20},{28,24},{32,28},{36,32}... | collective-permute-start | bytes 1572872 | tf_op jit(solution)/shard_map/ppermute | solution.py:10
Sparse Core Ops, SparseCore 0:
  76.5 88.4 reduce-scatter.1

commit v9 on v4

--- a/solution.py
+++ b/solution.py
@@ -68,7 +68,9 @@
     scaled = (weights_tok[:, None] * token_grad.astype(jnp.float32)).astype(jnp.bfloat16)
     both = jnp.concatenate([token_input, scaled], axis=1)
     send = jnp.dot(placer, both, preferred_element_type=jnp.float32).astype(jnp.bfloat16)
-    mine = lax.all_to_all(send, "x", split_axis=0, concat_axis=0, tiled=True)
+    lanes = 128
+    blocks = send.reshape(chips, send.size // (chips * lanes), lanes)
+    mine = lax.all_to_all(blocks, "x", split_axis=0, concat_axis=0, tiled=True).reshape(send.shape)
     mine, next_grad, next_routes = lax.optimization_barrier((mine, next_grad, next_routes))
     other = swapped(mine)
     grad_mine, gate_mine = expert_half(mine, gate_up, down_proj, width, half_units)
@@ -78,7 +80,7 @@
     )
     partner_part = swapped(grad_other)
     paired = (grad_mine.astype(jnp.float32) + partner_part.astype(jnp.float32)).astype(jnp.bfloat16)
-    paired = paired.reshape(chips, cap_rows, width)
+    paired = paired.reshape(chips, cap_rows * width // lanes, lanes)
     here = lax.axis_index("x")
     received = []
     for shift in range(chips):
@@ -89,7 +91,7 @@
             for s in range(1, sections)
         ]
         received.append(lax.ppermute(block, ("x", "section"), route))
-    returned = jnp.stack(received)
+    returned = jnp.stack(received).reshape(chips, cap_rows, width)
     next_placer = make_placer(next_routes, chips, cap_rows).reshape(chips, cap_rows, tok_count)
     order = (here - jnp.arange(chips, dtype=jnp.int32)) % chips
     placer_by_shift = jnp.take(next_placer, order, axis=0)

time: 176 us -> 166 us (0.943)
  the two profiles are of different devices: /device:TPU:287 before, /device:TPU:149 now
where the time goes in v9:
time: 166 us; the launch traced here: 164 us
  waiting for transfers between devices  65.5 us (39%)
  starting transfers between devices  38.6 us (23%)
  local copies, waits for them, and re-layouts  24 us (14%)
  matrix products  18.1 us (11%)
  between operations  14.5 us (9%)
  other arithmetic  3.71 us (2%)
    reduce_scatter x1, waiting for transfers between devices, shards(): lax.psum_scatter((gate_mine + gate_other).astype(jnp.bfloat16), 'dp', sca...  35.8 us
    all_to_all x1, waiting for transfers between devices, shards(): lax.all_to_all(blocks, 'x', split_axis=0, concat_axis=0, tiled=True)  24.2 us
    ppermute x8, starting transfers between devices, shards(): received.append(lax.ppermute(block, ('x', 'section'), route))  21.2 us
    dot_general x6, matrix products, contract(): lax.dot_general(left, right, (((left_dim,), (right_dim,)), ((), ())), pre...  11 us
    another operation x9, local copies, waits for them, and re-layouts, shards(): returned = jnp.stack(received).reshape(chips, cap_rows, width)  9.13 us
    all_to_all x1, starting transfers between devices, shards(): lax.all_to_all(blocks, 'x', split_axis=0, concat_axis=0, tiled=True)  6.83 us
    ppermute x2, starting transfers between devices, swapped(): return lax.ppermute(block, 'core', [(0, 1), (1, 0)])  6.63 us
    ppermute x2, starting transfers between devices, shifted(): return lax.ppermute(block, axis, route)  3.88 us
  transfers between devices with their start and end apart: 14, of which 7 were waited for; matrix products, arithmetic and copies ran while one was open for 19% of the time, Pallas kernels for 0%

profile of v9, /device:TPU:149, one launch (start us, length us, event | category | flops | bytes accessed | tf_op | source)
XLA Modules:
  0.0 164.5 jit_solution(1151130617210907454)
XLA Ops:
  10.3 2.6 %convolution_convert_fusion = bf16[144,4096]{1,0:T(8,128)(2,1)} fusion(bf16[128,2048]{1,0:T(8,128)(2,1)S(1)} %multiply_convert_fusion, bf16[128,2048]{1,0:T(8,128)(2,1)} %bitcast.57, s32[128]{0:T(128)S(1)} %select_reduce_fusion.1, s32[128]{0:T(128)} %bitcast.61, s32[144]{0:T(256)S(1)} %get-tuple-element.20, s32[144]{0:T(256)S(1)} %get-tuple-element.21), kind=kOutput, calls=%fused_computation.2 | convolution fusion | flops 153737216 | bytes 2230400 | tf_op jit(solution)/shard_map/dot_general | solution.py:70
  12.9 3.1 %reshape.151 = bf16[8,576,128]{2,1,0:T(8,128)(2,1)} reshape(bf16[144,4096]{1,0:T(8,128)(2,1)} %convolution_convert_fusion) | data formatting | bytes 2359296 | tf_op jit(solution)/shard_map/reshape | solution.py:72
  16.0 6.8 %all-to-all-start = ((bf16[8,576,128]{2,1,0:T(8,128)(2,1)}), bf16[8,576,128]{2,1,0:T(8,128)(2,1)}, u32[]{:S(2)}, u32[]{:S(2)}) async-start(bf16[8,576,128]{2,1,0:T(8,128)(2,1)} %reshape.151), calls=%async_computation | async-start | bytes 2359296 | tf_op jit(solution)/shard_map/all_to_all | solution.py:73
  22.8 2.0 %collective-permute-start = (bf16[128,2048]{1,0:T(8,128)(2,1)}, bf16[128,2048]{1,0:T(8,128)(2,1)}, u32[]{:S(2)}, u32[]{:S(2)}) collective-permute-start(bf16[128,2048]{1,0:T(8,128)(2,1)} %bitcast.58), channel_id=1, source_target_pairs={{4,0},{8,4},{12,8},{16,12},{20,16},{24,20},{28,24},{32,28},{36,32}... | collective-permute-start | bytes 1572872 | tf_op jit(solution)/shard_map/ppermute | solution.py:10
  24.8 1.9 %collective-permute-start.1 = (s32[128]{0:T(128)S(1)}, s32[128]{0:T(128)S(1)}, u32[]{:S(2)}, u32[]{:S(2)}) collective-permute-start(s32[128]{0:T(128)S(1)} %bitcast.62), channel_id=1, source_target_pairs={{4,0},{8,4},{12,8},{16,12},{20,16},{24,20},{28,24},{32,28},{36,32}... | collective-permute-start | bytes 1544 | tf_op jit(solution)/shard_map/ppermute | solution.py:10
  26.7 24.2 %all-to-all-done = bf16[8,576,128]{2,1,0:T(8,128)(2,1)} async-done(((bf16[8,576,128]{2,1,0:T(8,128)(2,1)}), bf16[8,576,128]{2,1,0:T(8,128)(2,1)}, u32[]{:S(2)}, u32[]{:S(2)}) %all-to-all-start) | async-done | bytes 1179680 | tf_op jit(solution)/shard_map/all_to_all | solution.py:73
  50.9 3.0 %reshape.152 = bf16[144,4096]{1,0:T(8,128)(2,1)} reshape(bf16[8,576,128]{2,1,0:T(8,128)(2,1)} %all-to-all-done) | data formatting | bytes 2359296 | tf_op jit(solution)/shard_map/reshape | solution.py:73
  54.0 4.4 %collective-permute-start.2 = (bf16[144,4096]{1,0:T(8,128)(2,1)}, bf16[144,4096]{1,0:T(8,128)(2,1)S(1)}, u32[]{:S(2)}, u32[]{:S(2)}) collective-permute-start(bf16[144,4096]{1,0:T(8,128)(2,1)} %reshape.152), channel_id=1, source_target_pairs={{0,64},{64,0},{1,65},{65,1},{2,66},{66,2},{3,67},{67,3},{4,68},{68... | collective-permute-start | bytes 3538952 | tf_op jit(solution)/shard_map/ppermute | solution.py:14
  63.4 2.7 %add_convert_fusion = bf16[2048,768]{1,0:T(8,128)(2,1)} fusion(f32[2048,768]{1,0:T(8,128)S(1)} %fusion.27, bf16[144,4096]{1,0:T(8,128)(2,1)S(1)} %copy-done.1, bf16[144,384]{1,0:T(8,128)(2,1)S(1)} %get-tuple-element.9, bf16[144,384]{1,0:T(8,128)(2,1)S(1)} %get-tuple-element.8), kind=kOutput, calls=%fused_computation.1 | convolution fusion | flops 456572928 | bytes 10248192 | tf_op jit(solution)/shard_map/dot_general | solution.py:18
  66.1 2.9 %fusion.11 = bf16[144,2048]{1,0:T(8,128)(2,1)} fusion(bf16[1,1,2048,768]{3,2,1,0:T(8,128)(2,1)S(1)} %copy-done, bf16[144,384]{1,0:T(8,128)(2,1)} %copy-done.2, bf16[144,384]{1,0:T(8,128)(2,1)S(1)} %get-tuple-element.10), kind=kOutput, calls=%fused_computation.13 | convolution fusion | flops 453722112 | bytes 3956736 | tf_op jit(solution)/shard_map/dot_general | solution.py:18
  69.0 2.3 %collective-permute-start.3 = (bf16[144,2048]{1,0:T(8,128)(2,1)}, bf16[144,2048]{1,0:T(8,128)(2,1)}, u32[]{:S(2)}, u32[]{:S(2)}) collective-permute-start(bf16[144,2048]{1,0:T(8,128)(2,1)} %fusion.11), channel_id=1, source_target_pairs={{0,64},{64,0},{1,65},{65,1},{2,66},{66,2},{3,67},{67,3},{4,68},{68... | collective-permute-start | bytes 1769480 | tf_op jit(solution)/shard_map/ppermute | solution.py:14
  73.2 3.0 %add_convert_fusion.1 = bf16[144,2048]{1,0:T(8,128)(2,1)} fusion(bf16[144,2048]{1,0:T(8,128)(2,1)} %collective-permute-done.3, bf16[1,1,2048,768]{3,2,1,0:T(8,128)(2,1)S(1)} %copy-done, bf16[144,384]{1,0:T(8,128)(2,1)S(1)} %get-tuple-element.9, bf16[144,384]{1,0:T(8,128)(2,1)S(1)} %get-tuple-element.8), kind=kOutput, calls=%fused_computation.19 | convolution fusion | flops 454901760 | bytes 4546560 | tf_op jit(solution)/shard_map/dot_general | solution.py:18
  76.3 2.1 %reshape.153 = bf16[8,288,128]{2,1,0:T(8,128)(2,1)} reshape(bf16[144,2048]{1,0:T(8,128)(2,1)} %add_convert_fusion.1) | data formatting | bytes 1179648 | tf_op jit(solution)/shard_map/reshape | solution.py:83
  78.4 1.9 %dynamic-slice_bitcast_fusion = (bf16[288,128]{1,0:T(8,128)(2,1)S(1)}, bf16[288,128]{1,0:T(8,128)(2,1)S(1)}, bf16[288,128]{1,0:T(8,128)(2,1)S(1)}, bf16[288,128]...) fusion(bf16[8,288,128]{2,1,0:T(8,128)(2,1)} %reshape.153, ...), kind=kLoop, calls=%fused_computation.48 | loop fusion | bytes 1179680 | tf_op jit(solution)/shard_map/jit(dynamic_index_in_dim)/squeeze | solution.py:87
  80.2 3.1 %collective-permute-start.11 = (bf16[288,128]{1,0:T(8,128)(2,1)S(1)}, bf16[288,128]{1,0:T(8,128)(2,1)S(1)}, u32[]{:S(2)}, u32[]{:S(2)}) collective-permute-start(bf16[288,128]{1,0:T(8,128)(2,1)S(1)} %get-tuple-element.12), channel_id=1, source_target_pairs={{4,896},{8,900},{12,904},{16,908},{20,912},{24,916},{28,920},{32,9... | collective-permute-start | bytes 221192 | tf_op jit(solution)/shard_map/ppermute | solution.py:93
  83.3 2.9 %collective-permute-start.10 = (bf16[288,128]{1,0:T(8,128)(2,1)S(1)}, bf16[288,128]{1,0:T(8,128)(2,1)S(1)}, u32[]{:S(2)}, u32[]{:S(2)}) collective-permute-start(bf16[288,128]{1,0:T(8,128)(2,1)S(1)} %get-tuple-element.13), channel_id=1, source_target_pairs={{4,768},{8,772},{12,776},{16,780},{20,784},{24,788},{28,792},{32,7... | collective-permute-start | bytes 221192 | tf_op jit(solution)/shard_map/ppermute | solution.py:93
  86.2 1.9 %collective-permute-start.9 = (bf16[288,128]{1,0:T(8,128)(2,1)S(1)}, bf16[288,128]{1,0:T(8,128)(2,1)S(1)}, u32[]{:S(2)}, u32[]{:S(2)}) collective-permute-start(bf16[288,128]{1,0:T(8,128)(2,1)S(1)} %get-tuple-element.14), channel_id=1, source_target_pairs={{4,640},{8,644},{12,648},{16,652},{20,656},{24,660},{28,664},{32,6... | collective-permute-start | bytes 221192 | tf_op jit(solution)/shard_map/ppermute | solution.py:93
  88.3 4.8 %collective-permute-start.8 = (bf16[288,128]{1,0:T(8,128)(2,1)S(1)}, bf16[288,128]{1,0:T(8,128)(2,1)}, u32[]{:S(2)}, u32[]{:S(2)}) collective-permute-start(bf16[288,128]{1,0:T(8,128)(2,1)S(1)} %get-tuple-element.15), channel_id=1, source_target_pairs={{4,512},{8,516},{12,520},{16,524},{20,528},{24,532},{28,536},{32,5... | collective-permute-start | bytes 221192 | tf_op jit(solution)/shard_map/ppermute | solution.py:93
  93.1 2.8 %collective-permute-start.7 = (bf16[288,128]{1,0:T(8,128)(2,1)}, bf16[288,128]{1,0:T(8,128)(2,1)}, u32[]{:S(2)}, u32[]{:S(2)}) collective-permute-start(bf16[288,128]{1,0:T(8,128)(2,1)} %get-tuple-element.16), channel_id=1, source_target_pairs={{4,384},{8,388},{12,392},{16,396},{20,400},{24,404},{28,408},{32,4... | collective-permute-start | bytes 221192 | tf_op jit(solution)/shard_map/ppermute | solution.py:93
  95.9 1.9 %collective-permute-start.6 = (bf16[288,128]{1,0:T(8,128)(2,1)}, bf16[288,128]{1,0:T(8,128)(2,1)}, u32[]{:S(2)}, u32[]{:S(2)}) collective-permute-start(bf16[288,128]{1,0:T(8,128)(2,1)} %get-tuple-element.17), channel_id=1, source_target_pairs={{4,256},{8,260},{12,264},{16,268},{20,272},{24,276},{28,280},{32,2... | collective-permute-start | bytes 221192 | tf_op jit(solution)/shard_map/ppermute | solution.py:93
  97.9 1.9 %collective-permute-start.5 = (bf16[288,128]{1,0:T(8,128)(2,1)}, bf16[288,128]{1,0:T(8,128)(2,1)}, u32[]{:S(2)}, u32[]{:S(2)}) collective-permute-start(bf16[288,128]{1,0:T(8,128)(2,1)} %get-tuple-element.18), channel_id=1, source_target_pairs={{4,128},{8,132},{12,136},{16,140},{20,144},{24,148},{28,152},{32,1... | collective-permute-start | bytes 221192 | tf_op jit(solution)/shard_map/ppermute | solution.py:93
  99.8 1.9 %collective-permute-start.4 = (bf16[288,128]{1,0:T(8,128)(2,1)}, bf16[288,128]{1,0:T(8,128)(2,1)}, u32[]{:S(2)}, u32[]{:S(2)}) collective-permute-start(bf16[288,128]{1,0:T(8,128)(2,1)} %get-tuple-element.19), channel_id=1, source_target_pairs={{4,0},{8,4},{12,8},{16,12},{20,16},{24,20},{28,24},{32,28},{36,32}... | collective-permute-start | bytes 221192 | tf_op jit(solution)/shard_map/ppermute | solution.py:93
  119.6 2.2 %fusion.26 = bf16[1,1,128,2048]{3,2,1,0:T(8,128)(2,1)} fusion(bf16[128,2048]{1,0:T(8,128)(2,1)} %collective-permute-done, bf16[8,18,2048]{2,1,0:T(8,128)(2,1)S(1)} %constant_dynamic-update-slice_fusion, bf16[8,18,128]{2,1,0:T(8,128)(2,1)S(1)} %copy-done.3, pred[8]{0:T(512)(128)(4,1)S(1)} %compare_and_fusion), kind=kOutput, calls=%fused_computation.27 | convolution fusion | flops 76302336 | bytes 1675272 | tf_op jit(solution)/shard_map/dot_general | solution.py:98
  121.8 35.8 %reduce-scatter.2.cloned.1.call-done = bf16[512,768]{1,0:T(8,128)(2,1)} async-done(((bf16[2048,768]{1,0:T(8,128)(2,1)}), bf16[512,768]{1,0:T(8,128)(2,1)}) %reduce-scatter.2.cloned.1.call-update) | async-done | bytes 786448 | tf_op jit(solution)/shard_map/reduce_scatter | solution.py:78
  (65 shorter events, 27.9 us)
Async XLA Ops:
  7.2 51.2 %copy-start = (bf16[1,1,2048,768]{3,2,1,0:T(8,128)(2,1)S(1)}, bf16[1,1,2048,768]{3,2,1,0:T(8,128)(2,1)}, u32[]{:S(2)}) copy-start(bf16[1,1,2048,768]{3,2,1,0:T(8,128)(2,1)} %param.10) | copy-start | bytes 9437188
  16.0 8.8 %copy-start.6 = (s32[1,1,128]{2,1,0:T(1,128)S(1)}, s32[1,1,128]{2,1,0:T(1,128)}, u32[]{:S(2)}) copy-start(s32[1,1,128]{2,1,0:T(1,128)} %param.9) | copy-start | bytes 1540
  16.0 34.9 %all-to-all-start = ((bf16[8,576,128]{2,1,0:T(8,128)(2,1)}), bf16[8,576,128]{2,1,0:T(8,128)(2,1)}, u32[]{:S(2)}, u32[]{:S(2)}) async-start(bf16[8,576,128]{2,1,0:T(8,128)(2,1)} %reshape.151), calls=%async_computation | async-start | bytes 2359296 | tf_op jit(solution)/shard_map/all_to_all | solution.py:73
  22.8 134.8 %reduce-scatter.2.cloned.1.call-start = ((), (), s32[]{:S(2)}) async-start(), calls=%async_computation.2 | async-start | bytes 3932160 | tf_op jit(solution)/shard_map/reduce_scatter | solution.py:78
  22.8 31.2 %collective-permute-start = (bf16[128,2048]{1,0:T(8,128)(2,1)}, bf16[128,2048]{1,0:T(8,128)(2,1)}, u32[]{:S(2)}, u32[]{:S(2)}) collective-permute-start(bf16[128,2048]{1,0:T(8,128)(2,1)} %bitcast.58), channel_id=1, source_target_pairs={{4,0},{8,4},{12,8},{16,12},{20,16},{24,20},{28,24},{32,28},{36,32}... | collective-permute-start | bytes 1572872 | tf_op jit(solution)/shard_map/ppermute | solution.py:10
  24.8 29.2 %collective-permute-start.1 = (s32[128]{0:T(128)S(1)}, s32[128]{0:T(128)S(1)}, u32[]{:S(2)}, u32[]{:S(2)}) collective-permute-start(s32[128]{0:T(128)S(1)} %bitcast.62), channel_id=1, source_target_pairs={{4,0},{8,4},{12,8},{16,12},{20,16},{24,20},{28,24},{32,28},{36,32}... | collective-permute-start | bytes 1544 | tf_op jit(solution)/shard_map/ppermute | solution.py:10
  54.0 6.1 %copy-start.1 = (bf16[144,4096]{1,0:T(8,128)(2,1)S(1)}, bf16[144,4096]{1,0:T(8,128)(2,1)}, u32[]{:S(2)}) copy-start(bf16[144,4096]{1,0:T(8,128)(2,1)} %reshape.152) | copy-start | bytes 3538948
  54.0 6.1 %copy-start.7 = (bf16[1,1,384,2048]{3,2,1,0:T(8,128)(2,1)S(1)}, bf16[1,1,384,2048]{3,2,1,0:T(8,128)(2,1)}, u32[]{:S(2)}) copy-start(bf16[1,1,384,2048]{3,2,1,0:T(8,128)(2,1)} %param.11) | copy-start | bytes 4718596
  54.0 7.0 %collective-permute-start.2 = (bf16[144,4096]{1,0:T(8,128)(2,1)}, bf16[144,4096]{1,0:T(8,128)(2,1)S(1)}, u32[]{:S(2)}, u32[]{:S(2)}) collective-permute-start(bf16[144,4096]{1,0:T(8,128)(2,1)} %reshape.152), channel_id=1, source_target_pairs={{0,64},{64,0},{1,65},{65,1},{2,66},{66,2},{3,67},{67,3},{4,68},{68... | collective-permute-start | bytes 3538952 | tf_op jit(solution)/shard_map/ppermute | solution.py:14
  62.3 1.1 copy-start.2
  69.0 4.2 %collective-permute-start.3 = (bf16[144,2048]{1,0:T(8,128)(2,1)}, bf16[144,2048]{1,0:T(8,128)(2,1)}, u32[]{:S(2)}, u32[]{:S(2)}) collective-permute-start(bf16[144,2048]{1,0:T(8,128)(2,1)} %fusion.11), channel_id=1, source_target_pairs={{0,64},{64,0},{1,65},{65,1},{2,66},{66,2},{3,67},{67,3},{4,68},{68... | collective-permute-start | bytes 1769480 | tf_op jit(solution)/shard_map/ppermute | solution.py:14
  80.2 15.7 %collective-permute-start.11 = (bf16[288,128]{1,0:T(8,128)(2,1)S(1)}, bf16[288,128]{1,0:T(8,128)(2,1)S(1)}, u32[]{:S(2)}, u32[]{:S(2)}) collective-permute-start(bf16[288,128]{1,0:T(8,128)(2,1)S(1)} %get-tuple-element.12), channel_id=1, source_target_pairs={{4,896},{8,900},{12,904},{16,908},{20,912},{24,916},{28,920},{32,9... | collective-permute-start | bytes 221192 | tf_op jit(solution)/shard_map/ppermute | solution.py:93
  83.3 14.5 %collective-permute-start.10 = (bf16[288,128]{1,0:T(8,128)(2,1)S(1)}, bf16[288,128]{1,0:T(8,128)(2,1)S(1)}, u32[]{:S(2)}, u32[]{:S(2)}) collective-permute-start(bf16[288,128]{1,0:T(8,128)(2,1)S(1)} %get-tuple-element.13), channel_id=1, source_target_pairs={{4,768},{8,772},{12,776},{16,780},{20,784},{24,788},{28,792},{32,7... | collective-permute-start | bytes 221192 | tf_op jit(solution)/shard_map/ppermute | solution.py:93
  86.2 13.6 %collective-permute-start.9 = (bf16[288,128]{1,0:T(8,128)(2,1)S(1)}, bf16[288,128]{1,0:T(8,128)(2,1)S(1)}, u32[]{:S(2)}, u32[]{:S(2)}) collective-permute-start(bf16[288,128]{1,0:T(8,128)(2,1)S(1)} %get-tuple-element.14), channel_id=1, source_target_pairs={{4,640},{8,644},{12,648},{16,652},{20,656},{24,660},{28,664},{32,6... | collective-permute-start | bytes 221192 | tf_op jit(solution)/shard_map/ppermute | solution.py:93
  88.3 16.7 %collective-permute-start.8 = (bf16[288,128]{1,0:T(8,128)(2,1)S(1)}, bf16[288,128]{1,0:T(8,128)(2,1)}, u32[]{:S(2)}, u32[]{:S(2)}) collective-permute-start(bf16[288,128]{1,0:T(8,128)(2,1)S(1)} %get-tuple-element.15), channel_id=1, source_target_pairs={{4,512},{8,516},{12,520},{16,524},{20,528},{24,532},{28,536},{32,5... | collective-permute-start | bytes 221192 | tf_op jit(solution)/shard_map/ppermute | solution.py:93
  93.1 12.8 %collective-permute-start.7 = (bf16[288,128]{1,0:T(8,128)(2,1)}, bf16[288,128]{1,0:T(8,128)(2,1)}, u32[]{:S(2)}, u32[]{:S(2)}) collective-permute-start(bf16[288,128]{1,0:T(8,128)(2,1)} %get-tuple-element.16), channel_id=1, source_target_pairs={{4,384},{8,388},{12,392},{16,396},{20,400},{24,404},{28,408},{32,4... | collective-permute-start | bytes 221192 | tf_op jit(solution)/shard_map/ppermute | solution.py:93
  95.9 13.0 %collective-permute-start.6 = (bf16[288,128]{1,0:T(8,128)(2,1)}, bf16[288,128]{1,0:T(8,128)(2,1)}, u32[]{:S(2)}, u32[]{:S(2)}) collective-permute-start(bf16[288,128]{1,0:T(8,128)(2,1)} %get-tuple-element.17), channel_id=1, source_target_pairs={{4,256},{8,260},{12,264},{16,268},{20,272},{24,276},{28,280},{32,2... | collective-permute-start | bytes 221192 | tf_op jit(solution)/shard_map/ppermute | solution.py:93
  97.9 3.9 %copy-start.4 = (bf16[288,128]{1,0:T(8,128)(2,1)}, bf16[288,128]{1,0:T(8,128)(2,1)S(1)}, u32[]{:S(2)}) copy-start(bf16[288,128]{1,0:T(8,128)(2,1)S(1)} %collective-permute-done.10) | copy-start | bytes 221188
  97.9 13.8 %collective-permute-start.5 = (bf16[288,128]{1,0:T(8,128)(2,1)}, bf16[288,128]{1,0:T(8,128)(2,1)}, u32[]{:S(2)}, u32[]{:S(2)}) collective-permute-start(bf16[288,128]{1,0:T(8,128)(2,1)} %get-tuple-element.18), channel_id=1, source_target_pairs={{4,128},{8,132},{12,136},{16,140},{20,144},{24,148},{28,152},{32,1... | collective-permute-start | bytes 221192 | tf_op jit(solution)/shard_map/ppermute | solution.py:93
  99.8 2.0 %copy-start.5 = (bf16[288,128]{1,0:T(8,128)(2,1)}, bf16[288,128]{1,0:T(8,128)(2,1)S(1)}, u32[]{:S(2)}) copy-start(bf16[288,128]{1,0:T(8,128)(2,1)S(1)} %collective-permute-done.9) | copy-start | bytes 221188
  99.8 14.5 %collective-permute-start.4 = (bf16[288,128]{1,0:T(8,128)(2,1)}, bf16[288,128]{1,0:T(8,128)(2,1)}, u32[]{:S(2)}, u32[]{:S(2)}) collective-permute-start(bf16[288,128]{1,0:T(8,128)(2,1)} %get-tuple-element.19), channel_id=1, source_target_pairs={{4,0},{8,4},{12,8},{16,12},{20,16},{24,20},{28,24},{32,28},{36,32}... | collective-permute-start | bytes 221192 | tf_op jit(solution)/shard_map/ppermute | solution.py:93
  115.9 3.7 %copy-start.3 = (bf16[8,18,128]{2,1,0:T(8,128)(2,1)S(1)}, bf16[8,18,128]{2,1,0:T(8,128)(2,1)}, u32[]{:S(2)}) copy-start(bf16[8,18,128]{2,1,0:T(8,128)(2,1)} %gather_fusion) | copy-start | bytes 110596
Sparse Core Ops, SparseCore 0:
  66.2 91.3 reduce-scatter.1

commit v10 on v9

--- a/solution.py
+++ b/solution.py
@@ -70,9 +70,11 @@
     send = jnp.dot(placer, both, preferred_element_type=jnp.float32).astype(jnp.bfloat16)
     lanes = 128
     blocks = send.reshape(chips, send.size // (chips * lanes), lanes)
-    mine = lax.all_to_all(blocks, "x", split_axis=0, concat_axis=0, tiled=True).reshape(send.shape)
+    arrived = lax.all_to_all(blocks, "x", split_axis=0, concat_axis=0, tiled=True)
+    forwarded = swapped(arrived)
+    mine = arrived.reshape(send.shape)
     mine, next_grad, next_routes = lax.optimization_barrier((mine, next_grad, next_routes))
-    other = swapped(mine)
+    other = forwarded.reshape(send.shape)
     grad_mine, gate_mine = expert_half(mine, gate_up, down_proj, width, half_units)
     grad_other, gate_other = expert_half(other, gate_up, down_proj, width, half_units)
     gate_sum = lax.psum_scatter(

time: 166 us -> 183 us (1.10)
  the two profiles are of different devices: /device:TPU:149 before, /device:TPU:147 now
where the time goes in v10:
time: 183 us; the launch traced here: 182 us
  waiting for transfers between devices  50.4 us (28%)
  blocking collectives  35.2 us (19%)
  starting transfers between devices  31.2 us (17%)
  local copies, waits for them, and re-layouts  27.5 us (15%)
  matrix products  19.4 us (11%)
  between operations  14.5 us (8%)
  other arithmetic  3.71 us (2%)
    all_to_all x1, blocking collectives, shards(): lax.all_to_all(blocks, 'x', split_axis=0, concat_axis=0, tiled=True)  35.2 us
    reduce_scatter x1, waiting for transfers between devices, shards(): lax.psum_scatter((gate_mine + gate_other).astype(jnp.bfloat16), 'dp', sca...  33.3 us
    ppermute x8, starting transfers between devices, shards(): received.append(lax.ppermute(block, ('x', 'section'), route))  19.8 us
    dot_general x6, matrix products, contract(): lax.dot_general(left, right, (((left_dim,), (right_dim,)), ((), ())), pre...  11 us
    ppermute x2, waiting for transfers between devices, shifted(): return lax.ppermute(block, axis, route)  10.3 us
    another operation x9, local copies, waits for them, and re-layouts, shards(): returned = jnp.stack(received).reshape(chips, cap_rows, width)  9.14 us
    ppermute x2, starting transfers between devices, swapped(): return lax.ppermute(block, 'core', [(0, 1), (1, 0)])  7.49 us
    ppermute x8, waiting for transfers between devices, shards(): received.append(lax.ppermute(block, ('x', 'section'), route))  5.27 us
  transfers between devices with their start and end apart: 13, of which 6 were waited for; matrix products, arithmetic and copies ran while one was open for 18% of the time, Pallas kernels for 0%

profile of v10, /device:TPU:147, one launch (start us, length us, event | category | flops | bytes accessed | tf_op | source)
XLA Modules:
  0.0 181.9 jit_solution(2145792612612210694)
XLA Ops:
  10.4 2.6 %convolution_convert_fusion = bf16[144,4096]{1,0:T(8,128)(2,1)} fusion(bf16[128,2048]{1,0:T(8,128)(2,1)S(1)} %multiply_convert_fusion, bf16[128,2048]{1,0:T(8,128)(2,1)} %bitcast.57, s32[128]{0:T(128)S(1)} %select_reduce_fusion.1, s32[128]{0:T(128)} %bitcast.60, s32[144]{0:T(256)S(1)} %get-tuple-element.20, s32[144]{0:T(256)S(1)} %get-tuple-element.21), kind=kOutput, calls=%fused_computation.2 | convolution fusion | flops 153737216 | bytes 2230400 | tf_op jit(solution)/shard_map/dot_general | solution.py:70
  13.0 3.1 %reshape.154 = bf16[8,576,128]{2,1,0:T(8,128)(2,1)} reshape(bf16[144,4096]{1,0:T(8,128)(2,1)} %convolution_convert_fusion) | data formatting | bytes 2359296 | tf_op jit(solution)/shard_map/reshape | solution.py:72
  16.0 35.2 %all_to_all.5 = bf16[8,576,128]{2,1,0:T(8,128)(2,1)} all-to-all(bf16[8,576,128]{2,1,0:T(8,128)(2,1)} %reshape.154), channel_id=1, replica_groups=mesh['x'=8,'core'=2,'section'=16,'dp'=4] {'x'}, dimensions={0} | all-to-all | bytes 2359296 | tf_op jit(solution)/shard_map/all_to_all | solution.py:73
  51.2 5.0 %collective-permute-start.2 = (bf16[8,576,128]{2,1,0:T(8,128)(2,1)}, bf16[8,576,128]{2,1,0:T(8,128)(2,1)}, u32[]{:S(2)}, u32[]{:S(2)}) collective-permute-start(bf16[8,576,128]{2,1,0:T(8,128)(2,1)} %all_to_all.5), channel_id=1, source_target_pairs={{0,64},{64,0},{1,65},{65,1},{2,66},{66,2},{3,67},{67,3},{4,68},{68... | collective-permute-start | bytes 3538952 | tf_op jit(solution)/shard_map/ppermute | solution.py:14
  56.2 2.0 %collective-permute-start = (bf16[128,2048]{1,0:T(8,128)(2,1)}, bf16[128,2048]{1,0:T(8,128)(2,1)}, u32[]{:S(2)}, u32[]{:S(2)}) collective-permute-start(bf16[128,2048]{1,0:T(8,128)(2,1)} %bitcast.3), channel_id=1, source_target_pairs={{4,0},{8,4},{12,8},{16,12},{20,16},{24,20},{28,24},{32,28},{36,32}... | collective-permute-start | bytes 1572872 | tf_op jit(solution)/shard_map/ppermute | solution.py:10
  60.1 3.1 %reshape.155 = bf16[144,4096]{1,0:T(8,128)(2,1)} reshape(bf16[8,576,128]{2,1,0:T(8,128)(2,1)} %all_to_all.5) | data formatting | bytes 2359296 | tf_op jit(solution)/shard_map/reshape | solution.py:75
  63.2 10.3 %collective-permute-done.1 = s32[128]{0:T(128)S(1)} collective-permute-done((s32[128]{0:T(128)S(1)}, s32[128]{0:T(128)S(1)}, u32[]{:S(2)}, u32[]{:S(2)}) %collective-permute-start.1) | collective-permute-done | bytes 544 | tf_op jit(solution)/shard_map/ppermute | solution.py:10
  75.9 3.1 %reshape.156 = bf16[144,4096]{1,0:T(8,128)(2,1)} reshape(bf16[8,576,128]{2,1,0:T(8,128)(2,1)} %collective-permute-done.2) | data formatting | bytes 2359296 | tf_op jit(solution)/shard_map/reshape | solution.py:77
  82.9 2.7 %add_convert_fusion = bf16[2048,768]{1,0:T(8,128)(2,1)} fusion(f32[2048,768]{1,0:T(8,128)S(1)} %fusion.27, bf16[144,4096]{1,0:T(8,128)(2,1)S(1)} %copy-done.3, bf16[144,384]{1,0:T(8,128)(2,1)S(1)} %get-tuple-element.9, bf16[144,384]{1,0:T(8,128)(2,1)S(1)} %get-tuple-element.8), kind=kOutput, calls=%fused_computation.1 | convolution fusion | flops 456572928 | bytes 10248192 | tf_op jit(solution)/shard_map/dot_general | solution.py:18
  85.6 2.9 %fusion.11 = bf16[144,2048]{1,0:T(8,128)(2,1)} fusion(bf16[1,1,2048,768]{3,2,1,0:T(8,128)(2,1)S(1)} %copy-done, bf16[144,384]{1,0:T(8,128)(2,1)} %copy-done.4, bf16[144,384]{1,0:T(8,128)(2,1)S(1)} %get-tuple-element.10), kind=kOutput, calls=%fused_computation.13 | convolution fusion | flops 453722112 | bytes 3956736 | tf_op jit(solution)/shard_map/dot_general | solution.py:18
  88.5 2.5 %collective-permute-start.3 = (bf16[144,2048]{1,0:T(8,128)(2,1)}, bf16[144,2048]{1,0:T(8,128)(2,1)}, u32[]{:S(2)}, u32[]{:S(2)}) collective-permute-start(bf16[144,2048]{1,0:T(8,128)(2,1)} %fusion.11), channel_id=1, source_target_pairs={{0,64},{64,0},{1,65},{65,1},{2,66},{66,2},{3,67},{67,3},{4,68},{68... | collective-permute-start | bytes 1769480 | tf_op jit(solution)/shard_map/ppermute | solution.py:14
  93.0 3.0 %add_convert_fusion.1 = bf16[144,2048]{1,0:T(8,128)(2,1)} fusion(bf16[144,2048]{1,0:T(8,128)(2,1)} %collective-permute-done.3, bf16[1,1,2048,768]{3,2,1,0:T(8,128)(2,1)S(1)} %copy-done, bf16[144,384]{1,0:T(8,128)(2,1)S(1)} %get-tuple-element.9, bf16[144,384]{1,0:T(8,128)(2,1)S(1)} %get-tuple-element.8), kind=kOutput, calls=%fused_computation.19 | convolution fusion | flops 454901760 | bytes 4546560 | tf_op jit(solution)/shard_map/dot_general | solution.py:18
  96.0 2.1 %reshape.157 = bf16[8,288,128]{2,1,0:T(8,128)(2,1)} reshape(bf16[144,2048]{1,0:T(8,128)(2,1)} %add_convert_fusion.1) | data formatting | bytes 1179648 | tf_op jit(solution)/shard_map/reshape | solution.py:85
  101.9 2.2 %collective-permute-start.10 = (bf16[288,128]{1,0:T(8,128)(2,1)S(1)}, bf16[288,128]{1,0:T(8,128)(2,1)S(1)}, u32[]{:S(2)}, u32[]{:S(2)}) collective-permute-start(bf16[288,128]{1,0:T(8,128)(2,1)S(1)} %get-tuple-element.13), channel_id=1, source_target_pairs={{4,768},{8,772},{12,776},{16,780},{20,784},{24,788},{28,792},{32,7... | collective-permute-start | bytes 221192 | tf_op jit(solution)/shard_map/ppermute | solution.py:95
  104.0 2.9 %collective-permute-start.9 = (bf16[288,128]{1,0:T(8,128)(2,1)S(1)}, bf16[288,128]{1,0:T(8,128)(2,1)S(1)}, u32[]{:S(2)}, u32[]{:S(2)}) collective-permute-start(bf16[288,128]{1,0:T(8,128)(2,1)S(1)} %get-tuple-element.14), channel_id=1, source_target_pairs={{4,640},{8,644},{12,648},{16,652},{20,656},{24,660},{28,664},{32,6... | collective-permute-start | bytes 221192 | tf_op jit(solution)/shard_map/ppermute | solution.py:95
  107.1 4.2 %collective-permute-start.8 = (bf16[288,128]{1,0:T(8,128)(2,1)S(1)}, bf16[288,128]{1,0:T(8,128)(2,1)}, u32[]{:S(2)}, u32[]{:S(2)}) collective-permute-start(bf16[288,128]{1,0:T(8,128)(2,1)S(1)} %get-tuple-element.15), channel_id=1, source_target_pairs={{4,512},{8,516},{12,520},{16,524},{20,528},{24,532},{28,536},{32,5... | collective-permute-start | bytes 221192 | tf_op jit(solution)/shard_map/ppermute | solution.py:95
  111.3 2.9 %collective-permute-start.7 = (bf16[288,128]{1,0:T(8,128)(2,1)}, bf16[288,128]{1,0:T(8,128)(2,1)}, u32[]{:S(2)}, u32[]{:S(2)}) collective-permute-start(bf16[288,128]{1,0:T(8,128)(2,1)} %get-tuple-element.16), channel_id=1, source_target_pairs={{4,384},{8,388},{12,392},{16,396},{20,400},{24,404},{28,408},{32,4... | collective-permute-start | bytes 221192 | tf_op jit(solution)/shard_map/ppermute | solution.py:95
  114.2 1.9 %collective-permute-start.6 = (bf16[288,128]{1,0:T(8,128)(2,1)}, bf16[288,128]{1,0:T(8,128)(2,1)}, u32[]{:S(2)}, u32[]{:S(2)}) collective-permute-start(bf16[288,128]{1,0:T(8,128)(2,1)} %get-tuple-element.17), channel_id=1, source_target_pairs={{4,256},{8,260},{12,264},{16,268},{20,272},{24,276},{28,280},{32,2... | collective-permute-start | bytes 221192 | tf_op jit(solution)/shard_map/ppermute | solution.py:95
  116.2 1.9 %collective-permute-start.5 = (bf16[288,128]{1,0:T(8,128)(2,1)}, bf16[288,128]{1,0:T(8,128)(2,1)}, u32[]{:S(2)}, u32[]{:S(2)}) collective-permute-start(bf16[288,128]{1,0:T(8,128)(2,1)} %get-tuple-element.18), channel_id=1, source_target_pairs={{4,128},{8,132},{12,136},{16,140},{20,144},{24,148},{28,152},{32,1... | collective-permute-start | bytes 221192 | tf_op jit(solution)/shard_map/ppermute | solution.py:95
  118.1 1.9 %collective-permute-start.4 = (bf16[288,128]{1,0:T(8,128)(2,1)}, bf16[288,128]{1,0:T(8,128)(2,1)}, u32[]{:S(2)}, u32[]{:S(2)}) collective-permute-start(bf16[288,128]{1,0:T(8,128)(2,1)} %get-tuple-element.19), channel_id=1, source_target_pairs={{4,0},{8,4},{12,8},{16,12},{20,16},{24,20},{28,24},{32,28},{36,32}... | collective-permute-start | bytes 221192 | tf_op jit(solution)/shard_map/ppermute | solution.py:95
  126.3 2.1 %collective-permute-done.6 = bf16[288,128]{1,0:T(8,128)(2,1)} collective-permute-done((bf16[288,128]{1,0:T(8,128)(2,1)}, bf16[288,128]{1,0:T(8,128)(2,1)}, u32[]{:S(2)}, u32[]{:S(2)}) %collective-permute-start.6) | collective-permute-done | bytes 73760 | tf_op jit(solution)/shard_map/ppermute | solution.py:95
  131.5 2.7 %collective-permute-done.4 = bf16[288,128]{1,0:T(8,128)(2,1)} collective-permute-done((bf16[288,128]{1,0:T(8,128)(2,1)}, bf16[288,128]{1,0:T(8,128)(2,1)}, u32[]{:S(2)}, u32[]{:S(2)}) %collective-permute-start.4) | collective-permute-done | bytes 73760 | tf_op jit(solution)/shard_map/ppermute | solution.py:95
  139.5 2.2 %fusion.26 = bf16[1,1,128,2048]{3,2,1,0:T(8,128)(2,1)} fusion(bf16[128,2048]{1,0:T(8,128)(2,1)} %collective-permute-done, bf16[8,18,2048]{2,1,0:T(8,128)(2,1)S(1)} %constant_dynamic-update-slice_fusion, bf16[8,18,128]{2,1,0:T(8,128)(2,1)S(1)} %copy-done.5, pred[8]{0:T(512)(128)(4,1)S(1)} %compare_and_fusion), kind=kOutput, calls=%fused_computation.27 | convolution fusion | flops 76302336 | bytes 1675272 | tf_op jit(solution)/shard_map/dot_general | solution.py:100
  141.7 33.3 %reduce-scatter.2.cloned.1.call-done = bf16[512,768]{1,0:T(8,128)(2,1)} async-done(((bf16[2048,768]{1,0:T(8,128)(2,1)}), bf16[512,768]{1,0:T(8,128)(2,1)}) %reduce-scatter.2.cloned.1.call-update) | async-done | bytes 786448 | tf_op jit(solution)/shard_map/reduce_scatter | solution.py:80
  (71 shorter events, 31.6 us)
Async XLA Ops:
  7.2 66.3 %copy-start = (bf16[1,1,2048,768]{3,2,1,0:T(8,128)(2,1)S(1)}, bf16[1,1,2048,768]{3,2,1,0:T(8,128)(2,1)}, u32[]{:S(2)}) copy-start(bf16[1,1,2048,768]{3,2,1,0:T(8,128)(2,1)} %param.10) | copy-start | bytes 9437188
  7.2 167.9 %reduce-scatter.2.cloned.1.call-start = ((), (), s32[]{:S(2)}) async-start(), calls=%async_computation.2 | async-start | bytes 3932160 | tf_op jit(solution)/shard_map/reduce_scatter | solution.py:80
  16.0 42.2 %copy-start.8 = (s32[1,1,128]{2,1,0:T(1,128)S(1)}, s32[1,1,128]{2,1,0:T(1,128)}, u32[]{:S(2)}) copy-start(s32[1,1,128]{2,1,0:T(1,128)} %param.9) | copy-start | bytes 1540
  51.2 24.7 %collective-permute-start.2 = (bf16[8,576,128]{2,1,0:T(8,128)(2,1)}, bf16[8,576,128]{2,1,0:T(8,128)(2,1)}, u32[]{:S(2)}, u32[]{:S(2)}) collective-permute-start(bf16[8,576,128]{2,1,0:T(8,128)(2,1)} %all_to_all.5), channel_id=1, source_target_pairs={{0,64},{64,0},{1,65},{65,1},{2,66},{66,2},{3,67},{67,3},{4,68},{68... | collective-permute-start | bytes 3538952 | tf_op jit(solution)/shard_map/ppermute | solution.py:14
  56.2 17.3 %collective-permute-start = (bf16[128,2048]{1,0:T(8,128)(2,1)}, bf16[128,2048]{1,0:T(8,128)(2,1)}, u32[]{:S(2)}, u32[]{:S(2)}) collective-permute-start(bf16[128,2048]{1,0:T(8,128)(2,1)} %bitcast.3), channel_id=1, source_target_pairs={{4,0},{8,4},{12,8},{16,12},{20,16},{24,20},{28,24},{32,28},{36,32}... | collective-permute-start | bytes 1572872 | tf_op jit(solution)/shard_map/ppermute | solution.py:10
  58.2 15.3 %collective-permute-start.1 = (s32[128]{0:T(128)S(1)}, s32[128]{0:T(128)S(1)}, u32[]{:S(2)}, u32[]{:S(2)}) collective-permute-start(s32[128]{0:T(128)S(1)} %bitcast.61), channel_id=1, source_target_pairs={{4,0},{8,4},{12,8},{16,12},{20,16},{24,20},{28,24},{32,28},{36,32}... | collective-permute-start | bytes 1544 | tf_op jit(solution)/shard_map/ppermute | solution.py:10
  63.2 12.0 %copy-start.2 = (bf16[144,4096]{1,0:T(8,128)(2,1)S(1)}, bf16[144,4096]{1,0:T(8,128)(2,1)}, u32[]{:S(2)}) copy-start(bf16[144,4096]{1,0:T(8,128)(2,1)} %reshape.155) | copy-start | bytes 3538948
  63.2 12.0 %copy-start.9 = (bf16[1,1,384,2048]{3,2,1,0:T(8,128)(2,1)S(1)}, bf16[1,1,384,2048]{3,2,1,0:T(8,128)(2,1)}, u32[]{:S(2)}) copy-start(bf16[1,1,384,2048]{3,2,1,0:T(8,128)(2,1)} %param.11) | copy-start | bytes 4718596
  78.9 1.8 %copy-start.1 = (bf16[144,4096]{1,0:T(8,128)(2,1)S(1)}, bf16[144,4096]{1,0:T(8,128)(2,1)}, u32[]{:S(2)}) copy-start(bf16[144,4096]{1,0:T(8,128)(2,1)} %reshape.156) | copy-start | bytes 3538948
  78.9 1.9 %copy-start.10 = (bf16[1,1,384,2048]{3,2,1,0:T(8,128)(2,1)S(1)}, bf16[1,1,384,2048]{3,2,1,0:T(8,128)(2,1)}, u32[]{:S(2)}) copy-start(bf16[1,1,384,2048]{3,2,1,0:T(8,128)(2,1)} %param.11) | copy-start | bytes 4718596
  81.5 1.1 copy-start.4
  81.6 1.3 copy-start.3
  88.5 4.5 %collective-permute-start.3 = (bf16[144,2048]{1,0:T(8,128)(2,1)}, bf16[144,2048]{1,0:T(8,128)(2,1)}, u32[]{:S(2)}, u32[]{:S(2)}) collective-permute-start(bf16[144,2048]{1,0:T(8,128)(2,1)} %fusion.11), channel_id=1, source_target_pairs={{0,64},{64,0},{1,65},{65,1},{2,66},{66,2},{3,67},{67,3},{4,68},{68... | collective-permute-start | bytes 1769480 | tf_op jit(solution)/shard_map/ppermute | solution.py:14
  100.0 14.2 %collective-permute-start.11 = (bf16[288,128]{1,0:T(8,128)(2,1)S(1)}, bf16[288,128]{1,0:T(8,128)(2,1)S(1)}, u32[]{:S(2)}, u32[]{:S(2)}) collective-permute-start(bf16[288,128]{1,0:T(8,128)(2,1)S(1)} %get-tuple-element.12), channel_id=1, source_target_pairs={{4,896},{8,900},{12,904},{16,908},{20,912},{24,916},{28,920},{32,9... | collective-permute-start | bytes 221192 | tf_op jit(solution)/shard_map/ppermute | solution.py:95
  101.9 14.3 %collective-permute-start.10 = (bf16[288,128]{1,0:T(8,128)(2,1)S(1)}, bf16[288,128]{1,0:T(8,128)(2,1)S(1)}, u32[]{:S(2)}, u32[]{:S(2)}) collective-permute-start(bf16[288,128]{1,0:T(8,128)(2,1)S(1)} %get-tuple-element.13), channel_id=1, source_target_pairs={{4,768},{8,772},{12,776},{16,780},{20,784},{24,788},{28,792},{32,7... | collective-permute-start | bytes 221192 | tf_op jit(solution)/shard_map/ppermute | solution.py:95
  104.0 14.0 %collective-permute-start.9 = (bf16[288,128]{1,0:T(8,128)(2,1)S(1)}, bf16[288,128]{1,0:T(8,128)(2,1)S(1)}, u32[]{:S(2)}, u32[]{:S(2)}) collective-permute-start(bf16[288,128]{1,0:T(8,128)(2,1)S(1)} %get-tuple-element.14), channel_id=1, source_target_pairs={{4,640},{8,644},{12,648},{16,652},{20,656},{24,660},{28,664},{32,6... | collective-permute-start | bytes 221192 | tf_op jit(solution)/shard_map/ppermute | solution.py:95
  107.1 16.6 %collective-permute-start.8 = (bf16[288,128]{1,0:T(8,128)(2,1)S(1)}, bf16[288,128]{1,0:T(8,128)(2,1)}, u32[]{:S(2)}, u32[]{:S(2)}) collective-permute-start(bf16[288,128]{1,0:T(8,128)(2,1)S(1)} %get-tuple-element.15), channel_id=1, source_target_pairs={{4,512},{8,516},{12,520},{16,524},{20,528},{24,532},{28,536},{32,5... | collective-permute-start | bytes 221192 | tf_op jit(solution)/shard_map/ppermute | solution.py:95
  111.3 13.4 %collective-permute-start.7 = (bf16[288,128]{1,0:T(8,128)(2,1)}, bf16[288,128]{1,0:T(8,128)(2,1)}, u32[]{:S(2)}, u32[]{:S(2)}) collective-permute-start(bf16[288,128]{1,0:T(8,128)(2,1)} %get-tuple-element.16), channel_id=1, source_target_pairs={{4,384},{8,388},{12,392},{16,396},{20,400},{24,404},{28,408},{32,4... | collective-permute-start | bytes 221192 | tf_op jit(solution)/shard_map/ppermute | solution.py:95
  114.2 14.1 %collective-permute-start.6 = (bf16[288,128]{1,0:T(8,128)(2,1)}, bf16[288,128]{1,0:T(8,128)(2,1)}, u32[]{:S(2)}, u32[]{:S(2)}) collective-permute-start(bf16[288,128]{1,0:T(8,128)(2,1)} %get-tuple-element.17), channel_id=1, source_target_pairs={{4,256},{8,260},{12,264},{16,268},{20,272},{24,276},{28,280},{32,2... | collective-permute-start | bytes 221192 | tf_op jit(solution)/shard_map/ppermute | solution.py:95
  116.1 3.9 %copy-start.6 = (bf16[288,128]{1,0:T(8,128)(2,1)}, bf16[288,128]{1,0:T(8,128)(2,1)S(1)}, u32[]{:S(2)}) copy-start(bf16[288,128]{1,0:T(8,128)(2,1)S(1)} %collective-permute-done.10) | copy-start | bytes 221188
  116.2 13.7 %collective-permute-start.5 = (bf16[288,128]{1,0:T(8,128)(2,1)}, bf16[288,128]{1,0:T(8,128)(2,1)}, u32[]{:S(2)}, u32[]{:S(2)}) collective-permute-start(bf16[288,128]{1,0:T(8,128)(2,1)} %get-tuple-element.18), channel_id=1, source_target_pairs={{4,128},{8,132},{12,136},{16,140},{20,144},{24,148},{28,152},{32,1... | collective-permute-start | bytes 221192 | tf_op jit(solution)/shard_map/ppermute | solution.py:95
  118.1 2.0 %copy-start.7 = (bf16[288,128]{1,0:T(8,128)(2,1)}, bf16[288,128]{1,0:T(8,128)(2,1)S(1)}, u32[]{:S(2)}) copy-start(bf16[288,128]{1,0:T(8,128)(2,1)S(1)} %collective-permute-done.9) | copy-start | bytes 221188
  118.1 16.1 %collective-permute-start.4 = (bf16[288,128]{1,0:T(8,128)(2,1)}, bf16[288,128]{1,0:T(8,128)(2,1)}, u32[]{:S(2)}, u32[]{:S(2)}) collective-permute-start(bf16[288,128]{1,0:T(8,128)(2,1)} %get-tuple-element.19), channel_id=1, source_target_pairs={{4,0},{8,4},{12,8},{16,12},{20,16},{24,20},{28,24},{32,28},{36,32}... | collective-permute-start | bytes 221192 | tf_op jit(solution)/shard_map/ppermute | solution.py:95
  135.8 3.7 %copy-start.5 = (bf16[8,18,128]{2,1,0:T(8,128)(2,1)S(1)}, bf16[8,18,128]{2,1,0:T(8,128)(2,1)}, u32[]{:S(2)}) copy-start(bf16[8,18,128]{2,1,0:T(8,128)(2,1)} %gather_fusion) | copy-start | bytes 110596
Sparse Core Ops, SparseCore 0:
  85.7 89.2 reduce-scatter.1

commit v11 on v9

--- a/solution.py
+++ b/solution.py
@@ -46,8 +46,7 @@
         axis=1,
     ).astype(jnp.bfloat16)
     row_grad = contract(act_grad, gate_up, 1, 1).astype(jnp.bfloat16)
-    gate_part = contract(input_rows, act_grad, 0, 0)
-    return row_grad, gate_part
+    return row_grad, act_grad
 
 
 def shards(tok_input, tok_grad, combine_weight, route_expert, gate_up_weight, down_weight):
@@ -73,10 +72,16 @@
     mine = lax.all_to_all(blocks, "x", split_axis=0, concat_axis=0, tiled=True).reshape(send.shape)
     mine, next_grad, next_routes = lax.optimization_barrier((mine, next_grad, next_routes))
     other = swapped(mine)
-    grad_mine, gate_mine = expert_half(mine, gate_up, down_proj, width, half_units)
-    grad_other, gate_other = expert_half(other, gate_up, down_proj, width, half_units)
+    grad_mine, act_mine = expert_half(mine, gate_up, down_proj, width, half_units)
+    grad_other, act_other = expert_half(other, gate_up, down_proj, width, half_units)
+    gate_total = contract(
+        jnp.concatenate([mine[:, :width], other[:, :width]], axis=0),
+        jnp.concatenate([act_mine, act_other], axis=0),
+        0,
+        0,
+    )
     gate_sum = lax.psum_scatter(
-        (gate_mine + gate_other).astype(jnp.bfloat16), "dp", scatter_dimension=0, tiled=True
+        gate_total.astype(jnp.bfloat16), "dp", scatter_dimension=0, tiled=True
     )
     partner_part = swapped(grad_other)
     paired = (grad_mine.astype(jnp.float32) + partner_part.astype(jnp.float32)).astype(jnp.bfloat16)

time: 166 us -> 167 us (level)
  the two profiles are of different devices: /device:TPU:149 before, /device:TPU:135 now
where the time goes in v11:
time: 167 us; the launch traced here: 165 us
  waiting for transfers between devices  65.4 us (39%)
  starting transfers between devices  37.3 us (22%)
  local copies, waits for them, and re-layouts  27.5 us (16%)
  matrix products  16.8 us (10%)
  between operations  14.5 us (9%)
  other arithmetic  3.71 us (2%)
    reduce_scatter x1, waiting for transfers between devices, shards(): lax.psum_scatter(gate_total.astype(jnp.bfloat16), 'dp', scatter_dimension...  36.3 us
    all_to_all x1, waiting for transfers between devices, shards(): lax.all_to_all(blocks, 'x', split_axis=0, concat_axis=0, tiled=True)  21.2 us
    ppermute x8, starting transfers between devices, shards(): received.append(lax.ppermute(block, ('x', 'section'), route))  19.3 us
    dot_general x5, matrix products, contract(): lax.dot_general(left, right, (((left_dim,), (right_dim,)), ((), ())), pre...  10.7 us
    another operation x9, local copies, waits for them, and re-layouts, shards(): returned = jnp.stack(received).reshape(chips, cap_rows, width)  10 us
    ppermute x2, starting transfers between devices, swapped(): return lax.ppermute(block, 'core', [(0, 1), (1, 0)])  7.3 us
    all_to_all x1, starting transfers between devices, shards(): lax.all_to_all(blocks, 'x', split_axis=0, concat_axis=0, tiled=True)  6.81 us
    ppermute x8, waiting for transfers between devices, shards(): received.append(lax.ppermute(block, ('x', 'section'), route))  6 us
  transfers between devices with their start and end apart: 14, of which 5 were waited for; matrix products, arithmetic and copies ran while one was open for 20% of the time, Pallas kernels for 0%

profile of v11, /device:TPU:135, one launch (start us, length us, event | category | flops | bytes accessed | tf_op | source)
XLA Modules:
  0.0 165.3 jit_solution(11130995804647286976)
XLA Ops:
  10.3 2.6 %convolution_convert_fusion = bf16[144,4096]{1,0:T(8,128)(2,1)} fusion(bf16[128,2048]{1,0:T(8,128)(2,1)S(1)} %multiply_convert_fusion, bf16[128,2048]{1,0:T(8,128)(2,1)} %bitcast.57, s32[128]{0:T(128)S(1)} %select_reduce_fusion.1, s32[128]{0:T(128)} %bitcast.61, s32[144]{0:T(256)S(1)} %get-tuple-element.20, s32[144]{0:T(256)S(1)} %get-tuple-element.21), kind=kOutput, calls=%fused_computation.1 | convolution fusion | flops 153737216 | bytes 2230400 | tf_op jit(solution)/shard_map/dot_general | solution.py:69
  12.9 3.1 %reshape.151 = bf16[8,576,128]{2,1,0:T(8,128)(2,1)} reshape(bf16[144,4096]{1,0:T(8,128)(2,1)} %convolution_convert_fusion) | data formatting | bytes 2359296 | tf_op jit(solution)/shard_map/reshape | solution.py:71
  16.0 6.8 %all-to-all-start = ((bf16[8,576,128]{2,1,0:T(8,128)(2,1)}), bf16[8,576,128]{2,1,0:T(8,128)(2,1)}, u32[]{:S(2)}, u32[]{:S(2)}) async-start(bf16[8,576,128]{2,1,0:T(8,128)(2,1)} %reshape.151), calls=%async_computation | async-start | bytes 2359296 | tf_op jit(solution)/shard_map/all_to_all | solution.py:72
  22.8 1.9 %collective-permute-start = (bf16[128,2048]{1,0:T(8,128)(2,1)}, bf16[128,2048]{1,0:T(8,128)(2,1)}, u32[]{:S(2)}, u32[]{:S(2)}) collective-permute-start(bf16[128,2048]{1,0:T(8,128)(2,1)} %bitcast.58), channel_id=1, source_target_pairs={{4,0},{8,4},{12,8},{16,12},{20,16},{24,20},{28,24},{32,28},{36,32}... | collective-permute-start | bytes 1572872 | tf_op jit(solution)/shard_map/ppermute | solution.py:10
  24.7 1.9 %collective-permute-start.1 = (s32[128]{0:T(128)S(1)}, s32[128]{0:T(128)S(1)}, u32[]{:S(2)}, u32[]{:S(2)}) collective-permute-start(s32[128]{0:T(128)S(1)} %bitcast.62), channel_id=1, source_target_pairs={{4,0},{8,4},{12,8},{16,12},{20,16},{24,20},{28,24},{32,28},{36,32}... | collective-permute-start | bytes 1544 | tf_op jit(solution)/shard_map/ppermute | solution.py:10
  26.7 21.2 %all-to-all-done = bf16[8,576,128]{2,1,0:T(8,128)(2,1)} async-done(((bf16[8,576,128]{2,1,0:T(8,128)(2,1)}), bf16[8,576,128]{2,1,0:T(8,128)(2,1)}, u32[]{:S(2)}, u32[]{:S(2)}) %all-to-all-start) | async-done | bytes 1179680 | tf_op jit(solution)/shard_map/all_to_all | solution.py:72
  47.9 3.1 %reshape.152 = bf16[144,4096]{1,0:T(8,128)(2,1)} reshape(bf16[8,576,128]{2,1,0:T(8,128)(2,1)} %all-to-all-done) | data formatting | bytes 2359296 | tf_op jit(solution)/shard_map/reshape | solution.py:72
  50.9 5.4 %collective-permute-start.2 = (bf16[144,4096]{1,0:T(8,128)(2,1)}, bf16[144,4096]{1,0:T(8,128)(2,1)S(1)}, u32[]{:S(2)}, u32[]{:S(2)}) collective-permute-start(bf16[144,4096]{1,0:T(8,128)(2,1)} %reshape.152), channel_id=1, source_target_pairs={{0,64},{64,0},{1,65},{65,1},{2,66},{66,2},{3,67},{67,3},{4,68},{68... | collective-permute-start | bytes 3538952 | tf_op jit(solution)/shard_map/ppermute | solution.py:14
  61.5 3.5 %convolution_convert_fusion.1 = bf16[2048,768]{1,0:T(8,128)(2,1)} fusion(bf16[144,2048]{1,0:T(8,128)(2,1)S(1)} %slice.36, bf16[144,2048]{1,0:T(8,128)(2,1)S(1)} %slice.26, bf16[144,384]{1,0:T(8,128)(2,1)S(1)} %get-tuple-element.11, bf16[144,384]{1,0:T(8,128)(2,1)S(1)} %get-tuple-element.10, bf16[144,384]{1,0:T(8,128)(2,1)S(1)} %get-tuple-element.9, ...), kind=kOutput, calls=%fused_computation.2 | convolution fusion | flops 911671296 | bytes 4767744 | tf_op jit(solution)/shard_map/dot_general | solution.py:18
  65.0 2.9 %fusion.11 = bf16[144,2048]{1,0:T(8,128)(2,1)} fusion(bf16[1,1,2048,768]{3,2,1,0:T(8,128)(2,1)S(1)} %copy-done, bf16[144,384]{1,0:T(8,128)(2,1)} %copy-done.3, bf16[144,384]{1,0:T(8,128)(2,1)S(1)} %get-tuple-element.10), kind=kOutput, calls=%fused_computation.13 | convolution fusion | flops 453722112 | bytes 3956736 | tf_op jit(solution)/shard_map/dot_general | solution.py:18
  67.9 1.9 %collective-permute-start.3 = (bf16[144,2048]{1,0:T(8,128)(2,1)}, bf16[144,2048]{1,0:T(8,128)(2,1)}, u32[]{:S(2)}, u32[]{:S(2)}) collective-permute-start(bf16[144,2048]{1,0:T(8,128)(2,1)} %fusion.11), channel_id=1, source_target_pairs={{0,64},{64,0},{1,65},{65,1},{2,66},{66,2},{3,67},{67,3},{4,68},{68... | collective-permute-start | bytes 1769480 | tf_op jit(solution)/shard_map/ppermute | solution.py:14
  72.1 3.0 %add_convert_fusion = bf16[144,2048]{1,0:T(8,128)(2,1)} fusion(bf16[144,2048]{1,0:T(8,128)(2,1)} %collective-permute-done.3, bf16[1,1,2048,768]{3,2,1,0:T(8,128)(2,1)S(1)} %copy-done, bf16[144,384]{1,0:T(8,128)(2,1)S(1)} %get-tuple-element.9, bf16[144,384]{1,0:T(8,128)(2,1)S(1)} %get-tuple-element.8), kind=kOutput, calls=%fused_computation.22 | convolution fusion | flops 454901760 | bytes 4546560 | tf_op jit(solution)/shard_map/dot_general | solution.py:18
  75.2 2.1 %reshape.153 = bf16[8,288,128]{2,1,0:T(8,128)(2,1)} reshape(bf16[144,2048]{1,0:T(8,128)(2,1)} %add_convert_fusion) | data formatting | bytes 1179648 | tf_op jit(solution)/shard_map/reshape | solution.py:88
  79.1 3.4 %collective-permute-start.11 = (bf16[288,128]{1,0:T(8,128)(2,1)S(1)}, bf16[288,128]{1,0:T(8,128)(2,1)S(1)}, u32[]{:S(2)}, u32[]{:S(2)}) collective-permute-start(bf16[288,128]{1,0:T(8,128)(2,1)S(1)} %get-tuple-element.12), channel_id=1, source_target_pairs={{4,896},{8,900},{12,904},{16,908},{20,912},{24,916},{28,920},{32,9... | collective-permute-start | bytes 221192 | tf_op jit(solution)/shard_map/ppermute | solution.py:98
  82.5 4.2 %collective-permute-start.10 = (bf16[288,128]{1,0:T(8,128)(2,1)S(1)}, bf16[288,128]{1,0:T(8,128)(2,1)S(1)}, u32[]{:S(2)}, u32[]{:S(2)}) collective-permute-start(bf16[288,128]{1,0:T(8,128)(2,1)S(1)} %get-tuple-element.13), channel_id=1, source_target_pairs={{4,768},{8,772},{12,776},{16,780},{20,784},{24,788},{28,792},{32,7... | collective-permute-start | bytes 221192 | tf_op jit(solution)/shard_map/ppermute | solution.py:98
  86.8 1.9 %collective-permute-start.9 = (bf16[288,128]{1,0:T(8,128)(2,1)S(1)}, bf16[288,128]{1,0:T(8,128)(2,1)S(1)}, u32[]{:S(2)}, u32[]{:S(2)}) collective-permute-start(bf16[288,128]{1,0:T(8,128)(2,1)S(1)} %get-tuple-element.14), channel_id=1, source_target_pairs={{4,640},{8,644},{12,648},{16,652},{20,656},{24,660},{28,664},{32,6... | collective-permute-start | bytes 221192 | tf_op jit(solution)/shard_map/ppermute | solution.py:98
  88.9 1.9 %collective-permute-start.8 = (bf16[288,128]{1,0:T(8,128)(2,1)S(1)}, bf16[288,128]{1,0:T(8,128)(2,1)}, u32[]{:S(2)}, u32[]{:S(2)}) collective-permute-start(bf16[288,128]{1,0:T(8,128)(2,1)S(1)} %get-tuple-element.15), channel_id=1, source_target_pairs={{4,512},{8,516},{12,520},{16,524},{20,528},{24,532},{28,536},{32,5... | collective-permute-start | bytes 221192 | tf_op jit(solution)/shard_map/ppermute | solution.py:98
  90.8 1.9 %collective-permute-start.7 = (bf16[288,128]{1,0:T(8,128)(2,1)}, bf16[288,128]{1,0:T(8,128)(2,1)}, u32[]{:S(2)}, u32[]{:S(2)}) collective-permute-start(bf16[288,128]{1,0:T(8,128)(2,1)} %get-tuple-element.16), channel_id=1, source_target_pairs={{4,384},{8,388},{12,392},{16,396},{20,400},{24,404},{28,408},{32,4... | collective-permute-start | bytes 221192 | tf_op jit(solution)/shard_map/ppermute | solution.py:98
  92.7 2.0 %collective-permute-start.6 = (bf16[288,128]{1,0:T(8,128)(2,1)}, bf16[288,128]{1,0:T(8,128)(2,1)}, u32[]{:S(2)}, u32[]{:S(2)}) collective-permute-start(bf16[288,128]{1,0:T(8,128)(2,1)} %get-tuple-element.17), channel_id=1, source_target_pairs={{4,256},{8,260},{12,264},{16,268},{20,272},{24,276},{28,280},{32,2... | collective-permute-start | bytes 221192 | tf_op jit(solution)/shard_map/ppermute | solution.py:98
  94.7 2.1 %collective-permute-start.5 = (bf16[288,128]{1,0:T(8,128)(2,1)}, bf16[288,128]{1,0:T(8,128)(2,1)}, u32[]{:S(2)}, u32[]{:S(2)}) collective-permute-start(bf16[288,128]{1,0:T(8,128)(2,1)} %get-tuple-element.18), channel_id=1, source_target_pairs={{4,128},{8,132},{12,136},{16,140},{20,144},{24,148},{28,152},{32,1... | collective-permute-start | bytes 221192 | tf_op jit(solution)/shard_map/ppermute | solution.py:98
  96.8 4.8 %collective-permute-done.9 = bf16[288,128]{1,0:T(8,128)(2,1)S(1)} collective-permute-done((bf16[288,128]{1,0:T(8,128)(2,1)S(1)}, bf16[288,128]{1,0:T(8,128)(2,1)S(1)}, u32[]{:S(2)}, u32[]{:S(2)}) %collective-permute-start.9) | collective-permute-done | bytes 73760 | tf_op jit(solution)/shard_map/ppermute | solution.py:98
  101.7 1.9 %collective-permute-start.4 = (bf16[288,128]{1,0:T(8,128)(2,1)}, bf16[288,128]{1,0:T(8,128)(2,1)}, u32[]{:S(2)}, u32[]{:S(2)}) collective-permute-start(bf16[288,128]{1,0:T(8,128)(2,1)} %get-tuple-element.19), channel_id=1, source_target_pairs={{4,0},{8,4},{12,8},{16,12},{20,16},{24,20},{28,24},{32,28},{36,32}... | collective-permute-start | bytes 221192 | tf_op jit(solution)/shard_map/ppermute | solution.py:98
  119.8 2.2 %fusion.29 = bf16[1,1,128,2048]{3,2,1,0:T(8,128)(2,1)} fusion(bf16[128,2048]{1,0:T(8,128)(2,1)} %collective-permute-done, bf16[8,18,2048]{2,1,0:T(8,128)(2,1)S(1)} %constant_dynamic-update-slice_fusion, bf16[8,18,128]{2,1,0:T(8,128)(2,1)S(1)} %copy-done.2, pred[8]{0:T(512)(128)(4,1)S(1)} %compare_and_fusion), kind=kOutput, calls=%fused_computation.30 | convolution fusion | flops 76302336 | bytes 1675272 | tf_op jit(solution)/shard_map/dot_general | solution.py:103
  122.1 36.3 %reduce-scatter.2.cloned.1.call-done = bf16[512,768]{1,0:T(8,128)(2,1)} async-done(((bf16[2048,768]{1,0:T(8,128)(2,1)}), bf16[512,768]{1,0:T(8,128)(2,1)}) %reduce-scatter.2.cloned.1.call-update) | async-done | bytes 786448 | tf_op jit(solution)/shard_map/reduce_scatter | solution.py:83
  (68 shorter events, 28.6 us)
Async XLA Ops:
  7.2 50.3 %copy-start = (bf16[1,1,2048,768]{3,2,1,0:T(8,128)(2,1)S(1)}, bf16[1,1,2048,768]{3,2,1,0:T(8,128)(2,1)}, u32[]{:S(2)}) copy-start(bf16[1,1,2048,768]{3,2,1,0:T(8,128)(2,1)} %param.10) | copy-start | bytes 9437188
  16.0 8.7 %copy-start.7 = (s32[1,1,128]{2,1,0:T(1,128)S(1)}, s32[1,1,128]{2,1,0:T(1,128)}, u32[]{:S(2)}) copy-start(s32[1,1,128]{2,1,0:T(1,128)} %param.9) | copy-start | bytes 1540
  16.0 31.9 %all-to-all-start = ((bf16[8,576,128]{2,1,0:T(8,128)(2,1)}), bf16[8,576,128]{2,1,0:T(8,128)(2,1)}, u32[]{:S(2)}, u32[]{:S(2)}) async-start(bf16[8,576,128]{2,1,0:T(8,128)(2,1)} %reshape.151), calls=%async_computation | async-start | bytes 2359296 | tf_op jit(solution)/shard_map/all_to_all | solution.py:72
  22.8 135.6 %reduce-scatter.2.cloned.1.call-start = ((), (), s32[]{:S(2)}) async-start(), calls=%async_computation.2 | async-start | bytes 3932160 | tf_op jit(solution)/shard_map/reduce_scatter | solution.py:83
  22.8 28.1 %collective-permute-start = (bf16[128,2048]{1,0:T(8,128)(2,1)}, bf16[128,2048]{1,0:T(8,128)(2,1)}, u32[]{:S(2)}, u32[]{:S(2)}) collective-permute-start(bf16[128,2048]{1,0:T(8,128)(2,1)} %bitcast.58), channel_id=1, source_target_pairs={{4,0},{8,4},{12,8},{16,12},{20,16},{24,20},{28,24},{32,28},{36,32}... | collective-permute-start | bytes 1572872 | tf_op jit(solution)/shard_map/ppermute | solution.py:10
  24.7 26.2 %collective-permute-start.1 = (s32[128]{0:T(128)S(1)}, s32[128]{0:T(128)S(1)}, u32[]{:S(2)}, u32[]{:S(2)}) collective-permute-start(s32[128]{0:T(128)S(1)} %bitcast.62), channel_id=1, source_target_pairs={{4,0},{8,4},{12,8},{16,12},{20,16},{24,20},{28,24},{32,28},{36,32}... | collective-permute-start | bytes 1544 | tf_op jit(solution)/shard_map/ppermute | solution.py:10
  50.9 6.5 %copy-start.1 = (bf16[144,4096]{1,0:T(8,128)(2,1)S(1)}, bf16[144,4096]{1,0:T(8,128)(2,1)}, u32[]{:S(2)}) copy-start(bf16[144,4096]{1,0:T(8,128)(2,1)} %reshape.152) | copy-start | bytes 3538948
  50.9 8.6 %collective-permute-start.2 = (bf16[144,4096]{1,0:T(8,128)(2,1)}, bf16[144,4096]{1,0:T(8,128)(2,1)S(1)}, u32[]{:S(2)}, u32[]{:S(2)}) collective-permute-start(bf16[144,4096]{1,0:T(8,128)(2,1)} %reshape.152), channel_id=1, source_target_pairs={{0,64},{64,0},{1,65},{65,1},{2,66},{66,2},{3,67},{67,3},{4,68},{68... | collective-permute-start | bytes 3538952 | tf_op jit(solution)/shard_map/ppermute | solution.py:14
  57.5 1.4 copy-start.8
  60.9 0.6 copy-start.3
  67.9 4.2 %collective-permute-start.3 = (bf16[144,2048]{1,0:T(8,128)(2,1)}, bf16[144,2048]{1,0:T(8,128)(2,1)}, u32[]{:S(2)}, u32[]{:S(2)}) collective-permute-start(bf16[144,2048]{1,0:T(8,128)(2,1)} %fusion.11), channel_id=1, source_target_pairs={{0,64},{64,0},{1,65},{65,1},{2,66},{66,2},{3,67},{67,3},{4,68},{68... | collective-permute-start | bytes 1769480 | tf_op jit(solution)/shard_map/ppermute | solution.py:14
  79.1 13.6 %collective-permute-start.11 = (bf16[288,128]{1,0:T(8,128)(2,1)S(1)}, bf16[288,128]{1,0:T(8,128)(2,1)S(1)}, u32[]{:S(2)}, u32[]{:S(2)}) collective-permute-start(bf16[288,128]{1,0:T(8,128)(2,1)S(1)} %get-tuple-element.12), channel_id=1, source_target_pairs={{4,896},{8,900},{12,904},{16,908},{20,912},{24,916},{28,920},{32,9... | collective-permute-start | bytes 221192 | tf_op jit(solution)/shard_map/ppermute | solution.py:98
  82.5 12.2 %collective-permute-start.10 = (bf16[288,128]{1,0:T(8,128)(2,1)S(1)}, bf16[288,128]{1,0:T(8,128)(2,1)S(1)}, u32[]{:S(2)}, u32[]{:S(2)}) collective-permute-start(bf16[288,128]{1,0:T(8,128)(2,1)S(1)} %get-tuple-element.13), channel_id=1, source_target_pairs={{4,768},{8,772},{12,776},{16,780},{20,784},{24,788},{28,792},{32,7... | collective-permute-start | bytes 221192 | tf_op jit(solution)/shard_map/ppermute | solution.py:98
  86.8 14.9 %collective-permute-start.9 = (bf16[288,128]{1,0:T(8,128)(2,1)S(1)}, bf16[288,128]{1,0:T(8,128)(2,1)S(1)}, u32[]{:S(2)}, u32[]{:S(2)}) collective-permute-start(bf16[288,128]{1,0:T(8,128)(2,1)S(1)} %get-tuple-element.14), channel_id=1, source_target_pairs={{4,640},{8,644},{12,648},{16,652},{20,656},{24,660},{28,664},{32,6... | collective-permute-start | bytes 221192 | tf_op jit(solution)/shard_map/ppermute | solution.py:98
  88.9 18.8 %collective-permute-start.8 = (bf16[288,128]{1,0:T(8,128)(2,1)S(1)}, bf16[288,128]{1,0:T(8,128)(2,1)}, u32[]{:S(2)}, u32[]{:S(2)}) collective-permute-start(bf16[288,128]{1,0:T(8,128)(2,1)S(1)} %get-tuple-element.15), channel_id=1, source_target_pairs={{4,512},{8,516},{12,520},{16,524},{20,528},{24,532},{28,536},{32,5... | collective-permute-start | bytes 221192 | tf_op jit(solution)/shard_map/ppermute | solution.py:98
  90.8 17.9 %collective-permute-start.7 = (bf16[288,128]{1,0:T(8,128)(2,1)}, bf16[288,128]{1,0:T(8,128)(2,1)}, u32[]{:S(2)}, u32[]{:S(2)}) collective-permute-start(bf16[288,128]{1,0:T(8,128)(2,1)} %get-tuple-element.16), channel_id=1, source_target_pairs={{4,384},{8,388},{12,392},{16,396},{20,400},{24,404},{28,408},{32,4... | collective-permute-start | bytes 221192 | tf_op jit(solution)/shard_map/ppermute | solution.py:98
  92.7 10.8 %copy-start.4 = (bf16[288,128]{1,0:T(8,128)(2,1)}, bf16[288,128]{1,0:T(8,128)(2,1)S(1)}, u32[]{:S(2)}) copy-start(bf16[288,128]{1,0:T(8,128)(2,1)S(1)} %collective-permute-done.11) | copy-start | bytes 221188
  92.7 17.5 %collective-permute-start.6 = (bf16[288,128]{1,0:T(8,128)(2,1)}, bf16[288,128]{1,0:T(8,128)(2,1)}, u32[]{:S(2)}, u32[]{:S(2)}) collective-permute-start(bf16[288,128]{1,0:T(8,128)(2,1)} %get-tuple-element.17), channel_id=1, source_target_pairs={{4,256},{8,260},{12,264},{16,268},{20,272},{24,276},{28,280},{32,2... | collective-permute-start | bytes 221192 | tf_op jit(solution)/shard_map/ppermute | solution.py:98
  94.7 8.9 %copy-start.5 = (bf16[288,128]{1,0:T(8,128)(2,1)}, bf16[288,128]{1,0:T(8,128)(2,1)S(1)}, u32[]{:S(2)}) copy-start(bf16[288,128]{1,0:T(8,128)(2,1)S(1)} %collective-permute-done.10) | copy-start | bytes 221188
  94.7 17.1 %collective-permute-start.5 = (bf16[288,128]{1,0:T(8,128)(2,1)}, bf16[288,128]{1,0:T(8,128)(2,1)}, u32[]{:S(2)}, u32[]{:S(2)}) collective-permute-start(bf16[288,128]{1,0:T(8,128)(2,1)} %get-tuple-element.18), channel_id=1, source_target_pairs={{4,128},{8,132},{12,136},{16,140},{20,144},{24,148},{28,152},{32,1... | collective-permute-start | bytes 221192 | tf_op jit(solution)/shard_map/ppermute | solution.py:98
  101.6 1.9 %copy-start.6 = (bf16[288,128]{1,0:T(8,128)(2,1)}, bf16[288,128]{1,0:T(8,128)(2,1)S(1)}, u32[]{:S(2)}) copy-start(bf16[288,128]{1,0:T(8,128)(2,1)S(1)} %collective-permute-done.9) | copy-start | bytes 221188
  101.7 12.9 %collective-permute-start.4 = (bf16[288,128]{1,0:T(8,128)(2,1)}, bf16[288,128]{1,0:T(8,128)(2,1)}, u32[]{:S(2)}, u32[]{:S(2)}) collective-permute-start(bf16[288,128]{1,0:T(8,128)(2,1)} %get-tuple-element.19), channel_id=1, source_target_pairs={{4,0},{8,4},{12,8},{16,12},{20,16},{24,20},{28,24},{32,28},{36,32}... | collective-permute-start | bytes 221192 | tf_op jit(solution)/shard_map/ppermute | solution.py:98
  116.1 3.7 %copy-start.2 = (bf16[8,18,128]{2,1,0:T(8,128)(2,1)S(1)}, bf16[8,18,128]{2,1,0:T(8,128)(2,1)}, u32[]{:S(2)}) copy-start(bf16[8,18,128]{2,1,0:T(8,128)(2,1)} %gather_fusion) | copy-start | bytes 110596
Sparse Core Ops, SparseCore 0:
  65.2 93.1 reduce-scatter.1
